TPU v7x, 512 devices: a whole 4x8x8 slice. The times are simulated.
512 devices in a mesh: ctx: 128 (over y, z, core), tp: 4 (over x).
Axes of the slice: x: 4, y: 8, z: 8, core: 2. Of those that a mesh axis runs over, the one named last changes fastest.
Arguments:
- outer_gate: bfloat16 [32768, 2048], P('ctx', 'tp'), may hold values from -6 to 6
- inner_gate: bfloat16 [32768, 2048], P('ctx', 'tp'), may hold values from -6 to 6
- stream: bfloat16 [32768, 2048], P('ctx', 'tp'), may hold values from -6 to 6
- filters: bfloat16 [128, 128], P('tp'), may hold values from -1 to 1
- query_rows: bfloat16 [32768, 2048], P('ctx', 'tp'), may hold values from -49 to 49
- key_rows: bfloat16 [32768, 2048], P('ctx', 'tp'), may hold values from -4 to 4
Outputs:
- mixed: bfloat16 [32768, 2048], P('ctx', 'tp')
- attended: bfloat16 [32768, 2048], P('ctx', 'tp')
All inputs are finite; a program needn't handle non-finite values.
Results may differ from a plain program's by a relative error of at most 0.007.
Values may be sent and summed in bfloat16 or wider, within the bound.
No kernel may reach another device: no remote copies, remote signals or barrier semaphores. Data moves between devices by JAX's collectives and lax.ppermute only.
A program may use at most 64 MiB of HBM per device.

v0:
```python
import functools
import math

import jax
import jax.numpy as jnp
from jax import lax
from jax.sharding import Mesh, NamedSharding
from jax.sharding import PartitionSpec as P

HEAD_DIM = 128
LENGTH = 8192
CORES = 2
WINDOW_SHARDS = 8

NEGATIVE = -1e30
CTX_AXES = ("row", "col", "core")


def passed_along(block, axis, size, distance):
    route = [(i - distance, i) for i in range(size) if i - distance >= 0]
    return lax.ppermute(block, axis, route)


def toeplitz_taps(filters, offset):
    groups, kernel = filters.shape
    flipped = filters[:, ::-1]
    zeros = jnp.zeros_like(flipped)
    pieces = [flipped, zeros] if offset == 0 else [zeros, flipped]
    lags = jnp.concatenate(pieces, axis=1)
    flat = jnp.tile(lags, (1, kernel))[:, : kernel * (2 * kernel - 1)]
    return flat.reshape(groups, kernel, 2 * kernel - 1)[:, :, kernel - 1 : 2 * kernel - 1]


def apply_blocks(matrix, blocks):
    return jnp.einsum("gts,bsgc->btgc", matrix, blocks, preferred_element_type=jnp.float32)


def body(outer_gate, inner_gate, stream, filters, query_rows, key_rows, *, rows, half):
    row_count, channels = outer_gate.shape
    groups, kernel = filters.shape
    group_size = channels // groups
    seq_span = 2 * half
    ctx_size = rows * half
    in_row = lax.axis_index("col") * CORES + lax.axis_index("core")
    row_index = lax.axis_index("row")
    shard_index = row_index * half + in_row
    seq_place = (shard_index + half) % seq_span
    product = (inner_gate.astype(jnp.float32) * stream.astype(jnp.float32)).astype(jnp.bfloat16)
    blocks = product.reshape(row_count // kernel, kernel, groups, group_size)
    near_taps = toeplitz_taps(filters, 0)
    far_taps = toeplitz_taps(filters, kernel)
    tail_rows = product[row_count - kernel + 1 :]
    earlier = passed_along(tail_rows, CTX_AXES, ctx_size, 1)
    earlier = jnp.where(seq_place == 0, jnp.zeros_like(earlier), earlier)
    first_block = jnp.concatenate([jnp.zeros((1, channels), jnp.bfloat16), earlier], 0)
    first_block = first_block.reshape(1, kernel, groups, group_size)
    before = jnp.concatenate([first_block, blocks[:-1]], 0)
    filtered = (apply_blocks(near_taps, blocks) + apply_blocks(far_taps, before)).reshape(
        row_count, channels
    )
    mixed = (outer_gate.astype(jnp.float32) * filtered).astype(jnp.bfloat16)
    local_heads = channels // HEAD_DIM
    queries = query_rows.reshape(row_count, local_heads, HEAD_DIM)
    score_scale = 1.0 / math.sqrt(HEAD_DIM)
    query_pos = shard_index * row_count + jnp.arange(row_count, dtype=jnp.int32)
    seq_start = jnp.maximum(shard_index - seq_place, 0) * row_count

    def row_down(array):
        return lax.ppermute(array, "row", [(r, r + 1) for r in range(rows - 1)])

    def row_gather(array):
        return lax.all_gather(jnp.stack([array, row_down(array)]), ("col", "core"), axis=0)

    keys_all = row_gather(key_rows)
    values_all = row_gather(mixed)
    gathered_rows = keys_all.shape[0] * keys_all.shape[1] * row_count
    keys_all = keys_all.reshape(gathered_rows, channels)
    values_all = values_all.reshape(gathered_rows, channels)
    key_index = jnp.arange(gathered_rows, dtype=jnp.int32)
    key_shard = key_index // (2 * row_count)
    key_source = (key_index // row_count) % 2
    key_pos = ((row_index - key_source) * half + key_shard) * row_count + key_index % row_count
    visible = (key_pos[None, :] >= seq_start) & (key_pos[None, :] <= query_pos[:, None])

    head_outputs = []
    for head in range(local_heads):
        lanes = slice(head * HEAD_DIM, (head + 1) * HEAD_DIM)
        scores = (
            lax.dot_general(
                query_rows[:, lanes],
                keys_all[:, lanes],
                (((1,), (1,)), ((), ())),
                preferred_element_type=jnp.float32,
            )
            * score_scale
        )
        scores = jnp.where(visible, scores, NEGATIVE)
        row_peak = jnp.max(scores, axis=1, keepdims=True)
        exp_terms = jnp.where(visible, jnp.exp(scores - row_peak), 0.0)
        row_total = jnp.sum(exp_terms, axis=1, keepdims=True)
        weighted = jnp.dot(
            exp_terms.astype(jnp.bfloat16), values_all[:, lanes], preferred_element_type=jnp.float32
        )
        head_outputs.append((weighted / row_total).astype(jnp.bfloat16))
    attended = jnp.concatenate(head_outputs, axis=1)
    return (mixed, attended)


def solution(mesh):
    def run(outer_gate, inner_gate, stream, filters, query_rows, key_rows):
        ctx = mesh.shape["ctx"]
        row_count = outer_gate.shape[0] // ctx
        half = (LENGTH // 2) // row_count
        rows = ctx // half
        devices = mesh.devices.reshape(rows, half // CORES, CORES, mesh.shape["tp"])
        split = Mesh(devices, CTX_AXES + ("tp",))
        rows_spec = P(CTX_AXES, "tp")
        in_specs = (rows_spec, rows_spec, rows_spec, P("tp", None), rows_spec, rows_spec)
        outs = jax.shard_map(
            functools.partial(body, rows=rows, half=half),
            mesh=split,
            in_specs=in_specs,
            out_specs=(rows_spec, rows_spec),
            check_vma=False,
        )(outer_gate, inner_gate, stream, filters, query_rows, key_rows)
        placed = NamedSharding(mesh, P("ctx", "tp"))
        return tuple(lax.with_sharding_constraint(o, placed) for o in outs)

    return run
```

profile of v0, /device:TPU:1, one launch (start us, length us, event | category | flops | bytes accessed | tf_op | source)
XLA Modules:
  0.0 174.1 jit_solution(5971536334402065381)
XLA Ops:
  7.2 4.0 %collective-permute-start.1 = (bf16[256,512]{1,0:T(8,128)(2,1)}, bf16[256,512]{1,0:T(8,128)(2,1)S(1)}, u32[]{:S(2)}, u32[]{:S(2)}) collective-permute-start(bf16[256,512]{1,0:T(8,128)(2,1)} %param.11), channel_id=1, source_target_pairs={{0,64},{64,128},{128,192},{192,256},{256,320},{320,384},{384,448},... | collective-permute-start | bytes 786440 | tf_op jit(solution)/shard_map/ppermute | solution.py:69
  11.3 3.6 %collective-permute-done.1 = bf16[256,512]{1,0:T(8,128)(2,1)S(1)} collective-permute-done((bf16[256,512]{1,0:T(8,128)(2,1)}, bf16[256,512]{1,0:T(8,128)(2,1)S(1)}, u32[]{:S(2)}, u32[]{:S(2)}) %collective-permute-start.1) | collective-permute-done | bytes 262176 | tf_op jit(solution)/shard_map/ppermute | solution.py:69
  14.9 1.8 %pad_maximum_fusion = bf16[2,256,512]{2,1,0:T(8,128)(2,1)} fusion(bf16[1,256,512]{2,1,0:T(8,128)(2,1)S(1)} %bitcast.63, bf16[1,256,512]{2,1,0:T(8,128)(2,1)} %bitcast.62), kind=kLoop, calls=%fused_computation.60 | loop fusion | flops 262144 | bytes 1048576 | tf_op jit(solution)/shard_map/stack | solution.py:72
  16.7 1.1 multiply_convert_fusion
  17.8 0.7 slice.78
  18.5 7.1 %collective-permute-start = (bf16[127,512]{1,0:T(8,128)(2,1)}, bf16[127,512]{1,0:T(8,128)(2,1)S(1)}, u32[]{:S(2)}, u32[]{:S(2)}) collective-permute-start(bf16[127,512]{1,0:T(8,128)(2,1)} %slice.78), channel_id=1, source_target_pairs={{0,4},{4,8},{8,12},{12,16},{16,20},{20,24},{24,28},{28,32},{32,36}... | collective-permute-start | bytes 390152 | tf_op jit(solution)/shard_map/ppermute | solution.py:21
  25.8 0.8 rev.4
  26.8 1.2 copy.41
  28.1 7.8 %reshape.95 = bf16[32,128,255]{2,1,0:T(8,128)(2,1)} reshape(bf16[32,32640]{1,0:T(8,128)(2,1)S(1)} %slice.76) | data formatting | bytes 4177920 | tf_op jit(solution)/shard_map/reshape | solution.py:31
  35.9 2.4 %fusion.81 = f32[32,2,16,128]{3,2,1,0:T(8,128)S(1)} fusion(bf16[32,128,255]{2,1,0:T(8,128)(2,1)} %reshape.95, bf16[2,128,32,16]{1,0,3,2:T(2,128)(2,1)S(1)} %reshape.94), kind=kOutput, calls=%fused_computation.57 | convolution fusion | flops 33554432 | bytes 1835008 | tf_op jit(solution)/shard_map/gts,bsgc->btgc/dot_general | solution.py:35
  38.6 1.2 copy.42
  40.0 7.8 %reshape.97 = bf16[32,128,255]{2,1,0:T(8,128)(2,1)} reshape(bf16[32,32640]{1,0:T(8,128)(2,1)S(1)} %slice.80) | data formatting | bytes 4177920 | tf_op jit(solution)/shard_map/reshape | solution.py:31
  48.2 2.3 %fusion.40 = f32[2,128,32,16]{1,3,0,2:T(8,128)S(1)} fusion(f32[32,2,16,128]{3,2,1,0:T(8,128)S(1)} %fusion.81, bf16[32,128,255]{2,1,0:T(8,128)(2,1)} %reshape.97, bf16[1,128,32,16]{1,3,0,2:T(8,128)(2,1)S(1)} %bitcast.60, bf16[1,128,32,16]{1,3,0,2:T(8,128)(2,1)S(1)} %bitcast.61), kind=kOutput, calls=%fused_computation.46 | convolution fusion | flops 33816576 | bytes 2359296 | tf_op jit(solution)/shard_map/gts,bsgc->btgc/dot_general | solution.py:35
  50.5 0.3 copy.34
  50.9 4.2 %collective-permute-start.2 = (bf16[256,512]{0,1:T(8,128)(2,1)S(1)}, bf16[256,512]{0,1:T(8,128)(2,1)S(1)}, u32[]{:S(2)}, u32[]{:S(2)}) collective-permute-start(bf16[256,512]{0,1:T(8,128)(2,1)S(1)} %fusion.82), channel_id=1, source_target_pairs={{0,64},{64,128},{128,192},{192,256},{256,320},{320,384},{384,448},... | collective-permute-start | bytes 786440 | tf_op jit(solution)/shard_map/ppermute | solution.py:69
  55.1 5.9 %collective-permute-done.2 = bf16[256,512]{0,1:T(8,128)(2,1)S(1)} collective-permute-done((bf16[256,512]{0,1:T(8,128)(2,1)S(1)}, bf16[256,512]{0,1:T(8,128)(2,1)S(1)}, u32[]{:S(2)}, u32[]{:S(2)}) %collective-permute-start.2) | collective-permute-done | bytes 262176 | tf_op jit(solution)/shard_map/ppermute | solution.py:69
  61.1 1.0 copy.35
  62.2 0.8 copy.36
  63.1 22.7 %all-gather.5.cloned.1.call-done = bf16[32,256,512]{2,1,0:T(8,128)(2,1)} async-done(((bf16[2,256,512]{2,1,0:T(8,128)(2,1)}), bf16[32,256,512]{2,1,0:T(8,128)(2,1)}) %all-gather.5.cloned.1.call-update) | async-done | bytes 8388624 | tf_op jit(solution)/shard_map/all_gather | solution.py:72
  85.8 6.5 %fusion.112 = (f32[256]{0:T(256)S(1)}, f32[256,8192]{0,1:T(8,128)S(1)}) fusion(bf16[256,512]{1,0:T(8,128)(2,1)S(1)} %copy-done.8, bf16[8192,512]{1,0:T(8,128)(2,1)} %bitcast.65, s32[256]{0:T(256)S(1)} %iota_add_fusion, s32[8192]{0:T(1024)S(1)} %fusion.102, pred[8192]{0:T(1024)(128)(4,1)S(1)} %broadcast_compare_fusion), kind=kOutput, calls=%fused_computation.106 | convolution fusion | flops 547356416 | bytes 10594304 | tf_op jit(solution)/shard_map/dot_general | solution.py:89
  92.3 2.4 %fusion.113 = (f32[256]{0:T(256)S(1)}, f32[256,8192]{0,1:T(8,128)S(1)}) fusion(bf16[256,512]{1,0:T(8,128)(2,1)S(1)} %copy-done.8, bf16[8192,512]{1,0:T(8,128)(2,1)S(1)} %bitcast.66, s32[256]{0:T(256)S(1)} %iota_add_fusion, s32[8192]{0:T(1024)S(1)} %fusion.102, pred[8192]{0:T(1024)(128)(4,1)S(1)} %broadcast_compare_fusion), kind=kOutput, calls=%fused_computation.107 | convolution fusion | flops 547356416 | bytes 10594304 | tf_op jit(solution)/shard_map/dot_general | solution.py:89
  94.7 2.4 %fusion.114 = (f32[256]{0:T(256)S(1)}, f32[256,8192]{0,1:T(8,128)S(1)}) fusion(bf16[256,512]{1,0:T(8,128)(2,1)S(1)} %copy-done.8, bf16[8192,512]{1,0:T(8,128)(2,1)S(1)} %bitcast.67, s32[256]{0:T(256)S(1)} %iota_add_fusion, s32[8192]{0:T(1024)S(1)} %fusion.102, pred[8192]{0:T(1024)(128)(4,1)S(1)} %broadcast_compare_fusion), kind=kOutput, calls=%fused_computation.108 | convolution fusion | flops 547356416 | bytes 10594304 | tf_op jit(solution)/shard_map/dot_general | solution.py:89
  97.0 2.4 %fusion.115 = (f32[256]{0:T(256)S(1)}, f32[256,8192]{0,1:T(8,128)S(1)}) fusion(bf16[256,512]{1,0:T(8,128)(2,1)S(1)} %copy-done.8, bf16[8192,512]{1,0:T(8,128)(2,1)S(1)} %bitcast.68, s32[256]{0:T(256)S(1)} %iota_add_fusion, s32[8192]{0:T(1024)S(1)} %fusion.102, pred[8192]{0:T(1024)(128)(4,1)S(1)} %broadcast_compare_fusion), kind=kOutput, calls=%fused_computation.109 | convolution fusion | flops 547356416 | bytes 10594304 | tf_op jit(solution)/shard_map/dot_general | solution.py:89
  99.4 1.4 copy-done.2
  100.8 2.4 %copy-done.1 = f32[256,8192]{0,1:T(8,128)} copy-done((f32[256,8192]{0,1:T(8,128)}, f32[256,8192]{0,1:T(8,128)S(1)}, u32[]{:S(2)}) %copy-start.1) | copy-done | bytes 8388632
  103.2 9.5 %fusion.8 = (f32[256]{0:T(256)S(1)}, f32[256]{0:T(256)S(1)}, f32[256]{0:T(256)S(1)}, f32[256]{0:T(256)S(1)}) fusion(f32[256,8192]{0,1:T(8,128)S(1)} %get-tuple-element.19, f32[256]{0:T(256)S(1)} %get-tuple-element.18, s32[256]{0:T(256)S(1)} %iota_add_fusion, s32[8192]{0:T(1024)S(1)} %fusion.102, pred[8192]{0:T(1024)(128)(4,1)S(1)} %broadcast_compare_fusion, ...), kind=kLoop, calls=%fused_computation.17 | loop fusion | flops 29359104 | bytes 33604608 | tf_op jit(solution)/shard_map/reduce_sum | solution.py:100
  112.7 32.6 %all-gather.7.cloned.1.call-done = bf16[32,256,512]{2,1,0:T(8,128)(2,1)} async-done(((bf16[2,256,512]{2,1,0:T(8,128)(2,1)}), bf16[32,256,512]{2,1,0:T(8,128)(2,1)}) %all-gather.7.cloned.1.call-update) | async-done | bytes 8388624 | tf_op jit(solution)/shard_map/all_gather | solution.py:72
  145.3 11.6 %fusion.46 = bf16[256,128]{0,1:T(8,128)(2,1)S(1)} fusion(bf16[8192,512]{1,0:T(8,128)(2,1)} %bitcast.69, f32[256,8192]{0,1:T(8,128)} %copy-done.4, f32[256]{0:T(256)S(1)} %get-tuple-element.18, s32[256]{0:T(256)S(1)} %iota_add_fusion, s32[8192]{0:T(1024)S(1)} %fusion.102, pred[8192]{0:T(1024)(128)(4,1)S(1)} %broadcast_compare_fusion, ...), kind=kOutput, calls=%fused_computation.48 | convolution fusion | flops 547422208 | bytes 10595328 | tf_op jit(solution)/shard_map/dot_general | solution.py:101
  157.0 3.1 %fusion.56 = bf16[256,128]{0,1:T(8,128)(2,1)S(1)} fusion(bf16[8192,512]{1,0:T(8,128)(2,1)S(1)} %bitcast.70, f32[256,8192]{0,1:T(8,128)S(1)} %copy-done.3, f32[256]{0:T(256)S(1)} %get-tuple-element.20, s32[256]{0:T(256)S(1)} %iota_add_fusion, s32[8192]{0:T(1024)S(1)} %fusion.102, pred[8192]{0:T(1024)(128)(4,1)S(1)} %broadcast_compare_fusion, ...), kind=kOutput, calls=%fused_computation.50 | convolution fusion | flops 547422208 | bytes 10595328 | tf_op jit(solution)/shard_map/dot_general | solution.py:101
  160.1 3.1 %fusion.66 = bf16[256,128]{0,1:T(8,128)(2,1)S(1)} fusion(bf16[8192,512]{1,0:T(8,128)(2,1)S(1)} %bitcast.71, f32[256,8192]{0,1:T(8,128)S(1)} %bitcast.55, f32[256]{0:T(256)S(1)} %get-tuple-element.22, s32[256]{0:T(256)S(1)} %iota_add_fusion, s32[8192]{0:T(1024)S(1)} %fusion.102, pred[8192]{0:T(1024)(128)(4,1)S(1)} %broadcast_compare_fusion, ...), kind=kOutput, calls=%fused_computation.52 | convolution fusion | flops 547422208 | bytes 10595328 | tf_op jit(solution)/shard_map/dot_general | solution.py:101
  163.2 3.1 %fusion.76 = bf16[256,128]{0,1:T(8,128)(2,1)S(1)} fusion(bf16[8192,512]{1,0:T(8,128)(2,1)S(1)} %bitcast.72, f32[256,8192]{0,1:T(8,128)S(1)} %bitcast.53, f32[256]{0:T(256)S(1)} %get-tuple-element.16, s32[256]{0:T(256)S(1)} %iota_add_fusion, s32[8192]{0:T(1024)S(1)} %fusion.102, pred[8192]{0:T(1024)(128)(4,1)S(1)} %broadcast_compare_fusion, ...), kind=kOutput, calls=%fused_computation.54 | convolution fusion | flops 547422208 | bytes 10595328 | tf_op jit(solution)/shard_map/dot_general | solution.py:101
  166.4 0.8 copy.37
  (50 shorter events, 1.6 us)
Async XLA Ops:
  7.2 78.6 %all-gather.5.cloned.1.call-start = ((), (), s32[]{:S(2)}) async-start(), calls=%async_computation | async-start | bytes 8912896 | tf_op jit(solution)/shard_map/all_gather | solution.py:72
  7.2 7.7 %collective-permute-start.1 = (bf16[256,512]{1,0:T(8,128)(2,1)}, bf16[256,512]{1,0:T(8,128)(2,1)S(1)}, u32[]{:S(2)}, u32[]{:S(2)}) collective-permute-start(bf16[256,512]{1,0:T(8,128)(2,1)} %param.11), channel_id=1, source_target_pairs={{0,64},{64,128},{128,192},{192,256},{256,320},{320,384},{384,448},... | collective-permute-start | bytes 786440 | tf_op jit(solution)/shard_map/ppermute | solution.py:69
  16.7 128.6 %all-gather.7.cloned.1.call-start = ((), (), s32[]{:S(2)}) async-start(), calls=%async_computation.1 | async-start | bytes 8912896 | tf_op jit(solution)/shard_map/all_gather | solution.py:72
  18.5 29.4 %collective-permute-start = (bf16[127,512]{1,0:T(8,128)(2,1)}, bf16[127,512]{1,0:T(8,128)(2,1)S(1)}, u32[]{:S(2)}, u32[]{:S(2)}) collective-permute-start(bf16[127,512]{1,0:T(8,128)(2,1)} %slice.78), channel_id=1, source_target_pairs={{0,4},{4,8},{8,12},{12,16},{16,20},{20,24},{24,28},{28,32},{32,36}... | collective-permute-start | bytes 390152 | tf_op jit(solution)/shard_map/ppermute | solution.py:21
  35.9 11.8 %copy-start.5 = (bf16[256,512]{1,0:T(8,128)(2,1)S(1)}, bf16[256,512]{1,0:T(8,128)(2,1)}, u32[]{:S(2)}) copy-start(bf16[256,512]{1,0:T(8,128)(2,1)} %param.6) | copy-start | bytes 786436
  39.8 46.0 %copy-start.8 = (bf16[256,512]{1,0:T(8,128)(2,1)S(1)}, bf16[256,512]{1,0:T(8,128)(2,1)}, u32[]{:S(2)}) copy-start(bf16[256,512]{1,0:T(8,128)(2,1)} %param.10) | copy-start | bytes 786436
  50.9 10.2 %collective-permute-start.2 = (bf16[256,512]{0,1:T(8,128)(2,1)S(1)}, bf16[256,512]{0,1:T(8,128)(2,1)S(1)}, u32[]{:S(2)}, u32[]{:S(2)}) collective-permute-start(bf16[256,512]{0,1:T(8,128)(2,1)S(1)} %fusion.82), channel_id=1, source_target_pairs={{0,64},{64,128},{128,192},{192,256},{256,320},{320,384},{384,448},... | collective-permute-start | bytes 786440 | tf_op jit(solution)/shard_map/ppermute | solution.py:69
  85.8 6.5 %copy-start.6 = (bf16[32,256,512]{2,1,0:T(8,128)(2,1)S(1)}, bf16[32,256,512]{2,1,0:T(8,128)(2,1)}, u32[]{:S(2)}) copy-start(bf16[32,256,512]{2,1,0:T(8,128)(2,1)} %all-gather.5.cloned.1.call-done) | copy-start | bytes 25165828
  92.3 7.1 %copy-start = (f32[256,8192]{0,1:T(8,128)}, f32[256,8192]{0,1:T(8,128)S(1)}, u32[]{:S(2)}) copy-start(f32[256,8192]{0,1:T(8,128)S(1)} %get-tuple-element.17) | copy-start | bytes 25165828
  94.7 4.8 %copy-start.4 = (f32[256,8192]{0,1:T(8,128)}, f32[256,8192]{0,1:T(8,128)S(1)}, u32[]{:S(2)}) copy-start(f32[256,8192]{0,1:T(8,128)S(1)} %get-tuple-element.19) | copy-start | bytes 25165828
  97.0 3.8 %copy-start.2 = (f32[256,8192]{0,1:T(8,128)}, f32[256,8192]{0,1:T(8,128)S(1)}, u32[]{:S(2)}) copy-start(f32[256,8192]{0,1:T(8,128)S(1)} %get-tuple-element.21) | copy-start | bytes 25165828
  99.4 3.8 %copy-start.1 = (f32[256,8192]{0,1:T(8,128)}, f32[256,8192]{0,1:T(8,128)S(1)}, u32[]{:S(2)}) copy-start(f32[256,8192]{0,1:T(8,128)S(1)} %get-tuple-element.23) | copy-start | bytes 25165828
  145.3 11.6 %copy-start.3 = (f32[256,8192]{0,1:T(8,128)S(1)}, f32[256,8192]{0,1:T(8,128)}, u32[]{:S(2)}) copy-start(f32[256,8192]{0,1:T(8,128)} %copy-done.2) | copy-start | bytes 25165828
  145.3 11.6 %copy-start.7 = (bf16[32,256,512]{2,1,0:T(8,128)(2,1)S(1)}, bf16[32,256,512]{2,1,0:T(8,128)(2,1)}, u32[]{:S(2)}) copy-start(bf16[32,256,512]{2,1,0:T(8,128)(2,1)} %all-gather.7.cloned.1.call-done) | copy-start | bytes 25165828
  145.3 14.7 %slice-start.2 = ((s8[8388608]{0:T(1024)(128)(4,1)}), s8[4194304]{0:T(1024)(128)(4,1)S(1)}, s32[]{:S(2)}) async-start(s8[8388608]{0:T(1024)(128)(4,1)} %bitcast.54), calls=%async_computation.4 | async-start | bytes 8388608
  156.9 3.2 %slice-start.3 = ((s8[8388608]{0:T(1024)(128)(4,1)}), s8[4194304]{0:T(1024)(128)(4,1)S(1)}, s32[]{:S(2)}) async-start(s8[8388608]{0:T(1024)(128)(4,1)} %bitcast.54), calls=%async_computation.5 | async-start | bytes 8388608
  157.0 6.3 %slice-start = ((s8[8388608]{0:T(1024)(128)(4,1)}), s8[4194304]{0:T(1024)(128)(4,1)S(1)}, s32[]{:S(2)}) async-start(s8[8388608]{0:T(1024)(128)(4,1)} %bitcast.52), calls=%async_computation.2 | async-start | bytes 8388608
  160.1 3.1 %slice-start.1 = ((s8[8388608]{0:T(1024)(128)(4,1)}), s8[4194304]{0:T(1024)(128)(4,1)S(1)}, s32[]{:S(2)}) async-start(s8[8388608]{0:T(1024)(128)(4,1)} %bitcast.52), calls=%async_computation.3 | async-start | bytes 8388608
Sparse Core Ops, SparseCore 0:
  16.8 68.9 all-gather.4
  87.9 57.3 all-gather.6
where the time goes:
time: 174 us
  waiting for transfers between devices  64.9 us (37%)
  matrix products  39.1 us (22%)
  local copies, waits for them, and re-layouts  27.6 us (16%)
  starting transfers between devices  15.4 us (9%)
  between operations  14.4 us (8%)
  other arithmetic  12.6 us (7%)
    all_gather x2, waiting for transfers between devices, row_gather(): lax.all_gather(jnp.stack([array, row_down(array)]), ('col', 'core'), axis=0)  55.4 us
    dot_general x4, matrix products, body(): jnp.dot(exp_terms.astype(jnp.bfloat16), values_all[:, lanes], preferred_e...  20.9 us
    reshape x2, local copies, waits for them, and re-layouts, toeplitz_taps(): flat.reshape(groups, kernel, 2 * kernel - 1)  15.6 us
    dot_general x4, matrix products, body(): lax.dot_general(query_rows[:, lanes], keys_all[:, lanes], (((1,), (1,)),...  13.5 us
    ppermute x2, waiting for transfers between devices, row_down(): return lax.ppermute(array, 'row', [(r, r + 1) for r in range(rows - 1)])  9.51 us
    reduce_sum x1, other arithmetic, body(): row_total = jnp.sum(exp_terms, axis=1, keepdims=True)  9.49 us
    ppermute x2, starting transfers between devices, row_down(): return lax.ppermute(array, 'row', [(r, r + 1) for r in range(rows - 1)])  8.29 us
    unnamed x32, local copies, waits for them, and re-layouts  8.16 us
  transfers between devices with their start and end apart: 5, of which 4 were waited for; matrix products, arithmetic and copies ran while one was open for 30% of the time, Pallas kernels for 0%

commit v1 on v0

--- a/solution.py
+++ b/solution.py
@@ -98,9 +98,8 @@
         row_peak = jnp.max(scores, axis=1, keepdims=True)
         exp_terms = jnp.where(visible, jnp.exp(scores - row_peak), 0.0)
         row_total = jnp.sum(exp_terms, axis=1, keepdims=True)
-        weighted = jnp.dot(
-            exp_terms.astype(jnp.bfloat16), values_all[:, lanes], preferred_element_type=jnp.float32
-        )
+        weights, row_total = lax.optimization_barrier((exp_terms.astype(jnp.bfloat16), row_total))
+        weighted = jnp.dot(weights, values_all[:, lanes], preferred_element_type=jnp.float32)
         head_outputs.append((weighted / row_total).astype(jnp.bfloat16))
     attended = jnp.concatenate(head_outputs, axis=1)
     return (mixed, attended)

time: 174 us -> 164 us (0.943)
  matrix products: 39.1 us -> 32.5 us
  local copies, waits for them, and re-layouts: 27.6 us -> 23.9 us
    dot_general x4, matrix products: 20.9 us -> 10.7 us  [body(): jnp.dot(weights, values_all[:, lanes], preferred_element_type=jnp.float32)]
    unnamed x32 -> x18, local copies, waits for them, and re-layouts: 8.16 us -> 4.49 us
    dot_general x4, matrix products: 13.5 us -> 17.2 us  [body(): lax.dot_general(query_rows[:, lanes], keys_all[:, lanes], (((1,), (1,)),...]
    reduce_sum x1, other arithmetic: 9.49 us -> 11.3 us  [body(): row_total = jnp.sum(exp_terms, axis=1, keepdims=True)]
  transfers between devices with their start and end apart: 5 -> 5, of which waited for: 4 -> 4; matrix products, arithmetic and copies ran while one was open for 30% -> 35% of each run, Pallas kernels for 0% -> 0%
where the time goes in v1:
time: 164 us
  waiting for transfers between devices  63.3 us (39%)
  matrix products  32.5 us (20%)
  local copies, waits for them, and re-layouts  23.9 us (15%)
  starting transfers between devices  15.4 us (9%)
  other arithmetic  14.3 us (9%)
  between operations  14.3 us (9%)
    all_gather x2, waiting for transfers between devices, row_gather(): lax.all_gather(jnp.stack([array, row_down(array)]), ('col', 'core'), axis=0)  53.8 us
    dot_general x4, matrix products, body(): lax.dot_general(query_rows[:, lanes], keys_all[:, lanes], (((1,), (1,)),...  17.2 us
    reshape x2, local copies, waits for them, and re-layouts, toeplitz_taps(): flat.reshape(groups, kernel, 2 * kernel - 1)  15.6 us
    reduce_sum x1, other arithmetic, body(): row_total = jnp.sum(exp_terms, axis=1, keepdims=True)  11.3 us
    dot_general x4, matrix products, body(): jnp.dot(weights, values_all[:, lanes], preferred_element_type=jnp.float32)  10.7 us
    ppermute x2, waiting for transfers between devices, row_down(): return lax.ppermute(array, 'row', [(r, r + 1) for r in range(rows - 1)])  9.51 us
    ppermute x2, starting transfers between devices, row_down(): return lax.ppermute(array, 'row', [(r, r + 1) for r in range(rows - 1)])  8.28 us
    ppermute x1, starting transfers between devices, passed_along(): return lax.ppermute(block, axis, route)  7.08 us
  transfers between devices with their start and end apart: 5, of which 4 were waited for; matrix products, arithmetic and copies ran while one was open for 35% of the time, Pallas kernels for 0%

profile of v1, /device:TPU:1, one launch (start us, length us, event | category | flops | bytes accessed | tf_op | source)
XLA Modules:
  0.0 163.9 jit_solution(15683055214356908501)
XLA Ops:
  7.2 4.0 %collective-permute-start.1 = (bf16[256,512]{1,0:T(8,128)(2,1)}, bf16[256,512]{1,0:T(8,128)(2,1)S(1)}, u32[]{:S(2)}, u32[]{:S(2)}) collective-permute-start(bf16[256,512]{1,0:T(8,128)(2,1)} %param.11), channel_id=1, source_target_pairs={{0,64},{64,128},{128,192},{192,256},{256,320},{320,384},{384,448},... | collective-permute-start | bytes 786440 | tf_op jit(solution)/shard_map/ppermute | solution.py:69
  11.3 3.6 %collective-permute-done.1 = bf16[256,512]{1,0:T(8,128)(2,1)S(1)} collective-permute-done((bf16[256,512]{1,0:T(8,128)(2,1)}, bf16[256,512]{1,0:T(8,128)(2,1)S(1)}, u32[]{:S(2)}, u32[]{:S(2)}) %collective-permute-start.1) | collective-permute-done | bytes 262176 | tf_op jit(solution)/shard_map/ppermute | solution.py:69
  14.9 1.8 %pad_maximum_fusion = bf16[2,256,512]{2,1,0:T(8,128)(2,1)} fusion(bf16[1,256,512]{2,1,0:T(8,128)(2,1)S(1)} %bitcast.71, bf16[1,256,512]{2,1,0:T(8,128)(2,1)} %bitcast.70), kind=kLoop, calls=%fused_computation.52 | loop fusion | flops 262144 | bytes 1048576 | tf_op jit(solution)/shard_map/stack | solution.py:72
  16.7 1.1 multiply_convert_fusion
  17.8 0.7 slice.78
  18.5 7.1 %collective-permute-start = (bf16[127,512]{1,0:T(8,128)(2,1)}, bf16[127,512]{1,0:T(8,128)(2,1)S(1)}, u32[]{:S(2)}, u32[]{:S(2)}) collective-permute-start(bf16[127,512]{1,0:T(8,128)(2,1)} %slice.78), channel_id=1, source_target_pairs={{0,4},{4,8},{8,12},{12,16},{16,20},{20,24},{24,28},{28,32},{32,36}... | collective-permute-start | bytes 390152 | tf_op jit(solution)/shard_map/ppermute | solution.py:21
  25.8 0.8 rev.4
  26.6 0.1 tile.8
  26.7 1.2 copy.41
  28.1 7.8 %reshape.91 = bf16[32,128,255]{2,1,0:T(8,128)(2,1)} reshape(bf16[32,32640]{1,0:T(8,128)(2,1)S(1)} %slice.76) | data formatting | bytes 4177920 | tf_op jit(solution)/shard_map/reshape | solution.py:31
  35.9 2.4 %fusion.53 = f32[32,2,16,128]{3,2,1,0:T(8,128)S(1)} fusion(bf16[32,128,255]{2,1,0:T(8,128)(2,1)} %reshape.91, bf16[2,128,32,16]{1,0,3,2:T(2,128)(2,1)S(1)} %reshape.90), kind=kOutput, calls=%fused_computation.49 | convolution fusion | flops 33554432 | bytes 1835008 | tf_op jit(solution)/shard_map/gts,bsgc->btgc/dot_general | solution.py:35
  38.4 0.1 tile.20
  38.6 1.2 copy.42
  40.0 7.8 %reshape.93 = bf16[32,128,255]{2,1,0:T(8,128)(2,1)} reshape(bf16[32,32640]{1,0:T(8,128)(2,1)S(1)} %slice.80) | data formatting | bytes 4177920 | tf_op jit(solution)/shard_map/reshape | solution.py:31
  48.2 2.3 %fusion.28 = f32[2,128,32,16]{1,3,0,2:T(8,128)S(1)} fusion(f32[32,2,16,128]{3,2,1,0:T(8,128)S(1)} %fusion.53, bf16[32,128,255]{2,1,0:T(8,128)(2,1)} %reshape.93, bf16[1,128,32,16]{1,3,0,2:T(8,128)(2,1)S(1)} %bitcast.68, bf16[1,128,32,16]{1,3,0,2:T(8,128)(2,1)S(1)} %bitcast.69), kind=kOutput, calls=%fused_computation.38 | convolution fusion | flops 33816576 | bytes 2359296 | tf_op jit(solution)/shard_map/gts,bsgc->btgc/dot_general | solution.py:35
  50.5 0.3 copy.34
  50.9 4.2 %collective-permute-start.2 = (bf16[256,512]{0,1:T(8,128)(2,1)S(1)}, bf16[256,512]{0,1:T(8,128)(2,1)S(1)}, u32[]{:S(2)}, u32[]{:S(2)}) collective-permute-start(bf16[256,512]{0,1:T(8,128)(2,1)S(1)} %fusion.54), channel_id=1, source_target_pairs={{0,64},{64,128},{128,192},{192,256},{256,320},{320,384},{384,448},... | collective-permute-start | bytes 786440 | tf_op jit(solution)/shard_map/ppermute | solution.py:69
  55.1 5.9 %collective-permute-done.2 = bf16[256,512]{0,1:T(8,128)(2,1)S(1)} collective-permute-done((bf16[256,512]{0,1:T(8,128)(2,1)S(1)}, bf16[256,512]{0,1:T(8,128)(2,1)S(1)}, u32[]{:S(2)}, u32[]{:S(2)}) %collective-permute-start.2) | collective-permute-done | bytes 262176 | tf_op jit(solution)/shard_map/ppermute | solution.py:69
  61.1 1.1 copy.35
  62.2 0.8 copy.36
  63.1 22.7 %all-gather.5.cloned.1.call-done = bf16[32,256,512]{2,1,0:T(8,128)(2,1)} async-done(((bf16[2,256,512]{2,1,0:T(8,128)(2,1)}), bf16[32,256,512]{2,1,0:T(8,128)(2,1)}) %all-gather.5.cloned.1.call-update) | async-done | bytes 8388624 | tf_op jit(solution)/shard_map/all_gather | solution.py:72
  85.8 6.5 %fusion.80 = (f32[256]{0:T(256)S(1)}, f32[256,8192]{0,1:T(8,128)S(1)}) fusion(bf16[256,512]{1,0:T(8,128)(2,1)S(1)} %copy-done.5, bf16[8192,512]{1,0:T(8,128)(2,1)} %bitcast.73, s32[256]{0:T(256)S(1)} %iota_add_fusion, s32[8192]{0:T(1024)S(1)} %fusion.74, pred[8192]{0:T(1024)(128)(4,1)S(1)} %broadcast_compare_fusion), kind=kOutput, calls=%fused_computation.94 | convolution fusion | flops 547356416 | bytes 10594304 | tf_op jit(solution)/shard_map/dot_general | solution.py:89
  92.3 2.4 %fusion.81 = (f32[256]{0:T(256)S(1)}, f32[256,8192]{0,1:T(8,128)S(1)}) fusion(bf16[256,512]{1,0:T(8,128)(2,1)S(1)} %copy-done.5, bf16[8192,512]{1,0:T(8,128)(2,1)S(1)} %bitcast.75, s32[256]{0:T(256)S(1)} %iota_add_fusion, s32[8192]{0:T(1024)S(1)} %fusion.74, pred[8192]{0:T(1024)(128)(4,1)S(1)} %broadcast_compare_fusion), kind=kOutput, calls=%fused_computation.95 | convolution fusion | flops 547356416 | bytes 10594304 | tf_op jit(solution)/shard_map/dot_general | solution.py:89
  94.6 2.4 %fusion.82 = (f32[256]{0:T(256)S(1)}, f32[256,8192]{0,1:T(8,128)S(1)}) fusion(bf16[256,512]{1,0:T(8,128)(2,1)S(1)} %copy-done.5, bf16[8192,512]{1,0:T(8,128)(2,1)S(1)} %bitcast.76, s32[256]{0:T(256)S(1)} %iota_add_fusion, s32[8192]{0:T(1024)S(1)} %fusion.74, pred[8192]{0:T(1024)(128)(4,1)S(1)} %broadcast_compare_fusion), kind=kOutput, calls=%fused_computation.96 | convolution fusion | flops 547356416 | bytes 10594304 | tf_op jit(solution)/shard_map/dot_general | solution.py:89
  97.0 6.0 %fusion.83 = (f32[256]{0:T(256)S(1)}, f32[256,8192]{0,1:T(8,128)S(1)}) fusion(bf16[256,512]{1,0:T(8,128)(2,1)S(1)} %copy-done.5, bf16[8192,512]{1,0:T(8,128)(2,1)} %bitcast.74, s32[256]{0:T(256)S(1)} %iota_add_fusion, s32[8192]{0:T(1024)S(1)} %fusion.74, pred[8192]{0:T(1024)(128)(4,1)S(1)} %broadcast_compare_fusion), kind=kOutput, calls=%fused_computation.97 | convolution fusion | flops 547356416 | bytes 10594304 | tf_op jit(solution)/shard_map/dot_general | solution.py:89
  103.0 11.3 %fusion.8 = (f32[256]{0:T(256)S(1)}, f32[256]{0:T(256)S(1)}, f32[256]{0:T(256)S(1)}, f32[256]{0:T(256)S(1)}, bf16[256,8192]{0,1:T(8,128)(2,1)}, /*index=5*/bf16[...) fusion(f32[256,8192]{0,1:T(8,128)S(1)} %get-tuple-element.37, f32[256]{0:T(256)S(1)} %get-tuple-element.36, ...), kind=kLoop, calls=%fused_computation.17 | loop fusion | flops 37747712 | bytes 50381824 | tf_op jit(solution)/shard_map/reduce_sum | solution.py:100
  114.2 31.1 %all-gather.7.cloned.1.call-done = bf16[32,256,512]{2,1,0:T(8,128)(2,1)} async-done(((bf16[2,256,512]{2,1,0:T(8,128)(2,1)}), bf16[32,256,512]{2,1,0:T(8,128)(2,1)}) %all-gather.7.cloned.1.call-update) | async-done | bytes 8388624 | tf_op jit(solution)/shard_map/all_gather | solution.py:72
  145.3 4.0 %fusion.32 = bf16[256,128]{0,1:T(8,128)(2,1)S(1)} fusion(bf16[256,8192]{0,1:T(8,128)(2,1)} %get-tuple-element.10, bf16[8192,512]{1,0:T(8,128)(2,1)} %bitcast.77, f32[256]{0:T(256)S(1)} %get-tuple-element.26), kind=kOutput, calls=%fused_computation.40 | convolution fusion | flops 536936448 | bytes 6358016 | tf_op jit(solution)/shard_map/dot_general | solution.py:102
  149.3 4.6 %fusion.38 = bf16[256,128]{0,1:T(8,128)(2,1)S(1)} fusion(bf16[256,8192]{0,1:T(8,128)(2,1)} %get-tuple-element.12, bf16[8192,512]{1,0:T(8,128)(2,1)} %bitcast.78, f32[256]{0:T(256)S(1)} %get-tuple-element.27), kind=kOutput, calls=%fused_computation.42 | convolution fusion | flops 536936448 | bytes 6358016 | tf_op jit(solution)/shard_map/dot_general | solution.py:102
  154.0 1.0 fusion.44
  155.1 1.0 fusion.50
  156.2 0.8 copy.37
  (34 shorter events, 1.4 us)
Async XLA Ops:
  7.2 78.6 %all-gather.5.cloned.1.call-start = ((), (), s32[]{:S(2)}) async-start(), calls=%async_computation | async-start | bytes 8912896 | tf_op jit(solution)/shard_map/all_gather | solution.py:72
  7.2 7.7 %collective-permute-start.1 = (bf16[256,512]{1,0:T(8,128)(2,1)}, bf16[256,512]{1,0:T(8,128)(2,1)S(1)}, u32[]{:S(2)}, u32[]{:S(2)}) collective-permute-start(bf16[256,512]{1,0:T(8,128)(2,1)} %param.11), channel_id=1, source_target_pairs={{0,64},{64,128},{128,192},{192,256},{256,320},{320,384},{384,448},... | collective-permute-start | bytes 786440 | tf_op jit(solution)/shard_map/ppermute | solution.py:69
  16.7 128.6 %all-gather.7.cloned.1.call-start = ((), (), s32[]{:S(2)}) async-start(), calls=%async_computation.1 | async-start | bytes 8912896 | tf_op jit(solution)/shard_map/all_gather | solution.py:72
  18.5 29.4 %collective-permute-start = (bf16[127,512]{1,0:T(8,128)(2,1)}, bf16[127,512]{1,0:T(8,128)(2,1)S(1)}, u32[]{:S(2)}, u32[]{:S(2)}) collective-permute-start(bf16[127,512]{1,0:T(8,128)(2,1)} %slice.78), channel_id=1, source_target_pairs={{0,4},{4,8},{8,12},{12,16},{16,20},{20,24},{24,28},{28,32},{32,36}... | collective-permute-start | bytes 390152 | tf_op jit(solution)/shard_map/ppermute | solution.py:21
  35.9 11.9 %copy-start.2 = (bf16[256,512]{1,0:T(8,128)(2,1)S(1)}, bf16[256,512]{1,0:T(8,128)(2,1)}, u32[]{:S(2)}) copy-start(bf16[256,512]{1,0:T(8,128)(2,1)} %param.6) | copy-start | bytes 786436
  39.8 46.0 %copy-start.5 = (bf16[256,512]{1,0:T(8,128)(2,1)S(1)}, bf16[256,512]{1,0:T(8,128)(2,1)}, u32[]{:S(2)}) copy-start(bf16[256,512]{1,0:T(8,128)(2,1)} %param.10) | copy-start | bytes 786436
  50.9 10.2 %collective-permute-start.2 = (bf16[256,512]{0,1:T(8,128)(2,1)S(1)}, bf16[256,512]{0,1:T(8,128)(2,1)S(1)}, u32[]{:S(2)}, u32[]{:S(2)}) collective-permute-start(bf16[256,512]{0,1:T(8,128)(2,1)S(1)} %fusion.54), channel_id=1, source_target_pairs={{0,64},{64,128},{128,192},{192,256},{256,320},{320,384},{384,448},... | collective-permute-start | bytes 786440 | tf_op jit(solution)/shard_map/ppermute | solution.py:69
  85.8 6.5 %copy-start.3 = (bf16[32,256,512]{2,1,0:T(8,128)(2,1)S(1)}, bf16[32,256,512]{2,1,0:T(8,128)(2,1)}, u32[]{:S(2)}) copy-start(bf16[32,256,512]{2,1,0:T(8,128)(2,1)} %all-gather.5.cloned.1.call-done) | copy-start | bytes 25165828
  145.3 8.7 %copy-start.1 = (bf16[256,8192]{0,1:T(8,128)(2,1)S(1)}, bf16[256,8192]{0,1:T(8,128)(2,1)}, u32[]{:S(2)}) copy-start(bf16[256,8192]{0,1:T(8,128)(2,1)} %get-tuple-element.14) | copy-start | bytes 12582916
  145.3 8.7 %copy-start.4 = (bf16[32,256,512]{2,1,0:T(8,128)(2,1)S(1)}, bf16[32,256,512]{2,1,0:T(8,128)(2,1)}, u32[]{:S(2)}) copy-start(bf16[32,256,512]{2,1,0:T(8,128)(2,1)} %all-gather.7.cloned.1.call-done) | copy-start | bytes 25165828
  149.3 5.8 %copy-start = (bf16[256,8192]{0,1:T(8,128)(2,1)S(1)}, bf16[256,8192]{0,1:T(8,128)(2,1)}, u32[]{:S(2)}) copy-start(bf16[256,8192]{0,1:T(8,128)(2,1)} %get-tuple-element.16) | copy-start | bytes 12582916
Sparse Core Ops, SparseCore 0:
  16.8 68.9 all-gather.4
  87.9 57.3 all-gather.6

commit v2 on v1

--- a/solution.py
+++ b/solution.py
@@ -23,12 +23,12 @@
 
 def toeplitz_taps(filters, offset):
     groups, kernel = filters.shape
-    flipped = filters[:, ::-1]
-    zeros = jnp.zeros_like(flipped)
-    pieces = [flipped, zeros] if offset == 0 else [zeros, flipped]
-    lags = jnp.concatenate(pieces, axis=1)
-    flat = jnp.tile(lags, (1, kernel))[:, : kernel * (2 * kernel - 1)]
-    return flat.reshape(groups, kernel, 2 * kernel - 1)[:, :, kernel - 1 : 2 * kernel - 1]
+    lag = jnp.arange(kernel, dtype=jnp.int32)[:, None, None]
+    out_row = jnp.arange(kernel, dtype=jnp.int32)[None, :, None]
+    in_row = jnp.arange(kernel, dtype=jnp.int32)[None, None, :]
+    picks = (out_row - in_row + offset == lag).astype(filters.dtype).reshape(kernel, kernel * kernel)
+    taps = jnp.dot(filters, picks, preferred_element_type=jnp.float32)
+    return taps.astype(filters.dtype).reshape(groups, kernel, kernel)
 
 
 def apply_blocks(matrix, blocks):

time: 164 us -> 164 us (level)
  local copies, waits for them, and re-layouts: 23.9 us -> 4.41 us
  waiting for transfers between devices: 63.3 us -> 82.7 us
    all_gather x2, waiting for transfers between devices: 53.8 us -> 75.7 us  [row_gather(): lax.all_gather(jnp.stack([array, row_down(array)]), ('col', 'core'), axis=0)]
    reshape x2 -> x0, local copies, waits for them, and re-layouts: 15.6 us -> none  [toeplitz_taps(): flat.reshape(groups, kernel, 2 * kernel - 1)]
    dot_general x0 -> x2, matrix products: none -> 3.54 us  [toeplitz_taps(): taps = jnp.dot(filters, picks, preferred_element_type=jnp.float32)]
    dot_general x2, matrix products: 4.68 us -> 1.29 us  [apply_blocks(): jnp.einsum('gts,bsgc->btgc', matrix, blocks, preferred_element_type=jnp.f...]
    ppermute x2, waiting for transfers between devices: 9.51 us -> 6.92 us  [row_down(): return lax.ppermute(array, 'row', [(r, r + 1) for r in range(rows - 1)])]
    unnamed x18 -> x22, local copies, waits for them, and re-layouts: 4.49 us -> 2.6 us
  transfers between devices with their start and end apart: 5 -> 5, of which waited for: 4 -> 4; matrix products, arithmetic and copies ran while one was open for 35% -> 23% of each run, Pallas kernels for 0% -> 0%
where the time goes in v2:
time: 164 us
  waiting for transfers between devices  82.7 us (50%)
  matrix products  32.6 us (20%)
  starting transfers between devices  15.4 us (9%)
  other arithmetic  14.4 us (9%)
  between operations  14.4 us (9%)
  local copies, waits for them, and re-layouts  4.41 us (3%)
    all_gather x2, waiting for transfers between devices, row_gather(): lax.all_gather(jnp.stack([array, row_down(array)]), ('col', 'core'), axis=0)  75.7 us
    dot_general x4, matrix products, body(): lax.dot_general(query_rows[:, lanes], keys_all[:, lanes], (((1,), (1,)),...  17.2 us
    reduce_sum x1, other arithmetic, body(): row_total = jnp.sum(exp_terms, axis=1, keepdims=True)  11.3 us
    dot_general x4, matrix products, body(): jnp.dot(weights, values_all[:, lanes], preferred_element_type=jnp.float32)  10.6 us
    ppermute x2, starting transfers between devices, row_down(): return lax.ppermute(array, 'row', [(r, r + 1) for r in range(rows - 1)])  8.24 us
    ppermute x1, starting transfers between devices, passed_along(): return lax.ppermute(block, axis, route)  7.09 us
    ppermute x2, waiting for transfers between devices, row_down(): return lax.ppermute(array, 'row', [(r, r + 1) for r in range(rows - 1)])  6.92 us
    dot_general x2, matrix products, toeplitz_taps(): taps = jnp.dot(filters, picks, preferred_element_type=jnp.float32)  3.54 us
  transfers between devices with their start and end apart: 5, of which 4 were waited for; matrix products, arithmetic and copies ran while one was open for 23% of the time, Pallas kernels for 0%

profile of v2, /device:TPU:1, one launch (start us, length us, event | category | flops | bytes accessed | tf_op | source)
XLA Modules:
  0.0 163.9 jit_solution(9345730913668698959)
XLA Ops:
  7.2 4.0 %collective-permute-start.1 = (bf16[256,512]{1,0:T(8,128)(2,1)}, bf16[256,512]{1,0:T(8,128)(2,1)S(1)}, u32[]{:S(2)}, u32[]{:S(2)}) collective-permute-start(bf16[256,512]{1,0:T(8,128)(2,1)} %param.11), channel_id=1, source_target_pairs={{0,64},{64,128},{128,192},{192,256},{256,320},{320,384},{384,448},... | collective-permute-start | bytes 786440 | tf_op jit(solution)/shard_map/ppermute | solution.py:69
  11.3 3.6 %collective-permute-done.1 = bf16[256,512]{1,0:T(8,128)(2,1)S(1)} collective-permute-done((bf16[256,512]{1,0:T(8,128)(2,1)}, bf16[256,512]{1,0:T(8,128)(2,1)S(1)}, u32[]{:S(2)}, u32[]{:S(2)}) %collective-permute-start.1) | collective-permute-done | bytes 262176 | tf_op jit(solution)/shard_map/ppermute | solution.py:69
  14.9 1.8 %pad_maximum_fusion = bf16[2,256,512]{2,1,0:T(8,128)(2,1)} fusion(bf16[1,256,512]{2,1,0:T(8,128)(2,1)S(1)} %bitcast.79, bf16[1,256,512]{2,1,0:T(8,128)(2,1)} %bitcast.78), kind=kLoop, calls=%fused_computation.60 | loop fusion | flops 262144 | bytes 1048576 | tf_op jit(solution)/shard_map/stack | solution.py:72
  16.8 1.1 multiply_convert_fusion
  17.9 7.1 %collective-permute-start = (bf16[127,512]{1,0:T(8,128)(2,1)S(1)}, bf16[127,512]{1,0:T(8,128)(2,1)S(1)}, u32[]{:S(2)}, u32[]{:S(2)}) collective-permute-start(bf16[127,512]{1,0:T(8,128)(2,1)S(1)} %slice.60), channel_id=1, source_target_pairs={{0,4},{4,8},{8,12},{12,16},{16,20},{20,24},{24,28},{28,32},{32,36}... | collective-permute-start | bytes 390152 | tf_op jit(solution)/shard_map/ppermute | solution.py:21
  25.0 0.1 copy.30
  25.3 1.8 %fusion.30 = bf16[4,8,128,128]{3,1,2,0:T(8,128)(2,1)S(1)} fusion(bf16[32,128]{1,0:T(8,128)(2,1)S(1)} %copy-done, s32[16384]{0:T(1024)S(1)} %subtract_bitcast_fusion), kind=kOutput, calls=%fused_computation.43 | convolution fusion | flops 136839168 | bytes 1122304 | tf_op jit(solution)/shard_map/dot_general | solution.py:30
  27.1 0.2 copy.41
  27.5 0.6 fusion.58
  28.1 1.8 %fusion.31 = bf16[4,8,128,128]{3,1,2,0:T(8,128)(2,1)S(1)} fusion(bf16[32,128]{1,0:T(8,128)(2,1)S(1)} %copy-done, s32[16384]{0:T(1024)S(1)} %broadcast_add_fusion), kind=kOutput, calls=%fused_computation.44 | convolution fusion | flops 136839168 | bytes 1122304 | tf_op jit(solution)/shard_map/dot_general | solution.py:30
  29.9 0.2 copy.42
  30.2 0.1 copy.29
  30.3 0.1 copy.40
  30.6 0.6 fusion.32
  31.2 0.3 copy.34
  31.6 4.2 %collective-permute-start.2 = (bf16[256,512]{0,1:T(8,128)(2,1)S(1)}, bf16[256,512]{0,1:T(8,128)(2,1)S(1)}, u32[]{:S(2)}, u32[]{:S(2)}) collective-permute-start(bf16[256,512]{0,1:T(8,128)(2,1)S(1)} %fusion.60), channel_id=1, source_target_pairs={{0,64},{64,128},{128,192},{192,256},{256,320},{320,384},{384,448},... | collective-permute-start | bytes 786440 | tf_op jit(solution)/shard_map/ppermute | solution.py:69
  35.8 3.3 %collective-permute-done.2 = bf16[256,512]{0,1:T(8,128)(2,1)S(1)} collective-permute-done((bf16[256,512]{0,1:T(8,128)(2,1)S(1)}, bf16[256,512]{0,1:T(8,128)(2,1)S(1)}, u32[]{:S(2)}, u32[]{:S(2)}) %collective-permute-start.2) | collective-permute-done | bytes 262176 | tf_op jit(solution)/shard_map/ppermute | solution.py:69
  39.2 1.1 copy.35
  40.3 0.8 copy.36
  41.2 44.7 %all-gather.5.cloned.1.call-done = bf16[32,256,512]{2,1,0:T(8,128)(2,1)} async-done(((bf16[2,256,512]{2,1,0:T(8,128)(2,1)}), bf16[32,256,512]{2,1,0:T(8,128)(2,1)}) %all-gather.5.cloned.1.call-update) | async-done | bytes 8388624 | tf_op jit(solution)/shard_map/all_gather | solution.py:72
  85.9 6.5 %fusion.85 = (f32[256]{0:T(256)S(1)}, f32[256,8192]{0,1:T(8,128)S(1)}) fusion(bf16[256,512]{1,0:T(8,128)(2,1)S(1)} %copy-done.7, bf16[8192,512]{1,0:T(8,128)(2,1)} %bitcast.81, s32[256]{0:T(256)S(1)} %iota_add_fusion, s32[8192]{0:T(1024)S(1)} %fusion.80, pred[8192]{0:T(1024)(128)(4,1)S(1)} %broadcast_compare_fusion), kind=kOutput, calls=%fused_computation.103 | convolution fusion | flops 547356416 | bytes 10594304 | tf_op jit(solution)/shard_map/dot_general | solution.py:89
  92.3 2.4 %fusion.86 = (f32[256]{0:T(256)S(1)}, f32[256,8192]{0,1:T(8,128)S(1)}) fusion(bf16[256,512]{1,0:T(8,128)(2,1)S(1)} %copy-done.7, bf16[8192,512]{1,0:T(8,128)(2,1)S(1)} %bitcast.83, s32[256]{0:T(256)S(1)} %iota_add_fusion, s32[8192]{0:T(1024)S(1)} %fusion.80, pred[8192]{0:T(1024)(128)(4,1)S(1)} %broadcast_compare_fusion), kind=kOutput, calls=%fused_computation.104 | convolution fusion | flops 547356416 | bytes 10594304 | tf_op jit(solution)/shard_map/dot_general | solution.py:89
  94.7 2.4 %fusion.87 = (f32[256]{0:T(256)S(1)}, f32[256,8192]{0,1:T(8,128)S(1)}) fusion(bf16[256,512]{1,0:T(8,128)(2,1)S(1)} %copy-done.7, bf16[8192,512]{1,0:T(8,128)(2,1)S(1)} %bitcast.84, s32[256]{0:T(256)S(1)} %iota_add_fusion, s32[8192]{0:T(1024)S(1)} %fusion.80, pred[8192]{0:T(1024)(128)(4,1)S(1)} %broadcast_compare_fusion), kind=kOutput, calls=%fused_computation.105 | convolution fusion | flops 547356416 | bytes 10594304 | tf_op jit(solution)/shard_map/dot_general | solution.py:89
  97.1 6.0 %fusion.88 = (f32[256]{0:T(256)S(1)}, f32[256,8192]{0,1:T(8,128)S(1)}) fusion(bf16[256,512]{1,0:T(8,128)(2,1)S(1)} %copy-done.7, bf16[8192,512]{1,0:T(8,128)(2,1)} %bitcast.82, s32[256]{0:T(256)S(1)} %iota_add_fusion, s32[8192]{0:T(1024)S(1)} %fusion.80, pred[8192]{0:T(1024)(128)(4,1)S(1)} %broadcast_compare_fusion), kind=kOutput, calls=%fused_computation.106 | convolution fusion | flops 547356416 | bytes 10594304 | tf_op jit(solution)/shard_map/dot_general | solution.py:89
  103.1 11.3 %fusion.8 = (f32[256]{0:T(256)S(1)}, f32[256]{0:T(256)S(1)}, f32[256]{0:T(256)S(1)}, f32[256]{0:T(256)S(1)}, bf16[256,8192]{0,1:T(8,128)(2,1)}, /*index=5*/bf16[...) fusion(f32[256,8192]{0,1:T(8,128)S(1)} %get-tuple-element.35, f32[256]{0:T(256)S(1)} %get-tuple-element.34, ...), kind=kLoop, calls=%fused_computation.21 | loop fusion | flops 37747712 | bytes 50381824 | tf_op jit(solution)/shard_map/reduce_sum | solution.py:100
  114.3 31.0 %all-gather.7.cloned.1.call-done = bf16[32,256,512]{2,1,0:T(8,128)(2,1)} async-done(((bf16[2,256,512]{2,1,0:T(8,128)(2,1)}), bf16[32,256,512]{2,1,0:T(8,128)(2,1)}) %all-gather.7.cloned.1.call-update) | async-done | bytes 8388624 | tf_op jit(solution)/shard_map/all_gather | solution.py:72
  145.4 4.0 %fusion.36 = bf16[256,128]{0,1:T(8,128)(2,1)S(1)} fusion(bf16[256,8192]{0,1:T(8,128)(2,1)} %get-tuple-element.10, bf16[8192,512]{1,0:T(8,128)(2,1)} %bitcast.85, f32[256]{0:T(256)S(1)} %get-tuple-element.26), kind=kOutput, calls=%fused_computation.48 | convolution fusion | flops 536936448 | bytes 6358016 | tf_op jit(solution)/shard_map/dot_general | solution.py:102
  149.4 4.6 %fusion.42 = bf16[256,128]{0,1:T(8,128)(2,1)S(1)} fusion(bf16[256,8192]{0,1:T(8,128)(2,1)} %get-tuple-element.12, bf16[8192,512]{1,0:T(8,128)(2,1)} %bitcast.86, f32[256]{0:T(256)S(1)} %get-tuple-element.27), kind=kOutput, calls=%fused_computation.50 | convolution fusion | flops 536936448 | bytes 6358016 | tf_op jit(solution)/shard_map/dot_general | solution.py:102
  154.1 1.0 fusion.48
  155.1 0.1 copy-done.2
  155.2 1.0 fusion.54
  156.2 0.8 copy.37
  (34 shorter events, 0.7 us)
Async XLA Ops:
  7.2 18.1 %copy-start = (bf16[32,128]{1,0:T(8,128)(2,1)S(1)}, bf16[32,128]{1,0:T(8,128)(2,1)}, u32[]{:S(2)}) copy-start(bf16[32,128]{1,0:T(8,128)(2,1)} %param.9) | copy-start | bytes 24580
  7.2 78.7 %all-gather.5.cloned.1.call-start = ((), (), s32[]{:S(2)}) async-start(), calls=%async_computation | async-start | bytes 8912896 | tf_op jit(solution)/shard_map/all_gather | solution.py:72
  7.2 7.7 %collective-permute-start.1 = (bf16[256,512]{1,0:T(8,128)(2,1)}, bf16[256,512]{1,0:T(8,128)(2,1)S(1)}, u32[]{:S(2)}, u32[]{:S(2)}) collective-permute-start(bf16[256,512]{1,0:T(8,128)(2,1)} %param.11), channel_id=1, source_target_pairs={{0,64},{64,128},{128,192},{192,256},{256,320},{320,384},{384,448},... | collective-permute-start | bytes 786440 | tf_op jit(solution)/shard_map/ppermute | solution.py:69
  14.9 15.3 %copy-start.4 = (bf16[256,512]{1,0:T(8,128)(2,1)S(1)}, bf16[256,512]{1,0:T(8,128)(2,1)}, u32[]{:S(2)}) copy-start(bf16[256,512]{1,0:T(8,128)(2,1)} %param.6) | copy-start | bytes 786436
  16.7 128.6 %all-gather.7.cloned.1.call-start = ((), (), s32[]{:S(2)}) async-start(), calls=%async_computation.1 | async-start | bytes 8912896 | tf_op jit(solution)/shard_map/all_gather | solution.py:72
  17.9 12.4 %collective-permute-start = (bf16[127,512]{1,0:T(8,128)(2,1)S(1)}, bf16[127,512]{1,0:T(8,128)(2,1)S(1)}, u32[]{:S(2)}, u32[]{:S(2)}) collective-permute-start(bf16[127,512]{1,0:T(8,128)(2,1)S(1)} %slice.60), channel_id=1, source_target_pairs={{0,4},{4,8},{8,12},{12,16},{16,20},{20,24},{24,28},{28,32},{32,36}... | collective-permute-start | bytes 390152 | tf_op jit(solution)/shard_map/ppermute | solution.py:21
  27.3 58.5 %copy-start.7 = (bf16[256,512]{1,0:T(8,128)(2,1)S(1)}, bf16[256,512]{1,0:T(8,128)(2,1)}, u32[]{:S(2)}) copy-start(bf16[256,512]{1,0:T(8,128)(2,1)} %param.10) | copy-start | bytes 786436
  31.6 7.5 %collective-permute-start.2 = (bf16[256,512]{0,1:T(8,128)(2,1)S(1)}, bf16[256,512]{0,1:T(8,128)(2,1)S(1)}, u32[]{:S(2)}, u32[]{:S(2)}) collective-permute-start(bf16[256,512]{0,1:T(8,128)(2,1)S(1)} %fusion.60), channel_id=1, source_target_pairs={{0,64},{64,128},{128,192},{192,256},{256,320},{320,384},{384,448},... | collective-permute-start | bytes 786440 | tf_op jit(solution)/shard_map/ppermute | solution.py:69
  85.9 6.5 %copy-start.5 = (bf16[32,256,512]{2,1,0:T(8,128)(2,1)S(1)}, bf16[32,256,512]{2,1,0:T(8,128)(2,1)}, u32[]{:S(2)}) copy-start(bf16[32,256,512]{2,1,0:T(8,128)(2,1)} %all-gather.5.cloned.1.call-done) | copy-start | bytes 25165828
  145.4 8.7 %copy-start.3 = (bf16[256,8192]{0,1:T(8,128)(2,1)S(1)}, bf16[256,8192]{0,1:T(8,128)(2,1)}, u32[]{:S(2)}) copy-start(bf16[256,8192]{0,1:T(8,128)(2,1)} %get-tuple-element.14) | copy-start | bytes 12582916
  145.4 8.7 %copy-start.6 = (bf16[32,256,512]{2,1,0:T(8,128)(2,1)S(1)}, bf16[32,256,512]{2,1,0:T(8,128)(2,1)}, u32[]{:S(2)}) copy-start(bf16[32,256,512]{2,1,0:T(8,128)(2,1)} %all-gather.7.cloned.1.call-done) | copy-start | bytes 25165828
  149.4 5.8 %copy-start.2 = (bf16[256,8192]{0,1:T(8,128)(2,1)S(1)}, bf16[256,8192]{0,1:T(8,128)(2,1)}, u32[]{:S(2)}) copy-start(bf16[256,8192]{0,1:T(8,128)(2,1)} %get-tuple-element.16) | copy-start | bytes 12582916
  154.0 3.0 %copy-start.1 = (bf16[32,128]{1,0:T(8,128)(2,1)S(1)}, bf16[32,128]{1,0:T(8,128)(2,1)}, u32[]{:S(2)}) copy-start(bf16[32,128]{1,0:T(8,128)(2,1)} %param.9) | copy-start | bytes 24580
Sparse Core Ops, SparseCore 0:
  16.9 68.9 all-gather.4
  88.0 57.3 all-gather.6

commit v3 on v2

--- a/solution.py
+++ b/solution.py
@@ -71,8 +71,9 @@
     def row_gather(array):
         return lax.all_gather(jnp.stack([array, row_down(array)]), ("col", "core"), axis=0)
 
-    keys_all = row_gather(key_rows)
-    values_all = row_gather(mixed)
+    both_all = row_gather(jnp.concatenate([key_rows, mixed], axis=1))
+    keys_all = both_all[..., :channels]
+    values_all = both_all[..., channels:]
     gathered_rows = keys_all.shape[0] * keys_all.shape[1] * row_count
     keys_all = keys_all.reshape(gathered_rows, channels)
     values_all = values_all.reshape(gathered_rows, channels)

time: 164 us -> 198 us (1.21)
  waiting for transfers between devices: 82.7 us -> 114 us
  local copies, waits for them, and re-layouts: 4.41 us -> 14.1 us
  starting transfers between devices: 15.4 us -> 8.84 us
    all_gather x2 -> x1, waiting for transfers between devices: 75.7 us -> 105 us  [row_gather(): lax.all_gather(jnp.stack([array, row_down(array)]), ('col', 'core'), axis=0)]
    slice x0 -> x1, local copies, waits for them, and re-layouts: none -> 6.7 us  [body(): values_all = both_all[..., channels:]]
    ppermute x2 -> x1, starting transfers between devices: 8.24 us -> 3.41 us  [row_down(): return lax.ppermute(array, 'row', [(r, r + 1) for r in range(rows - 1)])]
    unnamed x22 -> x17, local copies, waits for them, and re-layouts: 2.6 us -> 5.32 us
    ppermute x2 -> x1, waiting for transfers between devices: 6.92 us -> 9.28 us  [row_down(): return lax.ppermute(array, 'row', [(r, r + 1) for r in range(rows - 1)])]
    dot_general x4, matrix products: 10.6 us -> 8.59 us  [body(): jnp.dot(weights, values_all[:, lanes], preferred_element_type=jnp.float32)]
  transfers between devices with their start and end apart: 5 -> 3, of which waited for: 4 -> 2; matrix products, arithmetic and copies ran while one was open for 23% -> 4% of each run, Pallas kernels for 0% -> 0%
where the time goes in v3:
time: 198 us
  waiting for transfers between devices  114 us (58%)
  matrix products  32.5 us (16%)
  between operations  14.3 us (7%)
  local copies, waits for them, and re-layouts  14.1 us (7%)
  other arithmetic  13.4 us (7%)
  starting transfers between devices  8.84 us (4%)
    all_gather x1, waiting for transfers between devices, row_gather(): lax.all_gather(jnp.stack([array, row_down(array)]), ('col', 'core'), axis=0)  105 us
    dot_general x4, matrix products, body(): lax.dot_general(query_rows[:, lanes], keys_all[:, lanes], (((1,), (1,)),...  19.1 us
    reduce_sum x1, other arithmetic, body(): row_total = jnp.sum(exp_terms, axis=1, keepdims=True)  12 us
    ppermute x1, waiting for transfers between devices, row_down(): return lax.ppermute(array, 'row', [(r, r + 1) for r in range(rows - 1)])  9.28 us
    dot_general x4, matrix products, body(): jnp.dot(weights, values_all[:, lanes], preferred_element_type=jnp.float32)  8.59 us
    slice x1, local copies, waits for them, and re-layouts, body(): values_all = both_all[..., channels:]  6.7 us
    ppermute x1, starting transfers between devices, passed_along(): return lax.ppermute(block, axis, route)  5.39 us
    unnamed x17, local copies, waits for them, and re-layouts  5.32 us
  transfers between devices with their start and end apart: 3, of which 2 were waited for; matrix products, arithmetic and copies ran while one was open for 4% of the time, Pallas kernels for 0%

profile of v3, /device:TPU:1, one launch (start us, length us, event | category | flops | bytes accessed | tf_op | source)
XLA Modules:
  0.0 197.7 jit_solution(4979458042402228716)
XLA Ops:
  7.2 1.1 multiply_convert_fusion
  8.4 5.4 %collective-permute-start = (bf16[127,512]{1,0:T(8,128)(2,1)S(1)}, bf16[127,512]{1,0:T(8,128)(2,1)S(1)}, u32[]{:S(2)}, u32[]{:S(2)}) collective-permute-start(bf16[127,512]{1,0:T(8,128)(2,1)S(1)} %slice.68), channel_id=1, source_target_pairs={{0,4},{4,8},{8,12},{12,16},{16,20},{20,24},{24,28},{28,32},{32,36}... | collective-permute-start | bytes 390152 | tf_op jit(solution)/shard_map/ppermute | solution.py:21
  13.8 0.1 copy.33
  14.0 0.1 copy.36
  14.2 1.1 copy.32
  15.3 1.1 copy.38
  16.4 1.8 fusion.30
  18.1 0.2 copy.45
  18.4 0.6 fusion.58
  19.0 1.8 fusion.31
  20.8 0.2 copy.46
  21.1 0.1 copy.44
  21.2 0.1 concatenate.12.clone
  21.3 0.6 fusion.32
  22.0 0.3 copy.37
  22.4 3.4 %collective-permute-start.1 = (bf16[256,1024]{0,1:T(8,128)(2,1)S(1)}, bf16[256,1024]{0,1:T(8,128)(2,1)S(1)}, u32[]{:S(2)}, u32[]{:S(2)}) collective-permute-start(bf16[256,1024]{0,1:T(8,128)(2,1)S(1)} %get-tuple-element.37), channel_id=1, source_target_pairs={{0,64},{64,128},{128,192},{192,256},{256,320},{320,384},{384,448},... | collective-permute-start | bytes 1572872 | tf_op jit(solution)/shard_map/ppermute | solution.py:69
  25.9 9.3 %collective-permute-done.1 = bf16[256,1024]{0,1:T(8,128)(2,1)S(1)} collective-permute-done((bf16[256,1024]{0,1:T(8,128)(2,1)S(1)}, bf16[256,1024]{0,1:T(8,128)(2,1)S(1)}, u32[]{:S(2)}, u32[]{:S(2)}) %collective-permute-start.1) | collective-permute-done | bytes 524320 | tf_op jit(solution)/shard_map/ppermute | solution.py:69
  35.2 1.3 copy.39
  36.7 0.8 copy.40
  37.5 105.2 %all-gather.3.cloned.1.call-done = bf16[32,256,1024]{2,1,0:T(8,128)(2,1)} async-done(((bf16[2,256,1024]{2,1,0:T(8,128)(2,1)}), bf16[32,256,1024]{2,1,0:T(8,128)(2,1)}) %all-gather.3.cloned.1.call-update) | async-done | bytes 16777232 | tf_op jit(solution)/shard_map/all_gather | solution.py:72
  142.7 6.7 %fusion.86 = (bf16[16,2,256,512]{3,2,1,0:T(8,128)(2,1)S(1)}, bf16[16,2,256,512]{3,2,1,0:T(8,128)(2,1)S(1)}) fusion(bf16[16,2,256,1024]{3,2,1,0:T(8,128)(2,1)} %bitcast.72), kind=kLoop, calls=%fused_computation.104 | loop fusion | bytes 33554432 | tf_op jit(solution)/shard_map/slice | solution.py:76
  149.4 2.4 %fusion.90 = (f32[256]{0:T(256)S(1)}, f32[256,8192]{0,1:T(8,128)S(1)}) fusion(bf16[256,512]{1,0:T(8,128)(2,1)S(1)} %copy-done.4, bf16[8192,512]{1,0:T(8,128)(2,1)S(1)} %bitcast.77, s32[256]{0:T(256)S(1)} %iota_add_fusion, s32[8192]{0:T(1024)S(1)} %fusion.80, pred[8192]{0:T(1024)(128)(4,1)S(1)} %broadcast_compare_fusion), kind=kOutput, calls=%fused_computation.108 | convolution fusion | flops 547356416 | bytes 10594304 | tf_op jit(solution)/shard_map/dot_general | solution.py:90
  151.8 0.8 copy-done.2
  152.6 2.4 %fusion.89 = (f32[256]{0:T(256)S(1)}, f32[256,8192]{0,1:T(8,128)S(1)}) fusion(bf16[256,512]{1,0:T(8,128)(2,1)S(1)} %copy-done.4, bf16[8192,512]{1,0:T(8,128)(2,1)S(1)} %bitcast.78, s32[256]{0:T(256)S(1)} %iota_add_fusion, s32[8192]{0:T(1024)S(1)} %fusion.80, pred[8192]{0:T(1024)(128)(4,1)S(1)} %broadcast_compare_fusion), kind=kOutput, calls=%fused_computation.107 | convolution fusion | flops 547356416 | bytes 10594304 | tf_op jit(solution)/shard_map/dot_general | solution.py:90
  155.0 6.0 %fusion.88 = (f32[256]{0:T(256)S(1)}, f32[256,8192]{0,1:T(8,128)S(1)}) fusion(bf16[256,512]{1,0:T(8,128)(2,1)S(1)} %copy-done.4, bf16[8192,512]{1,0:T(8,128)(2,1)} %bitcast.79, s32[256]{0:T(256)S(1)} %iota_add_fusion, s32[8192]{0:T(1024)S(1)} %fusion.80, pred[8192]{0:T(1024)(128)(4,1)S(1)} %broadcast_compare_fusion), kind=kOutput, calls=%fused_computation.106 | convolution fusion | flops 547356416 | bytes 10594304 | tf_op jit(solution)/shard_map/dot_general | solution.py:90
  161.0 8.3 %fusion.87 = (f32[256]{0:T(256)S(1)}, f32[256,8192]{0,1:T(8,128)}) fusion(bf16[256,512]{1,0:T(8,128)(2,1)S(1)} %copy-done.4, bf16[8192,512]{1,0:T(8,128)(2,1)} %bitcast.80, s32[256]{0:T(256)S(1)} %iota_add_fusion, s32[8192]{0:T(1024)S(1)} %fusion.80, pred[8192]{0:T(1024)(128)(4,1)S(1)} %broadcast_compare_fusion), kind=kOutput, calls=%fused_computation.105 | convolution fusion | flops 547356416 | bytes 10594304 | tf_op jit(solution)/shard_map/dot_general | solution.py:90
  169.3 12.0 %fusion.8 = (f32[256]{0:T(256)S(1)}, f32[256]{0:T(256)S(1)}, f32[256]{0:T(256)S(1)}, f32[256]{0:T(256)S(1)}, bf16[256,8192]{0,1:T(8,128)(2,1)}, /*index=5*/bf16[...) fusion(f32[256,8192]{0,1:T(8,128)} %get-tuple-element.39, f32[256]{0:T(256)S(1)} %get-tuple-element.38, ...), kind=kLoop, calls=%fused_computation.21 | loop fusion | flops 37747712 | bytes 50381824 | tf_op jit(solution)/shard_map/reduce_sum | solution.py:101
  181.3 3.3 %fusion.42 = bf16[256,128]{0,1:T(8,128)(2,1)S(1)} fusion(bf16[256,8192]{0,1:T(8,128)(2,1)} %get-tuple-element.12, bf16[8192,512]{1,0:T(8,128)(2,1)S(1)} %bitcast.73, f32[256]{0:T(256)S(1)} %get-tuple-element.27), kind=kOutput, calls=%fused_computation.50 | convolution fusion | flops 536936448 | bytes 6358016 | tf_op jit(solution)/shard_map/dot_general | solution.py:103
  184.7 3.2 %fusion.36 = bf16[256,128]{0,1:T(8,128)(2,1)S(1)} fusion(bf16[256,8192]{0,1:T(8,128)(2,1)} %get-tuple-element.10, bf16[8192,512]{1,0:T(8,128)(2,1)S(1)} %bitcast.74, f32[256]{0:T(256)S(1)} %get-tuple-element.26), kind=kOutput, calls=%fused_computation.48 | convolution fusion | flops 536936448 | bytes 6358016 | tf_op jit(solution)/shard_map/dot_general | solution.py:103
  187.9 1.0 fusion.48
  188.9 1.0 fusion.54
  190.0 0.8 copy.41
  (25 shorter events, 0.5 us)
Async XLA Ops:
  7.2 9.2 %copy-start = (bf16[32,128]{1,0:T(8,128)(2,1)S(1)}, bf16[32,128]{1,0:T(8,128)(2,1)}, u32[]{:S(2)}) copy-start(bf16[32,128]{1,0:T(8,128)(2,1)} %param.9) | copy-start | bytes 24580
  7.2 135.5 %all-gather.3.cloned.1.call-start = ((), (), s32[]{:S(2)}) async-start(), calls=%async_computation | async-start | bytes 17825792 | tf_op jit(solution)/shard_map/all_gather | solution.py:72
  8.4 12.7 %collective-permute-start = (bf16[127,512]{1,0:T(8,128)(2,1)S(1)}, bf16[127,512]{1,0:T(8,128)(2,1)S(1)}, u32[]{:S(2)}, u32[]{:S(2)}) collective-permute-start(bf16[127,512]{1,0:T(8,128)(2,1)S(1)} %slice.68), channel_id=1, source_target_pairs={{0,4},{4,8},{8,12},{12,16},{16,20},{20,24},{24,28},{28,32},{32,36}... | collective-permute-start | bytes 390152 | tf_op jit(solution)/shard_map/ppermute | solution.py:21
  22.4 12.7 %collective-permute-start.1 = (bf16[256,1024]{0,1:T(8,128)(2,1)S(1)}, bf16[256,1024]{0,1:T(8,128)(2,1)S(1)}, u32[]{:S(2)}, u32[]{:S(2)}) collective-permute-start(bf16[256,1024]{0,1:T(8,128)(2,1)S(1)} %get-tuple-element.37), channel_id=1, source_target_pairs={{0,64},{64,128},{128,192},{192,256},{256,320},{320,384},{384,448},... | collective-permute-start | bytes 1572872 | tf_op jit(solution)/shard_map/ppermute | solution.py:69
  142.7 6.7 %copy-start.4 = (bf16[256,512]{1,0:T(8,128)(2,1)S(1)}, bf16[256,512]{1,0:T(8,128)(2,1)}, u32[]{:S(2)}) copy-start(bf16[256,512]{1,0:T(8,128)(2,1)} %param.10) | copy-start | bytes 786436
  149.4 3.2 %copy-start.2 = (bf16[16,2,256,512]{3,2,1,0:T(8,128)(2,1)}, bf16[16,2,256,512]{3,2,1,0:T(8,128)(2,1)S(1)}, u32[]{:S(2)}) copy-start(bf16[16,2,256,512]{3,2,1,0:T(8,128)(2,1)S(1)} %get-tuple-element.31) | copy-start | bytes 25165828
  181.3 6.6 %copy-start.3 = (bf16[256,8192]{0,1:T(8,128)(2,1)S(1)}, bf16[256,8192]{0,1:T(8,128)(2,1)}, u32[]{:S(2)}) copy-start(bf16[256,8192]{0,1:T(8,128)(2,1)} %get-tuple-element.14) | copy-start | bytes 12582916
  187.9 3.0 %copy-start.1 = (bf16[32,128]{1,0:T(8,128)(2,1)S(1)}, bf16[32,128]{1,0:T(8,128)(2,1)}, u32[]{:S(2)}) copy-start(bf16[32,128]{1,0:T(8,128)(2,1)} %param.9) | copy-start | bytes 24580
Sparse Core Ops, SparseCore 0:
  36.7 105.9 all-gather.2

commit v4 on v2

--- a/solution.py
+++ b/solution.py
@@ -65,30 +65,29 @@
     query_pos = shard_index * row_count + jnp.arange(row_count, dtype=jnp.int32)
     seq_start = jnp.maximum(shard_index - seq_place, 0) * row_count
 
-    def row_down(array):
-        return lax.ppermute(array, "row", [(r, r + 1) for r in range(rows - 1)])
+    def row_gather(array):
+        gathered = lax.all_gather(array, ("col", "core"), axis=0)
+        return gathered.reshape(half * row_count, channels)
 
-    def row_gather(array):
-        return lax.all_gather(jnp.stack([array, row_down(array)]), ("col", "core"), axis=0)
+    row_up = [(r + 1, r) for r in range(rows - 1)]
+    row_down = [(r, r + 1) for r in range(rows - 1)]
+    queries_below = lax.ppermute(query_rows, "row", row_up)
+    keys_row = row_gather(key_rows)
+    values_row = row_gather(mixed)
+    key_pos = row_index * half * row_count + jnp.arange(half * row_count, dtype=jnp.int32)
+    shard_below = shard_index + half
+    place_below = (shard_below + half) % seq_span
+    start_below = jnp.maximum(shard_below - place_below, 0) * row_count
+    pos_below = shard_below * row_count + jnp.arange(row_count, dtype=jnp.int32)
+    visible_own = (key_pos[None, :] >= seq_start) & (key_pos[None, :] <= query_pos[:, None])
+    visible_below = (key_pos[None, :] >= start_below) & (key_pos[None, :] <= pos_below[:, None])
 
-    keys_all = row_gather(key_rows)
-    values_all = row_gather(mixed)
-    gathered_rows = keys_all.shape[0] * keys_all.shape[1] * row_count
-    keys_all = keys_all.reshape(gathered_rows, channels)
-    values_all = values_all.reshape(gathered_rows, channels)
-    key_index = jnp.arange(gathered_rows, dtype=jnp.int32)
-    key_shard = key_index // (2 * row_count)
-    key_source = (key_index // row_count) % 2
-    key_pos = ((row_index - key_source) * half + key_shard) * row_count + key_index % row_count
-    visible = (key_pos[None, :] >= seq_start) & (key_pos[None, :] <= query_pos[:, None])
-
-    head_outputs = []
-    for head in range(local_heads):
+    def softmax_part(queries, visible, head):
         lanes = slice(head * HEAD_DIM, (head + 1) * HEAD_DIM)
         scores = (
             lax.dot_general(
-                query_rows[:, lanes],
-                keys_all[:, lanes],
+                queries[:, lanes],
+                keys_row[:, lanes],
                 (((1,), (1,)), ((), ())),
                 preferred_element_type=jnp.float32,
             )
@@ -98,9 +97,36 @@
         row_peak = jnp.max(scores, axis=1, keepdims=True)
         exp_terms = jnp.where(visible, jnp.exp(scores - row_peak), 0.0)
         row_total = jnp.sum(exp_terms, axis=1, keepdims=True)
-        weights, row_total = lax.optimization_barrier((exp_terms.astype(jnp.bfloat16), row_total))
-        weighted = jnp.dot(weights, values_all[:, lanes], preferred_element_type=jnp.float32)
-        head_outputs.append((weighted / row_total).astype(jnp.bfloat16))
+        return lax.optimization_barrier((exp_terms.astype(jnp.bfloat16), row_peak, row_total))
+
+    def weighted_part(weights, head):
+        lanes = slice(head * HEAD_DIM, (head + 1) * HEAD_DIM)
+        return jnp.dot(weights, values_row[:, lanes], preferred_element_type=jnp.float32)
+
+    below_parts = [softmax_part(queries_below, visible_below, head) for head in range(local_heads)]
+    own_parts = [softmax_part(query_rows, visible_own, head) for head in range(local_heads)]
+    below_sums = jnp.concatenate(
+        [weighted_part(weights, head) for head, (weights, _, _) in enumerate(below_parts)], axis=1
+    )
+    below_stats = jnp.concatenate(
+        [jnp.concatenate([peak, total], axis=1) for _, peak, total in below_parts], axis=1
+    )
+    above_sums, above_stats = lax.ppermute((below_sums, below_stats), "row", row_down)
+
+    head_outputs = []
+    for head, (weights, own_peak, own_total) in enumerate(own_parts):
+        own_sum = weighted_part(weights, head)
+        lanes = slice(head * HEAD_DIM, (head + 1) * HEAD_DIM)
+        above_total = above_stats[:, 2 * head + 1 : 2 * head + 2]
+        above_peak = jnp.where(
+            above_total > 0, above_stats[:, 2 * head : 2 * head + 1], NEGATIVE
+        )
+        row_peak = jnp.maximum(own_peak, above_peak)
+        own_scale = jnp.exp(own_peak - row_peak)
+        above_scale = jnp.exp(above_peak - row_peak)
+        total = own_total * own_scale + above_total * above_scale
+        weighted = own_sum * own_scale + above_sums[:, lanes] * above_scale
+        head_outputs.append((weighted / total).astype(jnp.bfloat16))
     attended = jnp.concatenate(head_outputs, axis=1)
     return (mixed, attended)
 

time: 164 us -> 154 us (0.939); the launches traced: 164 us -> 152 us
  waiting for transfers between devices: 82.7 us -> 64.5 us
  matrix products: 32.6 us -> 41.3 us
  starting transfers between devices: 15.4 us -> 13.7 us
    all_gather x2, waiting for transfers between devices: 75.7 us -> 55.3 us  [row_gather(): gathered = lax.all_gather(array, ('col', 'core'), axis=0)]
    dot_general x8 -> x16, matrix products: 27.8 us -> 36.4 us  [the longest x8 20.7 us: softmax_part(): lax.dot_general(queries[:, lanes], keys_row[:, lanes], (((1,), (1,)), (()...]
    another operation x2 -> x0, other arithmetic: 1.88 us -> none  [row_gather(): jnp.stack([array, row_down(array)])]
    ppermute x1, starting transfers between devices: 7.09 us -> 5.39 us  [passed_along(): return lax.ppermute(block, axis, route)]
    ppermute x2 -> x3, waiting for transfers between devices: 6.92 us -> 8.55 us  [the longest x2 4.81 us: body(): lax.ppermute((below_sums, below_stats), 'row', row_down)]
    unnamed x22 -> x28, local copies, waits for them, and re-layouts: 2.6 us -> 3.44 us
    reduce_sum x1 -> x2, other arithmetic: 11.3 us -> 11.8 us  [softmax_part(): row_total = jnp.sum(exp_terms, axis=1, keepdims=True)]
    ppermute x2 -> x3, starting transfers between devices: 8.24 us -> 8.22 us  [the longest x2 6.75 us: body(): lax.ppermute((below_sums, below_stats), 'row', row_down)]
  transfers between devices with their start and end apart: 5 -> 6, of which waited for: 4 -> 4; matrix products, arithmetic and copies ran while one was open for 23% -> 35% of each run, Pallas kernels for 0% -> 0%
where the time goes in v4:
time: 154 us; the launch traced here: 152 us
  waiting for transfers between devices  64.5 us (42%)
  matrix products  41.3 us (27%)
  between operations  14.5 us (9%)
  other arithmetic  13.9 us (9%)
  starting transfers between devices  13.7 us (9%)
  local copies, waits for them, and re-layouts  4.22 us (3%)
    all_gather x2, waiting for transfers between devices, row_gather(): gathered = lax.all_gather(array, ('col', 'core'), axis=0)  55.3 us
    dot_general x8, matrix products, softmax_part(): lax.dot_general(queries[:, lanes], keys_row[:, lanes], (((1,), (1,)), (()...  20.7 us
    dot_general x8, matrix products, weighted_part(): jnp.dot(weights, values_row[:, lanes], preferred_element_type=jnp.float32)  15.7 us
    reduce_sum x2, other arithmetic, softmax_part(): row_total = jnp.sum(exp_terms, axis=1, keepdims=True)  11.8 us
    ppermute x2, starting transfers between devices, body(): lax.ppermute((below_sums, below_stats), 'row', row_down)  6.75 us
    ppermute x1, starting transfers between devices, passed_along(): return lax.ppermute(block, axis, route)  5.39 us
    ppermute x2, waiting for transfers between devices, body(): lax.ppermute((below_sums, below_stats), 'row', row_down)  4.81 us
    ppermute x1, waiting for transfers between devices, body(): queries_below = lax.ppermute(query_rows, 'row', row_up)  3.74 us
  transfers between devices with their start and end apart: 6, of which 4 were waited for; matrix products, arithmetic and copies ran while one was open for 35% of the time, Pallas kernels for 0%

profile of v4, /device:TPU:1, one launch (start us, length us, event | category | flops | bytes accessed | tf_op | source)
XLA Modules:
  0.0 152.1 jit_solution(13904909338544465571)
XLA Ops:
  8.0 1.1 multiply_convert_fusion
  9.1 5.4 %collective-permute-start = (bf16[127,512]{1,0:T(8,128)(2,1)S(1)}, bf16[127,512]{1,0:T(8,128)(2,1)S(1)}, u32[]{:S(2)}, u32[]{:S(2)}) collective-permute-start(bf16[127,512]{1,0:T(8,128)(2,1)S(1)} %slice.132), channel_id=1, source_target_pairs={{0,4},{4,8},{8,12},{12,16},{16,20},{20,24},{24,28},{28,32},{32,36}... | collective-permute-start | bytes 390152 | tf_op jit(solution)/shard_map/ppermute | solution.py:21
  14.7 1.8 %fusion.26 = bf16[4,8,128,128]{3,1,2,0:T(8,128)(2,1)S(1)} fusion(bf16[32,128]{1,0:T(8,128)(2,1)S(1)} %copy-done, s32[16384]{0:T(1024)S(1)} %subtract_bitcast_fusion), kind=kOutput, calls=%fused_computation.48 | convolution fusion | flops 136839168 | bytes 1122304 | tf_op jit(solution)/shard_map/dot_general | solution.py:30
  17.5 1.8 %fusion.27 = bf16[4,8,128,128]{3,1,2,0:T(8,128)(2,1)S(1)} fusion(bf16[32,128]{1,0:T(8,128)(2,1)S(1)} %copy-done, s32[16384]{0:T(1024)S(1)} %broadcast_add_fusion), kind=kOutput, calls=%fused_computation.49 | convolution fusion | flops 136839168 | bytes 1122304 | tf_op jit(solution)/shard_map/dot_general | solution.py:30
  21.0 0.8 fusion.52
  21.8 1.5 collective-permute-start.1
  23.4 1.8 %copy.18 = bf16[256,512]{1,0:T(8,128)(2,1)} copy(bf16[256,512]{0,1:T(8,128)(2,1)} %fusion.52) | data formatting | bytes 524288
  25.2 3.7 %collective-permute-done.1 = bf16[256,512]{1,0:T(8,128)(2,1)S(1)} collective-permute-done((bf16[256,512]{1,0:T(8,128)(2,1)S(1)}, bf16[256,512]{1,0:T(8,128)(2,1)S(1)}, u32[]{:S(2)}, u32[]{:S(2)}) %collective-permute-start.1) | collective-permute-done | bytes 262176 | tf_op jit(solution)/shard_map/ppermute | solution.py:74
  28.9 32.8 %all-gather.5.cloned.1.call-done = bf16[4096,512]{1,0:T(8,128)(2,1)} async-done(((bf16[256,512]{1,0:T(8,128)(2,1)}), bf16[4096,512]{1,0:T(8,128)(2,1)}) %all-gather.5.cloned.1.call-update) | async-done | bytes 4194320 | tf_op jit(solution)/shard_map/all_gather | solution.py:69
  61.8 2.7 %fusion.104 = (f32[256]{0:T(256)S(1)}, f32[256,4096]{1,0:T(8,128)S(1)}) fusion(bf16[4096,512]{1,0:T(8,128)(2,1)} %all-gather.5.cloned.1.call-done, bf16[256,512]{1,0:T(8,128)(2,1)S(1)} %collective-permute-done.1, s32[256]{0:T(256)S(1)} %iota_add_fusion.1, s32[4096]{0:T(1024)S(1)} %iota_add_fusion, pred[4096]{0:T(1024)(128)(4,1)S(1)} %fusion.85), kind=kOutput, calls=%fused_computation.145 | convolution fusion | flops 273678080 | bytes 5330944 | tf_op jit(solution)/shard_map/dot_general | solution.py:88
  64.4 1.3 fusion.105
  65.8 1.3 fusion.106
  67.1 1.3 fusion.107
  68.4 5.7 %fusion.12 = (f32[256]{0:T(256)S(1)}, f32[256]{0:T(256)S(1)}, f32[256]{0:T(256)S(1)}, f32[256]{0:T(256)S(1)}, bf16[256,4096]{1,0:T(8,128)(2,1)S(1)}, /*index=5*/...) fusion(f32[256,4096]{1,0:T(8,128)S(1)} %get-tuple-element.92, f32[256]{0:T(256)S(1)} %get-tuple-element.91, ...), kind=kLoop, calls=%fused_computation.34 | loop fusion | flops 18873344 | bytes 25195520 | tf_op jit(solution)/shard_map/reduce_sum | solution.py:99
  74.2 3.6 %collective-permute-start.2 = (f32[256,8]{0,1:T(8,128)S(1)}, f32[256,8]{0,1:T(8,128)S(1)}, u32[]{:S(2)}, u32[]{:S(2)}) collective-permute-start(f32[256,8]{0,1:T(8,128)S(1)} %concatenate.17), channel_id=1, source_target_pairs={{0,64},{64,128},{128,192},{192,256},{256,320},{320,384},{384,448},... | collective-permute-start | bytes 24584 | tf_op jit(solution)/shard_map/ppermute | solution.py:114
  77.8 4.4 %fusion.108 = (f32[256]{0:T(256)S(1)}, f32[256,4096]{1,0:T(8,128)}) fusion(bf16[4096,512]{1,0:T(8,128)(2,1)} %all-gather.5.cloned.1.call-done, bf16[256,512]{1,0:T(8,128)(2,1)S(1)} %copy-done.10, s32[256]{0:T(256)S(1)} %iota_add_fusion.2, s32[4096]{0:T(1024)S(1)} %iota_add_fusion, pred[4096]{0:T(1024)(128)(4,1)S(1)} %fusion.86), kind=kOutput, calls=%fused_computation.149 | convolution fusion | flops 273678080 | bytes 5330944 | tf_op jit(solution)/shard_map/dot_general | solution.py:88
  82.2 3.2 %fusion.109 = (f32[256]{0:T(256)S(1)}, f32[256,4096]{1,0:T(8,128)}) fusion(bf16[4096,512]{1,0:T(8,128)(2,1)S(1)} %copy-done.8, bf16[256,512]{1,0:T(8,128)(2,1)S(1)} %copy-done.10, s32[256]{0:T(256)S(1)} %iota_add_fusion.2, s32[4096]{0:T(1024)S(1)} %iota_add_fusion, pred[4096]{0:T(1024)(128)(4,1)S(1)} %fusion.86), kind=kOutput, calls=%fused_computation.150 | convolution fusion | flops 273678080 | bytes 5330944 | tf_op jit(solution)/shard_map/dot_general | solution.py:88
  85.5 3.2 %fusion.110 = (f32[256]{0:T(256)S(1)}, f32[256,4096]{1,0:T(8,128)}) fusion(bf16[4096,512]{1,0:T(8,128)(2,1)S(1)} %copy-done.8, bf16[256,512]{1,0:T(8,128)(2,1)S(1)} %copy-done.10, s32[256]{0:T(256)S(1)} %iota_add_fusion.2, s32[4096]{0:T(1024)S(1)} %iota_add_fusion, pred[4096]{0:T(1024)(128)(4,1)S(1)} %fusion.86), kind=kOutput, calls=%fused_computation.151 | convolution fusion | flops 273678080 | bytes 5330944 | tf_op jit(solution)/shard_map/dot_general | solution.py:88
  88.6 3.2 %fusion.111 = (f32[256]{0:T(256)S(1)}, f32[256,4096]{1,0:T(8,128)}) fusion(bf16[4096,512]{1,0:T(8,128)(2,1)S(1)} %copy-done.8, bf16[256,512]{1,0:T(8,128)(2,1)S(1)} %copy-done.10, s32[256]{0:T(256)S(1)} %iota_add_fusion.2, s32[4096]{0:T(1024)S(1)} %iota_add_fusion, pred[4096]{0:T(1024)(128)(4,1)S(1)} %fusion.86), kind=kOutput, calls=%fused_computation.152 | convolution fusion | flops 273678080 | bytes 5330944 | tf_op jit(solution)/shard_map/dot_general | solution.py:88
  91.8 22.5 %all-gather.7.cloned.1.call-done = bf16[4096,512]{0,1:T(8,128)(2,1)} async-done(((bf16[256,512]{0,1:T(8,128)(2,1)}), bf16[4096,512]{0,1:T(8,128)(2,1)}) %all-gather.7.cloned.1.call-update) | async-done | bytes 4194320 | tf_op jit(solution)/shard_map/all_gather | solution.py:69
  114.3 2.8 %fusion.33 = f32[256,128]{0,1:T(8,128)S(1)} fusion(bf16[256,4096]{1,0:T(8,128)(2,1)} %get-tuple-element.39, bf16[4096,512]{0,1:T(8,128)(2,1)} %all-gather.7.cloned.1.call-done), kind=kOutput, calls=%fused_computation.60 | convolution fusion | flops 268435456 | bytes 3276800 | tf_op jit(solution)/shard_map/dot_general | solution.py:104
  117.2 2.8 %fusion.36 = f32[256,128]{0,1:T(8,128)S(1)} fusion(bf16[256,4096]{1,0:T(8,128)(2,1)} %get-tuple-element.38, bf16[4096,512]{0,1:T(8,128)(2,1)} %all-gather.7.cloned.1.call-done), kind=kOutput, calls=%fused_computation.63 | convolution fusion | flops 268435456 | bytes 3276800 | tf_op jit(solution)/shard_map/dot_general | solution.py:104
  120.0 2.2 %fusion.39 = f32[256,128]{0,1:T(8,128)S(1)} fusion(bf16[256,4096]{1,0:T(8,128)(2,1)S(1)} %copy-done.5, bf16[4096,512]{0,1:T(8,128)(2,1)} %all-gather.7.cloned.1.call-done), kind=kOutput, calls=%fused_computation.66 | convolution fusion | flops 268435456 | bytes 3276800 | tf_op jit(solution)/shard_map/dot_general | solution.py:104
  122.2 2.1 %fusion.47 = f32[256,128]{0,1:T(8,128)S(1)} fusion(bf16[256,4096]{1,0:T(8,128)(2,1)S(1)} %get-tuple-element.36, bf16[4096,512]{0,1:T(8,128)(2,1)} %all-gather.7.cloned.1.call-done), kind=kOutput, calls=%fused_computation.74 | convolution fusion | flops 268435456 | bytes 3276800 | tf_op jit(solution)/shard_map/dot_general | solution.py:104
  124.4 3.2 %collective-permute-start.3 = (f32[256,512]{0,1:T(8,128)S(1)}, f32[256,512]{0,1:T(8,128)S(1)}, u32[]{:S(2)}, u32[]{:S(2)}) collective-permute-start(f32[256,512]{0,1:T(8,128)S(1)} %pad_maximum_fusion), channel_id=1, source_target_pairs={{0,64},{64,128},{128,192},{192,256},{256,320},{320,384},{384,448},... | collective-permute-start | bytes 1572872 | tf_op jit(solution)/shard_map/ppermute | solution.py:114
  127.6 6.1 %fusion.10 = (f32[256]{0:T(256)S(1)}, f32[256]{0:T(256)S(1)}, f32[256]{0:T(256)S(1)}, f32[256]{0:T(256)S(1)}, bf16[256,4096]{1,0:T(8,128)(2,1)S(1)}, /*index=5*/...) fusion(f32[256,4096]{1,0:T(8,128)S(1)} %copy-done.2, ...), kind=kLoop, calls=%fused_computation.32 | loop fusion | flops 18873344 | bytes 25195520 | tf_op jit(solution)/shard_map/reduce_sum | solution.py:99
  133.7 4.8 %collective-permute-done.3 = f32[256,512]{0,1:T(8,128)S(1)} collective-permute-done((f32[256,512]{0,1:T(8,128)S(1)}, f32[256,512]{0,1:T(8,128)S(1)}, u32[]{:S(2)}, u32[]{:S(2)}) %collective-permute-start.3) | collective-permute-done | bytes 524320 | tf_op jit(solution)/shard_map/ppermute | solution.py:114
  138.5 2.1 %fusion.68 = bf16[256,128]{0,1:T(8,128)(2,1)S(1)} fusion(f32[256,512]{0,1:T(8,128)S(1)} %collective-permute-done.3, f32[256]{0:T(256)S(1)} %bitcast.104, f32[256]{0:T(256)S(1)} %bitcast.105, f32[256]{0:T(256)S(1)} %bitcast.106, bf16[256,4096]{1,0:T(8,128)(2,1)S(1)} %get-tuple-element.47, bf16[4096,512]{0,1:T(8,128)(2,1)} %all-gather.7.cloned.1.call-done), kind=kOutput, calls=%fused_computation.103 | convolution fusion | flops 268599296 | bytes 3345408 | tf_op jit(solution)/shard_map/dot_general | solution.py:104
  140.6 2.1 %fusion.67 = bf16[256,128]{0,1:T(8,128)(2,1)S(1)} fusion(f32[256,512]{0,1:T(8,128)S(1)} %collective-permute-done.3, f32[256]{0:T(256)S(1)} %bitcast.101, f32[256]{0:T(256)S(1)} %bitcast.102, f32[256]{0:T(256)S(1)} %bitcast.103, bf16[256,4096]{1,0:T(8,128)(2,1)S(1)} %get-tuple-element.44, bf16[4096,512]{0,1:T(8,128)(2,1)} %all-gather.7.cloned.1.call-done), kind=kOutput, calls=%fused_computation.102 | convolution fusion | flops 268599296 | bytes 3345408 | tf_op jit(solution)/shard_map/dot_general | solution.py:104
  142.7 0.8 fusion.66
  143.5 0.8 fusion.65
  144.4 0.8 copy.19
  (53 shorter events, 3.8 us)
Async XLA Ops:
  7.2 7.5 %copy-start = (bf16[32,128]{1,0:T(8,128)(2,1)S(1)}, bf16[32,128]{1,0:T(8,128)(2,1)}, u32[]{:S(2)}) copy-start(bf16[32,128]{1,0:T(8,128)(2,1)} %param.9) | copy-start | bytes 24580
  7.2 54.6 %all-gather.5.cloned.1.call-start = ((), (), s32[]{:S(2)}) async-start(), calls=%async_computation | async-start | bytes 4456448 | tf_op jit(solution)/shard_map/all_gather | solution.py:69
  7.9 106.4 %all-gather.7.cloned.1.call-start = ((), (), s32[]{:S(2)}) async-start(), calls=%async_computation.1 | async-start | bytes 4456448 | tf_op jit(solution)/shard_map/all_gather | solution.py:69
  9.1 10.7 %collective-permute-start = (bf16[127,512]{1,0:T(8,128)(2,1)S(1)}, bf16[127,512]{1,0:T(8,128)(2,1)S(1)}, u32[]{:S(2)}, u32[]{:S(2)}) collective-permute-start(bf16[127,512]{1,0:T(8,128)(2,1)S(1)} %slice.132), channel_id=1, source_target_pairs={{0,4},{4,8},{8,12},{12,16},{16,20},{20,24},{24,28},{28,32},{32,36}... | collective-permute-start | bytes 390152 | tf_op jit(solution)/shard_map/ppermute | solution.py:21
  16.7 2.9 %copy-start.6 = (bf16[256,512]{1,0:T(8,128)(2,1)S(1)}, bf16[256,512]{1,0:T(8,128)(2,1)}, u32[]{:S(2)}) copy-start(bf16[256,512]{1,0:T(8,128)(2,1)} %param.6) | copy-start | bytes 786436
  19.2 2.6 %copy-start.10 = (bf16[256,512]{1,0:T(8,128)(2,1)S(1)}, bf16[256,512]{1,0:T(8,128)(2,1)}, u32[]{:S(2)}) copy-start(bf16[256,512]{1,0:T(8,128)(2,1)} %param.10) | copy-start | bytes 786436
  21.8 7.1 %collective-permute-start.1 = (bf16[256,512]{1,0:T(8,128)(2,1)S(1)}, bf16[256,512]{1,0:T(8,128)(2,1)S(1)}, u32[]{:S(2)}, u32[]{:S(2)}) collective-permute-start(bf16[256,512]{1,0:T(8,128)(2,1)S(1)} %copy-done.10), channel_id=1, source_target_pairs={{64,0},{128,64},{192,128},{256,192},{320,256},{384,320},{448,384},... | collective-permute-start | bytes 786440 | tf_op jit(solution)/shard_map/ppermute | solution.py:74
  61.8 2.7 %copy-start.7 = (bf16[4096,512]{1,0:T(8,128)(2,1)S(1)}, bf16[4096,512]{1,0:T(8,128)(2,1)}, u32[]{:S(2)}) copy-start(bf16[4096,512]{1,0:T(8,128)(2,1)} %all-gather.5.cloned.1.call-done) | copy-start | bytes 12582916
  74.2 8.0 %copy-start.8 = (bf16[4096,512]{1,0:T(8,128)(2,1)S(1)}, bf16[4096,512]{1,0:T(8,128)(2,1)}, u32[]{:S(2)}) copy-start(bf16[4096,512]{1,0:T(8,128)(2,1)} %all-gather.5.cloned.1.call-done) | copy-start | bytes 12582916
  74.2 59.5 %collective-permute-start.2 = (f32[256,8]{0,1:T(8,128)S(1)}, f32[256,8]{0,1:T(8,128)S(1)}, u32[]{:S(2)}, u32[]{:S(2)}) collective-permute-start(f32[256,8]{0,1:T(8,128)S(1)} %concatenate.17), channel_id=1, source_target_pairs={{0,64},{64,128},{128,192},{192,256},{256,320},{320,384},{384,448},... | collective-permute-start | bytes 24584 | tf_op jit(solution)/shard_map/ppermute | solution.py:114
  114.3 5.7 %copy-start.5 = (bf16[256,4096]{1,0:T(8,128)(2,1)S(1)}, bf16[256,4096]{1,0:T(8,128)(2,1)}, u32[]{:S(2)}) copy-start(bf16[256,4096]{1,0:T(8,128)(2,1)} %get-tuple-element.37) | copy-start | bytes 6291460
  114.3 13.2 %copy-start.4 = (f32[256,4096]{1,0:T(8,128)S(1)}, f32[256,4096]{1,0:T(8,128)}, u32[]{:S(2)}) copy-start(f32[256,4096]{1,0:T(8,128)} %get-tuple-element.104) | copy-start | bytes 12582916
  117.2 10.4 %copy-start.3 = (f32[256,4096]{1,0:T(8,128)S(1)}, f32[256,4096]{1,0:T(8,128)}, u32[]{:S(2)}) copy-start(f32[256,4096]{1,0:T(8,128)} %get-tuple-element.102) | copy-start | bytes 12582916
  120.0 7.5 %copy-start.2 = (f32[256,4096]{1,0:T(8,128)S(1)}, f32[256,4096]{1,0:T(8,128)}, u32[]{:S(2)}) copy-start(f32[256,4096]{1,0:T(8,128)} %get-tuple-element.100) | copy-start | bytes 12582916
  124.4 14.2 %collective-permute-start.3 = (f32[256,512]{0,1:T(8,128)S(1)}, f32[256,512]{0,1:T(8,128)S(1)}, u32[]{:S(2)}, u32[]{:S(2)}) collective-permute-start(f32[256,512]{0,1:T(8,128)S(1)} %pad_maximum_fusion), channel_id=1, source_target_pairs={{0,64},{64,128},{128,192},{192,256},{256,320},{320,384},{384,448},... | collective-permute-start | bytes 1572872 | tf_op jit(solution)/shard_map/ppermute | solution.py:114
  133.7 9.0 %copy-start.9 = (bf16[4096,512]{0,1:T(8,128)(2,1)S(1)}, bf16[4096,512]{0,1:T(8,128)(2,1)}, u32[]{:S(2)}) copy-start(bf16[4096,512]{0,1:T(8,128)(2,1)} %all-gather.7.cloned.1.call-done) | copy-start | bytes 12582916
  142.7 2.6 %copy-start.1 = (bf16[32,128]{1,0:T(8,128)(2,1)S(1)}, bf16[32,128]{1,0:T(8,128)(2,1)}, u32[]{:S(2)}) copy-start(bf16[32,128]{1,0:T(8,128)(2,1)} %param.9) | copy-start | bytes 24580
Sparse Core Ops, SparseCore 0:
  10.1 51.5 all-gather.4
  64.4 49.8 all-gather.6

commit v5 on v4

--- a/solution.py
+++ b/solution.py
@@ -111,10 +111,13 @@
     below_stats = jnp.concatenate(
         [jnp.concatenate([peak, total], axis=1) for _, peak, total in below_parts], axis=1
     )
+    below_sums, below_stats, own_weights = lax.optimization_barrier(
+        (below_sums, below_stats, [weights for weights, _, _ in own_parts])
+    )
     above_sums, above_stats = lax.ppermute((below_sums, below_stats), "row", row_down)
 
     head_outputs = []
-    for head, (weights, own_peak, own_total) in enumerate(own_parts):
+    for head, (weights, (_, own_peak, own_total)) in enumerate(zip(own_weights, own_parts)):
         own_sum = weighted_part(weights, head)
         lanes = slice(head * HEAD_DIM, (head + 1) * HEAD_DIM)
         above_total = above_stats[:, 2 * head + 1 : 2 * head + 2]

time: 154 us -> 153 us (level)
  waiting for transfers between devices: 64.5 us -> 74.6 us
  matrix products: 41.3 us -> 31.3 us
    dot_general x8, matrix products: 20.7 us -> 12.1 us  [softmax_part(): lax.dot_general(queries[:, lanes], keys_row[:, lanes], (((1,), (1,)), (()...]
    all_gather x2, waiting for transfers between devices: 55.3 us -> 61.2 us  [row_gather(): gathered = lax.all_gather(array, ('col', 'core'), axis=0)]
    ppermute x2, waiting for transfers between devices: 4.81 us -> 7 us  [body(): lax.ppermute((below_sums, below_stats), 'row', row_down)]
    ppermute x1, waiting for transfers between devices: 3.74 us -> 5.72 us  [body(): queries_below = lax.ppermute(query_rows, 'row', row_up)]
  transfers between devices with their start and end apart: 6 -> 6, of which waited for: 4 -> 4; matrix products, arithmetic and copies ran while one was open for 35% -> 22% of each run, Pallas kernels for 0% -> 0%
where the time goes in v5:
time: 153 us; the launch traced here: 151 us
  waiting for transfers between devices  74.6 us (49%)
  matrix products  31.3 us (20%)
  between operations  14.5 us (9%)
  other arithmetic  14.1 us (9%)
  starting transfers between devices  13.2 us (9%)
  local copies, waits for them, and re-layouts  3.27 us (2%)
    all_gather x2, waiting for transfers between devices, row_gather(): gathered = lax.all_gather(array, ('col', 'core'), axis=0)  61.2 us
    dot_general x8, matrix products, weighted_part(): jnp.dot(weights, values_row[:, lanes], preferred_element_type=jnp.float32)  14.4 us
    reduce_sum x2, other arithmetic, softmax_part(): row_total = jnp.sum(exp_terms, axis=1, keepdims=True)  12.1 us
    dot_general x8, matrix products, softmax_part(): lax.dot_general(queries[:, lanes], keys_row[:, lanes], (((1,), (1,)), (()...  12.1 us
    ppermute x2, waiting for transfers between devices, body(): lax.ppermute((below_sums, below_stats), 'row', row_down)  7 us
    ppermute x2, starting transfers between devices, body(): lax.ppermute((below_sums, below_stats), 'row', row_down)  6.44 us
    ppermute x1, waiting for transfers between devices, body(): queries_below = lax.ppermute(query_rows, 'row', row_up)  5.72 us
    ppermute x1, starting transfers between devices, passed_along(): return lax.ppermute(block, axis, route)  5.39 us
  transfers between devices with their start and end apart: 6, of which 4 were waited for; matrix products, arithmetic and copies ran while one was open for 22% of the time, Pallas kernels for 0%

profile of v5, /device:TPU:1, one launch (start us, length us, event | category | flops | bytes accessed | tf_op | source)
XLA Modules:
  0.0 151.0 jit_solution(9453749419555028444)
XLA Ops:
  8.0 1.1 multiply_convert_fusion
  9.1 5.4 %collective-permute-start = (bf16[127,512]{1,0:T(8,128)(2,1)S(1)}, bf16[127,512]{1,0:T(8,128)(2,1)S(1)}, u32[]{:S(2)}, u32[]{:S(2)}) collective-permute-start(bf16[127,512]{1,0:T(8,128)(2,1)S(1)} %slice.132), channel_id=1, source_target_pairs={{0,4},{4,8},{8,12},{12,16},{16,20},{20,24},{24,28},{28,32},{32,36}... | collective-permute-start | bytes 390152 | tf_op jit(solution)/shard_map/ppermute | solution.py:21
  14.7 1.8 %fusion.26 = bf16[4,8,128,128]{3,1,2,0:T(8,128)(2,1)S(1)} fusion(bf16[32,128]{1,0:T(8,128)(2,1)S(1)} %copy-done, s32[16384]{0:T(1024)S(1)} %subtract_bitcast_fusion), kind=kOutput, calls=%fused_computation.48 | convolution fusion | flops 136839168 | bytes 1122304 | tf_op jit(solution)/shard_map/dot_general | solution.py:30
  17.5 1.8 %fusion.27 = bf16[4,8,128,128]{3,1,2,0:T(8,128)(2,1)S(1)} fusion(bf16[32,128]{1,0:T(8,128)(2,1)S(1)} %copy-done, s32[16384]{0:T(1024)S(1)} %broadcast_add_fusion), kind=kOutput, calls=%fused_computation.49 | convolution fusion | flops 136839168 | bytes 1122304 | tf_op jit(solution)/shard_map/dot_general | solution.py:30
  21.0 0.8 fusion.52
  21.8 1.3 collective-permute-start.1
  23.2 5.7 %collective-permute-done.1 = bf16[256,512]{1,0:T(8,128)(2,1)S(1)} collective-permute-done((bf16[256,512]{1,0:T(8,128)(2,1)S(1)}, bf16[256,512]{1,0:T(8,128)(2,1)S(1)}, u32[]{:S(2)}, u32[]{:S(2)}) %collective-permute-start.1) | collective-permute-done | bytes 262176 | tf_op jit(solution)/shard_map/ppermute | solution.py:74
  28.9 32.8 %all-gather.5.cloned.1.call-done = bf16[4096,512]{1,0:T(8,128)(2,1)} async-done(((bf16[256,512]{1,0:T(8,128)(2,1)}), bf16[4096,512]{1,0:T(8,128)(2,1)}) %all-gather.5.cloned.1.call-update) | async-done | bytes 4194320 | tf_op jit(solution)/shard_map/all_gather | solution.py:69
  61.8 2.7 %fusion.104 = (f32[256]{0:T(256)S(1)}, f32[256,4096]{1,0:T(8,128)S(1)}) fusion(bf16[4096,512]{1,0:T(8,128)(2,1)} %all-gather.5.cloned.1.call-done, bf16[256,512]{1,0:T(8,128)(2,1)S(1)} %collective-permute-done.1, s32[256]{0:T(256)S(1)} %iota_add_fusion.2, s32[4096]{0:T(1024)S(1)} %iota_add_fusion, pred[4096]{0:T(1024)(128)(4,1)S(1)} %fusion.86), kind=kOutput, calls=%fused_computation.145 | convolution fusion | flops 273678080 | bytes 5330944 | tf_op jit(solution)/shard_map/dot_general | solution.py:88
  64.5 1.3 fusion.105
  65.8 1.3 fusion.106
  67.1 1.3 fusion.107
  68.5 6.3 %fusion.10 = (f32[256]{0:T(256)S(1)}, f32[256]{0:T(256)S(1)}, f32[256]{0:T(256)S(1)}, f32[256]{0:T(256)S(1)}, bf16[256,4096]{1,0:T(8,128)(2,1)}, /*index=5*/bf16...) fusion(f32[256,4096]{1,0:T(8,128)S(1)} %get-tuple-element.104, f32[256]{0:T(256)S(1)} %get-tuple-element.103, ...), kind=kLoop, calls=%fused_computation.32 | loop fusion | flops 18873344 | bytes 25195520 | tf_op jit(solution)/shard_map/reduce_sum | solution.py:99
  74.7 1.3 fusion.108
  76.1 1.3 fusion.109
  77.4 1.3 fusion.110
  78.7 1.3 fusion.111
  80.1 5.8 %fusion.24 = (f32[256]{0:T(256)S(1)}, f32[256]{0:T(256)S(1)}, f32[256]{0:T(256)S(1)}, f32[256]{0:T(256)S(1)}, bf16[256,4096]{1,0:T(8,128)(2,1)}, /*index=5*/bf16...) fusion(f32[256,4096]{1,0:T(8,128)S(1)} %get-tuple-element.112, ...), kind=kLoop, calls=%fused_computation.46 | loop fusion | flops 18873344 | bytes 25195520 | tf_op jit(solution)/shard_map/reduce_sum | solution.py:99
  85.9 28.4 %all-gather.7.cloned.1.call-done = bf16[4096,512]{0,1:T(8,128)(2,1)} async-done(((bf16[256,512]{0,1:T(8,128)(2,1)}), bf16[4096,512]{0,1:T(8,128)(2,1)}) %all-gather.7.cloned.1.call-update) | async-done | bytes 4194320 | tf_op jit(solution)/shard_map/all_gather | solution.py:69
  114.3 2.8 %fusion.33 = f32[256,128]{0,1:T(8,128)S(1)} fusion(bf16[256,4096]{1,0:T(8,128)(2,1)} %get-tuple-element.35, bf16[4096,512]{0,1:T(8,128)(2,1)} %all-gather.7.cloned.1.call-done), kind=kOutput, calls=%fused_computation.60 | convolution fusion | flops 268435456 | bytes 3276800 | tf_op jit(solution)/shard_map/dot_general | solution.py:104
  117.2 2.8 %fusion.38 = f32[256,128]{0,1:T(8,128)S(1)} fusion(bf16[256,4096]{1,0:T(8,128)(2,1)} %get-tuple-element.34, bf16[4096,512]{0,1:T(8,128)(2,1)} %all-gather.7.cloned.1.call-done), kind=kOutput, calls=%fused_computation.65 | convolution fusion | flops 268435456 | bytes 3276800 | tf_op jit(solution)/shard_map/dot_general | solution.py:104
  120.1 0.8 fusion.43
  120.9 0.8 fusion.48
  121.8 3.1 %collective-permute-start.3 = (f32[256,512]{0,1:T(8,128)S(1)}, f32[256,512]{0,1:T(8,128)S(1)}, u32[]{:S(2)}, u32[]{:S(2)}) collective-permute-start(f32[256,512]{0,1:T(8,128)S(1)} %pad_maximum_fusion), channel_id=1, source_target_pairs={{0,64},{64,128},{128,192},{192,256},{256,320},{320,384},{384,448},... | collective-permute-start | bytes 1572872 | tf_op jit(solution)/shard_map/ppermute | solution.py:117
  124.9 3.3 %collective-permute-start.2 = (f32[256,8]{0,1:T(8,128)S(1)}, f32[256,8]{0,1:T(8,128)S(1)}, u32[]{:S(2)}, u32[]{:S(2)}) collective-permute-start(f32[256,8]{0,1:T(8,128)S(1)} %concatenate.18), channel_id=1, source_target_pairs={{0,64},{64,128},{128,192},{192,256},{256,320},{320,384},{384,448},... | collective-permute-start | bytes 24584 | tf_op jit(solution)/shard_map/ppermute | solution.py:117
  128.3 0.8 copy.18
  129.1 7.0 %collective-permute-done.2 = f32[256,8]{0,1:T(8,128)S(1)} collective-permute-done((f32[256,8]{0,1:T(8,128)S(1)}, f32[256,8]{0,1:T(8,128)S(1)}, u32[]{:S(2)}, u32[]{:S(2)}) %collective-permute-start.2) | collective-permute-done | bytes 8224 | tf_op jit(solution)/shard_map/ppermute | solution.py:117
  136.2 2.7 %fusion.68 = bf16[256,128]{0,1:T(8,128)(2,1)S(1)} fusion(f32[256,512]{0,1:T(8,128)S(1)} %collective-permute-done.3, f32[256]{0:T(256)S(1)} %bitcast.104, f32[256]{0:T(256)S(1)} %bitcast.105, f32[256]{0:T(256)S(1)} %bitcast.106, bf16[256,4096]{1,0:T(8,128)(2,1)} %get-tuple-element.59, bf16[4096,512]{0,1:T(8,128)(2,1)} %all-gather.7.cloned.1.call-done), kind=kOutput, calls=%fused_computation.103 | convolution fusion | flops 268599296 | bytes 3345408 | tf_op jit(solution)/shard_map/dot_general | solution.py:104
  138.9 2.7 %fusion.67 = bf16[256,128]{0,1:T(8,128)(2,1)S(1)} fusion(f32[256,512]{0,1:T(8,128)S(1)} %collective-permute-done.3, f32[256]{0:T(256)S(1)} %bitcast.101, f32[256]{0:T(256)S(1)} %bitcast.102, f32[256]{0:T(256)S(1)} %bitcast.103, bf16[256,4096]{1,0:T(8,128)(2,1)} %get-tuple-element.56, bf16[4096,512]{0,1:T(8,128)(2,1)} %all-gather.7.cloned.1.call-done), kind=kOutput, calls=%fused_computation.102 | convolution fusion | flops 268599296 | bytes 3345408 | tf_op jit(solution)/shard_map/dot_general | solution.py:104
  141.6 0.8 fusion.66
  142.4 0.8 fusion.65
  143.3 0.8 copy.19
  (53 shorter events, 3.8 us)
Async XLA Ops:
  7.2 7.5 %copy-start = (bf16[32,128]{1,0:T(8,128)(2,1)S(1)}, bf16[32,128]{1,0:T(8,128)(2,1)}, u32[]{:S(2)}) copy-start(bf16[32,128]{1,0:T(8,128)(2,1)} %param.9) | copy-start | bytes 24580
  7.2 54.6 %all-gather.5.cloned.1.call-start = ((), (), s32[]{:S(2)}) async-start(), calls=%async_computation | async-start | bytes 4456448 | tf_op jit(solution)/shard_map/all_gather | solution.py:69
  7.9 106.4 %all-gather.7.cloned.1.call-start = ((), (), s32[]{:S(2)}) async-start(), calls=%async_computation.1 | async-start | bytes 4456448 | tf_op jit(solution)/shard_map/all_gather | solution.py:69
  9.1 10.7 %collective-permute-start = (bf16[127,512]{1,0:T(8,128)(2,1)S(1)}, bf16[127,512]{1,0:T(8,128)(2,1)S(1)}, u32[]{:S(2)}, u32[]{:S(2)}) collective-permute-start(bf16[127,512]{1,0:T(8,128)(2,1)S(1)} %slice.132), channel_id=1, source_target_pairs={{0,4},{4,8},{8,12},{12,16},{16,20},{20,24},{24,28},{28,32},{32,36}... | collective-permute-start | bytes 390152 | tf_op jit(solution)/shard_map/ppermute | solution.py:21
  16.7 2.9 %copy-start.6 = (bf16[256,512]{1,0:T(8,128)(2,1)S(1)}, bf16[256,512]{1,0:T(8,128)(2,1)}, u32[]{:S(2)}) copy-start(bf16[256,512]{1,0:T(8,128)(2,1)} %param.6) | copy-start | bytes 786436
  19.2 2.6 %copy-start.10 = (bf16[256,512]{1,0:T(8,128)(2,1)S(1)}, bf16[256,512]{1,0:T(8,128)(2,1)}, u32[]{:S(2)}) copy-start(bf16[256,512]{1,0:T(8,128)(2,1)} %param.10) | copy-start | bytes 786436
  21.8 7.1 %collective-permute-start.1 = (bf16[256,512]{1,0:T(8,128)(2,1)S(1)}, bf16[256,512]{1,0:T(8,128)(2,1)S(1)}, u32[]{:S(2)}, u32[]{:S(2)}) collective-permute-start(bf16[256,512]{1,0:T(8,128)(2,1)S(1)} %copy-done.10), channel_id=1, source_target_pairs={{64,0},{128,64},{192,128},{256,192},{320,256},{384,320},{448,384},... | collective-permute-start | bytes 786440 | tf_op jit(solution)/shard_map/ppermute | solution.py:74
  61.8 2.7 %copy-start.7 = (bf16[4096,512]{1,0:T(8,128)(2,1)S(1)}, bf16[4096,512]{1,0:T(8,128)(2,1)}, u32[]{:S(2)}) copy-start(bf16[4096,512]{1,0:T(8,128)(2,1)} %all-gather.5.cloned.1.call-done) | copy-start | bytes 12582916
  114.3 5.7 %copy-start.5 = (bf16[256,4096]{1,0:T(8,128)(2,1)S(1)}, bf16[256,4096]{1,0:T(8,128)(2,1)}, u32[]{:S(2)}) copy-start(bf16[256,4096]{1,0:T(8,128)(2,1)} %get-tuple-element.33) | copy-start | bytes 6291460
  114.3 5.7 %copy-start.8 = (bf16[4096,512]{0,1:T(8,128)(2,1)S(1)}, bf16[4096,512]{0,1:T(8,128)(2,1)}, u32[]{:S(2)}) copy-start(bf16[4096,512]{0,1:T(8,128)(2,1)} %all-gather.7.cloned.1.call-done) | copy-start | bytes 12582916
  117.2 3.7 %copy-start.4 = (bf16[256,4096]{1,0:T(8,128)(2,1)S(1)}, bf16[256,4096]{1,0:T(8,128)(2,1)}, u32[]{:S(2)}) copy-start(bf16[256,4096]{1,0:T(8,128)(2,1)} %get-tuple-element.32) | copy-start | bytes 6291460
  120.0 8.2 %copy-start.2 = (bf16[256,512]{0,1:T(8,128)(2,1)S(1)}, bf16[256,512]{0,1:T(8,128)(2,1)}, u32[]{:S(2)}) copy-start(bf16[256,512]{0,1:T(8,128)(2,1)} %fusion.52) | copy-start | bytes 786436
  121.8 14.3 %collective-permute-start.3 = (f32[256,512]{0,1:T(8,128)S(1)}, f32[256,512]{0,1:T(8,128)S(1)}, u32[]{:S(2)}, u32[]{:S(2)}) collective-permute-start(f32[256,512]{0,1:T(8,128)S(1)} %pad_maximum_fusion), channel_id=1, source_target_pairs={{0,64},{64,128},{128,192},{192,256},{256,320},{320,384},{384,448},... | collective-permute-start | bytes 1572872 | tf_op jit(solution)/shard_map/ppermute | solution.py:117
  124.9 11.2 %collective-permute-start.2 = (f32[256,8]{0,1:T(8,128)S(1)}, f32[256,8]{0,1:T(8,128)S(1)}, u32[]{:S(2)}, u32[]{:S(2)}) collective-permute-start(f32[256,8]{0,1:T(8,128)S(1)} %concatenate.18), channel_id=1, source_target_pairs={{0,64},{64,128},{128,192},{192,256},{256,320},{320,384},{384,448},... | collective-permute-start | bytes 24584 | tf_op jit(solution)/shard_map/ppermute | solution.py:117
  129.1 12.5 %copy-start.3 = (bf16[256,4096]{1,0:T(8,128)(2,1)S(1)}, bf16[256,4096]{1,0:T(8,128)(2,1)}, u32[]{:S(2)}) copy-start(bf16[256,4096]{1,0:T(8,128)(2,1)} %get-tuple-element.53) | copy-start | bytes 6291460
  129.1 12.5 %copy-start.9 = (bf16[4096,512]{0,1:T(8,128)(2,1)S(1)}, bf16[4096,512]{0,1:T(8,128)(2,1)}, u32[]{:S(2)}) copy-start(bf16[4096,512]{0,1:T(8,128)(2,1)} %all-gather.7.cloned.1.call-done) | copy-start | bytes 12582916
  141.6 2.6 %copy-start.1 = (bf16[32,128]{1,0:T(8,128)(2,1)S(1)}, bf16[32,128]{1,0:T(8,128)(2,1)}, u32[]{:S(2)}) copy-start(bf16[32,128]{1,0:T(8,128)(2,1)} %param.9) | copy-start | bytes 24580
Sparse Core Ops, SparseCore 0:
  10.1 51.5 all-gather.4
  64.4 49.9 all-gather.6

commit v6 on v5

--- a/solution.py
+++ b/solution.py
@@ -114,7 +114,13 @@
     below_sums, below_stats, own_weights = lax.optimization_barrier(
         (below_sums, below_stats, [weights for weights, _, _ in own_parts])
     )
-    above_sums, above_stats = lax.ppermute((below_sums, below_stats), "row", row_down)
+    stat_lanes = 2 * local_heads
+    packed = jnp.concatenate(
+        [below_sums, below_stats, jnp.zeros((row_count, HEAD_DIM - stat_lanes), jnp.float32)], axis=1
+    )
+    packed = lax.ppermute(packed, "row", row_down)
+    above_sums = packed[:, :channels]
+    above_stats = packed[:, channels : channels + stat_lanes]
 
     head_outputs = []
     for head, (weights, (_, own_peak, own_total)) in enumerate(zip(own_weights, own_parts)):

time: 153 us -> 159 us (1.039)
  waiting for transfers between devices: 74.6 us -> 79.7 us
  starting transfers between devices: 13.2 us -> 10.7 us
  matrix products: 31.3 us -> 33.2 us
    ppermute x2 -> x1, waiting for transfers between devices: 7 us -> 12.1 us  [body(): packed = lax.ppermute(packed, 'row', row_down)]
    ppermute x2 -> x1, starting transfers between devices: 6.44 us -> 3.93 us  [body(): packed = lax.ppermute(packed, 'row', row_down)]
    dot_general x8, matrix products: 14.4 us -> 16.4 us  [weighted_part(): jnp.dot(weights, values_row[:, lanes], preferred_element_type=jnp.float32)]
  transfers between devices with their start and end apart: 6 -> 5, of which waited for: 4 -> 4; matrix products, arithmetic and copies ran while one was open for 22% -> 21% of each run, Pallas kernels for 0% -> 0%
where the time goes in v6:
time: 159 us; the launch traced here: 157 us
  waiting for transfers between devices  79.7 us (50%)
  matrix products  33.2 us (21%)
  other arithmetic  15.2 us (10%)
  between operations  14.5 us (9%)
  starting transfers between devices  10.7 us (7%)
  local copies, waits for them, and re-layouts  3.35 us (2%)
    all_gather x2, waiting for transfers between devices, row_gather(): gathered = lax.all_gather(array, ('col', 'core'), axis=0)  61.3 us
    dot_general x8, matrix products, weighted_part(): jnp.dot(weights, values_row[:, lanes], preferred_element_type=jnp.float32)  16.4 us
    ppermute x1, waiting for transfers between devices, body(): packed = lax.ppermute(packed, 'row', row_down)  12.1 us
    reduce_sum x2, other arithmetic, softmax_part(): row_total = jnp.sum(exp_terms, axis=1, keepdims=True)  12.1 us
    dot_general x8, matrix products, softmax_part(): lax.dot_general(queries[:, lanes], keys_row[:, lanes], (((1,), (1,)), (()...  12 us
    ppermute x1, waiting for transfers between devices, body(): queries_below = lax.ppermute(query_rows, 'row', row_up)  5.65 us
    ppermute x1, starting transfers between devices, passed_along(): return lax.ppermute(block, axis, route)  5.39 us
    ppermute x1, starting transfers between devices, body(): packed = lax.ppermute(packed, 'row', row_down)  3.93 us
  transfers between devices with their start and end apart: 5, of which 4 were waited for; matrix products, arithmetic and copies ran while one was open for 21% of the time, Pallas kernels for 0%

profile of v6, /device:TPU:1, one launch (start us, length us, event | category | flops | bytes accessed | tf_op | source)
XLA Modules:
  0.0 156.7 jit_solution(13914123543478168586)
XLA Ops:
  8.0 1.1 multiply_convert_fusion
  9.1 5.4 %collective-permute-start = (bf16[127,512]{1,0:T(8,128)(2,1)S(1)}, bf16[127,512]{1,0:T(8,128)(2,1)S(1)}, u32[]{:S(2)}, u32[]{:S(2)}) collective-permute-start(bf16[127,512]{1,0:T(8,128)(2,1)S(1)} %slice.146), channel_id=1, source_target_pairs={{0,4},{4,8},{8,12},{12,16},{16,20},{20,24},{24,28},{28,32},{32,36}... | collective-permute-start | bytes 390152 | tf_op jit(solution)/shard_map/ppermute | solution.py:21
  14.7 1.8 %fusion.26 = bf16[4,8,128,128]{3,1,2,0:T(8,128)(2,1)S(1)} fusion(bf16[32,128]{1,0:T(8,128)(2,1)S(1)} %copy-done, s32[16384]{0:T(1024)S(1)} %subtract_bitcast_fusion), kind=kOutput, calls=%fused_computation.48 | convolution fusion | flops 136839168 | bytes 1122304 | tf_op jit(solution)/shard_map/dot_general | solution.py:30
  17.5 1.8 %fusion.27 = bf16[4,8,128,128]{3,1,2,0:T(8,128)(2,1)S(1)} fusion(bf16[32,128]{1,0:T(8,128)(2,1)S(1)} %copy-done, s32[16384]{0:T(1024)S(1)} %broadcast_add_fusion), kind=kOutput, calls=%fused_computation.49 | convolution fusion | flops 136839168 | bytes 1122304 | tf_op jit(solution)/shard_map/dot_general | solution.py:30
  21.0 0.8 fusion.52
  21.8 1.3 collective-permute-start.1
  23.3 5.6 %collective-permute-done.1 = bf16[256,512]{1,0:T(8,128)(2,1)S(1)} collective-permute-done((bf16[256,512]{1,0:T(8,128)(2,1)S(1)}, bf16[256,512]{1,0:T(8,128)(2,1)S(1)}, u32[]{:S(2)}, u32[]{:S(2)}) %collective-permute-start.1) | collective-permute-done | bytes 262176 | tf_op jit(solution)/shard_map/ppermute | solution.py:74
  28.9 32.8 %all-gather.5.cloned.1.call-done = bf16[4096,512]{1,0:T(8,128)(2,1)} async-done(((bf16[256,512]{1,0:T(8,128)(2,1)}), bf16[4096,512]{1,0:T(8,128)(2,1)}) %all-gather.5.cloned.1.call-update) | async-done | bytes 4194320 | tf_op jit(solution)/shard_map/all_gather | solution.py:69
  61.8 2.7 %fusion.104 = (f32[256]{0:T(256)S(1)}, f32[256,4096]{1,0:T(8,128)S(1)}) fusion(bf16[4096,512]{1,0:T(8,128)(2,1)} %all-gather.5.cloned.1.call-done, bf16[256,512]{1,0:T(8,128)(2,1)S(1)} %collective-permute-done.1, s32[256]{0:T(256)S(1)} %iota_add_fusion.2, s32[4096]{0:T(1024)S(1)} %iota_add_fusion, pred[4096]{0:T(1024)(128)(4,1)S(1)} %fusion.86), kind=kOutput, calls=%fused_computation.146 | convolution fusion | flops 273678080 | bytes 5330944 | tf_op jit(solution)/shard_map/dot_general | solution.py:88
  64.4 1.3 fusion.105
  65.8 1.3 fusion.106
  67.1 1.3 fusion.107
  68.4 6.3 %fusion.10 = (f32[256]{0:T(256)S(1)}, f32[256]{0:T(256)S(1)}, f32[256]{0:T(256)S(1)}, f32[256]{0:T(256)S(1)}, bf16[256,4096]{1,0:T(8,128)(2,1)}, /*index=5*/bf16...) fusion(f32[256,4096]{1,0:T(8,128)S(1)} %get-tuple-element.104, f32[256]{0:T(256)S(1)} %get-tuple-element.103, ...), kind=kLoop, calls=%fused_computation.32 | loop fusion | flops 18873344 | bytes 25195520 | tf_op jit(solution)/shard_map/reduce_sum | solution.py:99
  74.8 1.3 fusion.108
  76.1 1.3 fusion.109
  77.4 1.3 fusion.110
  78.8 1.3 fusion.111
  80.1 5.8 %fusion.24 = (f32[256]{0:T(256)S(1)}, f32[256]{0:T(256)S(1)}, f32[256]{0:T(256)S(1)}, f32[256]{0:T(256)S(1)}, bf16[256,4096]{1,0:T(8,128)(2,1)}, /*index=5*/bf16...) fusion(f32[256,4096]{1,0:T(8,128)S(1)} %get-tuple-element.112, ...), kind=kLoop, calls=%fused_computation.46 | loop fusion | flops 18873344 | bytes 25195520 | tf_op jit(solution)/shard_map/reduce_sum | solution.py:99
  85.9 28.4 %all-gather.7.cloned.1.call-done = bf16[4096,512]{0,1:T(8,128)(2,1)} async-done(((bf16[256,512]{0,1:T(8,128)(2,1)}), bf16[4096,512]{0,1:T(8,128)(2,1)}) %all-gather.7.cloned.1.call-update) | async-done | bytes 4194320 | tf_op jit(solution)/shard_map/all_gather | solution.py:69
  114.3 2.8 %fusion.33 = f32[256,128]{0,1:T(8,128)S(1)} fusion(bf16[256,4096]{1,0:T(8,128)(2,1)} %get-tuple-element.35, bf16[4096,512]{0,1:T(8,128)(2,1)} %all-gather.7.cloned.1.call-done), kind=kOutput, calls=%fused_computation.60 | convolution fusion | flops 268435456 | bytes 3276800 | tf_op jit(solution)/shard_map/dot_general | solution.py:104
  117.2 2.8 %fusion.38 = f32[256,128]{0,1:T(8,128)S(1)} fusion(bf16[256,4096]{1,0:T(8,128)(2,1)} %get-tuple-element.34, bf16[4096,512]{0,1:T(8,128)(2,1)} %all-gather.7.cloned.1.call-done), kind=kOutput, calls=%fused_computation.65 | convolution fusion | flops 268435456 | bytes 3276800 | tf_op jit(solution)/shard_map/dot_general | solution.py:104
  120.1 0.8 fusion.43
  120.9 0.8 fusion.48
  121.9 3.9 %collective-permute-start.2 = (f32[256,640]{0,1:T(8,128)S(1)}, f32[256,640]{0,1:T(8,128)}, u32[]{:S(2)}, u32[]{:S(2)}) collective-permute-start(f32[256,640]{0,1:T(8,128)S(1)} %maximum_maximum_fusion), channel_id=1, source_target_pairs={{0,64},{64,128},{128,192},{192,256},{256,320},{320,384},{384,448},... | collective-permute-start | bytes 1966088 | tf_op jit(solution)/shard_map/ppermute | solution.py:121
  125.9 0.8 copy.18
  126.7 12.1 %collective-permute-done.2 = f32[256,640]{0,1:T(8,128)} collective-permute-done((f32[256,640]{0,1:T(8,128)S(1)}, f32[256,640]{0,1:T(8,128)}, u32[]{:S(2)}, u32[]{:S(2)}) %collective-permute-start.2) | collective-permute-done | bytes 655392 | tf_op jit(solution)/shard_map/ppermute | solution.py:121
  138.9 1.0 multiply_add_fusion.3
  139.9 2.8 %fusion.68 = bf16[256,128]{0,1:T(8,128)(2,1)S(1)} fusion(f32[256,640]{0,1:T(8,128)} %collective-permute-done.2, f32[256]{0:T(256)S(1)} %bitcast.104, f32[256]{0:T(256)S(1)} %bitcast.105, f32[256]{0:T(256)S(1)} %bitcast.106, bf16[256,4096]{1,0:T(8,128)(2,1)} %get-tuple-element.59, bf16[4096,512]{0,1:T(8,128)(2,1)} %all-gather.7.cloned.1.call-done), kind=kOutput, calls=%fused_computation.104 | convolution fusion | flops 268599296 | bytes 3345408 | tf_op jit(solution)/shard_map/dot_general | solution.py:104
  142.6 2.8 %fusion.67 = bf16[256,128]{0,1:T(8,128)(2,1)S(1)} fusion(f32[256,640]{0,1:T(8,128)} %collective-permute-done.2, f32[256]{0:T(256)S(1)} %bitcast.101, f32[256]{0:T(256)S(1)} %bitcast.102, f32[256]{0:T(256)S(1)} %bitcast.103, bf16[256,4096]{1,0:T(8,128)(2,1)} %get-tuple-element.56, bf16[4096,512]{0,1:T(8,128)(2,1)} %all-gather.7.cloned.1.call-done), kind=kOutput, calls=%fused_computation.103 | convolution fusion | flops 268599296 | bytes 3345408 | tf_op jit(solution)/shard_map/dot_general | solution.py:104
  145.5 1.7 %fusion.66 = bf16[256,128]{0,1:T(8,128)(2,1)S(1)} fusion(f32[256,640]{0,1:T(8,128)} %collective-permute-done.2, f32[256]{0:T(256)S(1)} %bitcast.98, f32[256]{0:T(256)S(1)} %bitcast.99, f32[256]{0:T(256)S(1)} %bitcast.100, bf16[256,4096]{1,0:T(8,128)(2,1)S(1)} %copy-done.3, bf16[4096,512]{0,1:T(8,128)(2,1)S(1)} %copy-done.9), kind=kOutput, calls=%fused_computation.102 | convolution fusion | flops 268599296 | bytes 3345408 | tf_op jit(solution)/shard_map/dot_general | solution.py:104
  147.2 1.7 %fusion.65 = bf16[256,128]{0,1:T(8,128)(2,1)S(1)} fusion(f32[256,640]{0,1:T(8,128)} %collective-permute-done.2, f32[256]{0:T(256)S(1)} %bitcast.95, f32[256]{0:T(256)S(1)} %bitcast.97, f32[256]{0:T(256)S(1)} %bitcast.96, bf16[256,4096]{1,0:T(8,128)(2,1)S(1)} %get-tuple-element.48, bf16[4096,512]{0,1:T(8,128)(2,1)S(1)} %copy-done.9), kind=kOutput, calls=%fused_computation.101 | convolution fusion | flops 268599296 | bytes 3345408 | tf_op jit(solution)/shard_map/dot_general | solution.py:104
  149.0 0.8 copy.19
  (54 shorter events, 4.0 us)
Async XLA Ops:
  7.2 7.5 %copy-start = (bf16[32,128]{1,0:T(8,128)(2,1)S(1)}, bf16[32,128]{1,0:T(8,128)(2,1)}, u32[]{:S(2)}) copy-start(bf16[32,128]{1,0:T(8,128)(2,1)} %param.9) | copy-start | bytes 24580
  7.2 54.6 %all-gather.5.cloned.1.call-start = ((), (), s32[]{:S(2)}) async-start(), calls=%async_computation | async-start | bytes 4456448 | tf_op jit(solution)/shard_map/all_gather | solution.py:69
  7.9 106.4 %all-gather.7.cloned.1.call-start = ((), (), s32[]{:S(2)}) async-start(), calls=%async_computation.1 | async-start | bytes 4456448 | tf_op jit(solution)/shard_map/all_gather | solution.py:69
  9.1 10.7 %collective-permute-start = (bf16[127,512]{1,0:T(8,128)(2,1)S(1)}, bf16[127,512]{1,0:T(8,128)(2,1)S(1)}, u32[]{:S(2)}, u32[]{:S(2)}) collective-permute-start(bf16[127,512]{1,0:T(8,128)(2,1)S(1)} %slice.146), channel_id=1, source_target_pairs={{0,4},{4,8},{8,12},{12,16},{16,20},{20,24},{24,28},{28,32},{32,36}... | collective-permute-start | bytes 390152 | tf_op jit(solution)/shard_map/ppermute | solution.py:21
  16.7 2.9 %copy-start.6 = (bf16[256,512]{1,0:T(8,128)(2,1)S(1)}, bf16[256,512]{1,0:T(8,128)(2,1)}, u32[]{:S(2)}) copy-start(bf16[256,512]{1,0:T(8,128)(2,1)} %param.6) | copy-start | bytes 786436
  19.2 2.6 %copy-start.10 = (bf16[256,512]{1,0:T(8,128)(2,1)S(1)}, bf16[256,512]{1,0:T(8,128)(2,1)}, u32[]{:S(2)}) copy-start(bf16[256,512]{1,0:T(8,128)(2,1)} %param.10) | copy-start | bytes 786436
  21.8 7.1 %collective-permute-start.1 = (bf16[256,512]{1,0:T(8,128)(2,1)S(1)}, bf16[256,512]{1,0:T(8,128)(2,1)S(1)}, u32[]{:S(2)}, u32[]{:S(2)}) collective-permute-start(bf16[256,512]{1,0:T(8,128)(2,1)S(1)} %copy-done.10), channel_id=1, source_target_pairs={{64,0},{128,64},{192,128},{256,192},{320,256},{384,320},{448,384},... | collective-permute-start | bytes 786440 | tf_op jit(solution)/shard_map/ppermute | solution.py:74
  61.8 2.7 %copy-start.7 = (bf16[4096,512]{1,0:T(8,128)(2,1)S(1)}, bf16[4096,512]{1,0:T(8,128)(2,1)}, u32[]{:S(2)}) copy-start(bf16[4096,512]{1,0:T(8,128)(2,1)} %all-gather.5.cloned.1.call-done) | copy-start | bytes 12582916
  114.3 5.7 %copy-start.5 = (bf16[256,4096]{1,0:T(8,128)(2,1)S(1)}, bf16[256,4096]{1,0:T(8,128)(2,1)}, u32[]{:S(2)}) copy-start(bf16[256,4096]{1,0:T(8,128)(2,1)} %get-tuple-element.33) | copy-start | bytes 6291460
  114.3 5.7 %copy-start.8 = (bf16[4096,512]{0,1:T(8,128)(2,1)S(1)}, bf16[4096,512]{0,1:T(8,128)(2,1)}, u32[]{:S(2)}) copy-start(bf16[4096,512]{0,1:T(8,128)(2,1)} %all-gather.7.cloned.1.call-done) | copy-start | bytes 12582916
  117.2 3.7 %copy-start.4 = (bf16[256,4096]{1,0:T(8,128)(2,1)S(1)}, bf16[256,4096]{1,0:T(8,128)(2,1)}, u32[]{:S(2)}) copy-start(bf16[256,4096]{1,0:T(8,128)(2,1)} %get-tuple-element.32) | copy-start | bytes 6291460
  120.0 5.8 %copy-start.2 = (bf16[256,512]{0,1:T(8,128)(2,1)S(1)}, bf16[256,512]{0,1:T(8,128)(2,1)}, u32[]{:S(2)}) copy-start(bf16[256,512]{0,1:T(8,128)(2,1)} %fusion.52) | copy-start | bytes 786436
  121.9 16.9 %collective-permute-start.2 = (f32[256,640]{0,1:T(8,128)S(1)}, f32[256,640]{0,1:T(8,128)}, u32[]{:S(2)}, u32[]{:S(2)}) collective-permute-start(f32[256,640]{0,1:T(8,128)S(1)} %maximum_maximum_fusion), channel_id=1, source_target_pairs={{0,64},{64,128},{128,192},{192,256},{256,320},{320,384},{384,448},... | collective-permute-start | bytes 1966088 | tf_op jit(solution)/shard_map/ppermute | solution.py:121
  126.7 18.7 %copy-start.3 = (bf16[256,4096]{1,0:T(8,128)(2,1)S(1)}, bf16[256,4096]{1,0:T(8,128)(2,1)}, u32[]{:S(2)}) copy-start(bf16[256,4096]{1,0:T(8,128)(2,1)} %get-tuple-element.53) | copy-start | bytes 6291460
  126.7 18.7 %copy-start.9 = (bf16[4096,512]{0,1:T(8,128)(2,1)S(1)}, bf16[4096,512]{0,1:T(8,128)(2,1)}, u32[]{:S(2)}) copy-start(bf16[4096,512]{0,1:T(8,128)(2,1)} %all-gather.7.cloned.1.call-done) | copy-start | bytes 12582916
  145.4 4.4 %copy-start.1 = (bf16[32,128]{1,0:T(8,128)(2,1)S(1)}, bf16[32,128]{1,0:T(8,128)(2,1)}, u32[]{:S(2)}) copy-start(bf16[32,128]{1,0:T(8,128)(2,1)} %param.9) | copy-start | bytes 24580
Sparse Core Ops, SparseCore 0:
  10.1 51.5 all-gather.4
  64.4 49.8 all-gather.6

commit v7 on v5

--- a/solution.py
+++ b/solution.py
@@ -114,7 +114,10 @@
     below_sums, below_stats, own_weights = lax.optimization_barrier(
         (below_sums, below_stats, [weights for weights, _, _ in own_parts])
     )
-    above_sums, above_stats = lax.ppermute((below_sums, below_stats), "row", row_down)
+    above_sums, above_stats = lax.ppermute(
+        (below_sums.astype(jnp.bfloat16), below_stats), "row", row_down
+    )
+    above_sums = above_sums.astype(jnp.float32)
 
     head_outputs = []
     for head, (weights, (_, own_peak, own_total)) in enumerate(zip(own_weights, own_parts)):

time: 153 us -> 147 us (0.961)
  waiting for transfers between devices: 74.6 us -> 69.1 us
    ppermute x2, waiting for transfers between devices: 7 us -> 1.42 us  [body(): lax.ppermute((below_sums.astype(jnp.bfloat16), below_stats), 'row', row_d...]
  transfers between devices with their start and end apart: 6 -> 6, of which waited for: 4 -> 4; matrix products, arithmetic and copies ran while one was open for 22% -> 23% of each run, Pallas kernels for 0% -> 0%
where the time goes in v7:
time: 147 us; the launch traced here: 145 us
  waiting for transfers between devices  69.1 us (47%)
  matrix products  30.8 us (21%)
  between operations  14.5 us (10%)
  other arithmetic  14.1 us (10%)
  starting transfers between devices  13.2 us (9%)
  local copies, waits for them, and re-layouts  3.28 us (2%)
    all_gather x2, waiting for transfers between devices, row_gather(): gathered = lax.all_gather(array, ('col', 'core'), axis=0)  61.2 us
    dot_general x8, matrix products, weighted_part(): jnp.dot(weights, values_row[:, lanes], preferred_element_type=jnp.float32)  13.9 us
    reduce_sum x2, other arithmetic, softmax_part(): row_total = jnp.sum(exp_terms, axis=1, keepdims=True)  12.1 us
    dot_general x8, matrix products, softmax_part(): lax.dot_general(queries[:, lanes], keys_row[:, lanes], (((1,), (1,)), (()...  12 us
    ppermute x2, starting transfers between devices, body(): lax.ppermute((below_sums.astype(jnp.bfloat16), below_stats), 'row', row_d...  6.44 us
    ppermute x1, waiting for transfers between devices, body(): queries_below = lax.ppermute(query_rows, 'row', row_up)  5.72 us
    ppermute x1, starting transfers between devices, passed_along(): return lax.ppermute(block, axis, route)  5.39 us
    dot_general x2, matrix products, toeplitz_taps(): taps = jnp.dot(filters, picks, preferred_element_type=jnp.float32)  3.54 us
  transfers between devices with their start and end apart: 6, of which 4 were waited for; matrix products, arithmetic and copies ran while one was open for 23% of the time, Pallas kernels for 0%

profile of v7, /device:TPU:1, one launch (start us, length us, event | category | flops | bytes accessed | tf_op | source)
XLA Modules:
  0.0 145.0 jit_solution(17289138728972505569)
XLA Ops:
  8.0 1.1 multiply_convert_fusion
  9.1 5.4 %collective-permute-start = (bf16[127,512]{1,0:T(8,128)(2,1)S(1)}, bf16[127,512]{1,0:T(8,128)(2,1)S(1)}, u32[]{:S(2)}, u32[]{:S(2)}) collective-permute-start(bf16[127,512]{1,0:T(8,128)(2,1)S(1)} %slice.132), channel_id=1, source_target_pairs={{0,4},{4,8},{8,12},{12,16},{16,20},{20,24},{24,28},{28,32},{32,36}... | collective-permute-start | bytes 390152 | tf_op jit(solution)/shard_map/ppermute | solution.py:21
  14.7 1.8 %fusion.26 = bf16[4,8,128,128]{3,1,2,0:T(8,128)(2,1)S(1)} fusion(bf16[32,128]{1,0:T(8,128)(2,1)S(1)} %copy-done, s32[16384]{0:T(1024)S(1)} %subtract_bitcast_fusion), kind=kOutput, calls=%fused_computation.48 | convolution fusion | flops 136839168 | bytes 1122304 | tf_op jit(solution)/shard_map/dot_general | solution.py:30
  17.5 1.8 %fusion.27 = bf16[4,8,128,128]{3,1,2,0:T(8,128)(2,1)S(1)} fusion(bf16[32,128]{1,0:T(8,128)(2,1)S(1)} %copy-done, s32[16384]{0:T(1024)S(1)} %broadcast_add_fusion), kind=kOutput, calls=%fused_computation.49 | convolution fusion | flops 136839168 | bytes 1122304 | tf_op jit(solution)/shard_map/dot_general | solution.py:30
  21.0 0.8 fusion.52
  21.8 1.3 collective-permute-start.1
  23.2 5.7 %collective-permute-done.1 = bf16[256,512]{1,0:T(8,128)(2,1)S(1)} collective-permute-done((bf16[256,512]{1,0:T(8,128)(2,1)S(1)}, bf16[256,512]{1,0:T(8,128)(2,1)S(1)}, u32[]{:S(2)}, u32[]{:S(2)}) %collective-permute-start.1) | collective-permute-done | bytes 262176 | tf_op jit(solution)/shard_map/ppermute | solution.py:74
  28.9 32.8 %all-gather.5.cloned.1.call-done = bf16[4096,512]{1,0:T(8,128)(2,1)} async-done(((bf16[256,512]{1,0:T(8,128)(2,1)}), bf16[4096,512]{1,0:T(8,128)(2,1)}) %all-gather.5.cloned.1.call-update) | async-done | bytes 4194320 | tf_op jit(solution)/shard_map/all_gather | solution.py:69
  61.8 2.7 %fusion.104 = (f32[256]{0:T(256)S(1)}, f32[256,4096]{1,0:T(8,128)S(1)}) fusion(bf16[4096,512]{1,0:T(8,128)(2,1)} %all-gather.5.cloned.1.call-done, bf16[256,512]{1,0:T(8,128)(2,1)S(1)} %collective-permute-done.1, s32[256]{0:T(256)S(1)} %iota_add_fusion.2, s32[4096]{0:T(1024)S(1)} %iota_add_fusion, pred[4096]{0:T(1024)(128)(4,1)S(1)} %fusion.86), kind=kOutput, calls=%fused_computation.145 | convolution fusion | flops 273678080 | bytes 5330944 | tf_op jit(solution)/shard_map/dot_general | solution.py:88
  64.4 1.3 fusion.105
  65.8 1.3 fusion.106
  67.1 1.3 fusion.107
  68.4 6.3 %fusion.10 = (f32[256]{0:T(256)S(1)}, f32[256]{0:T(256)S(1)}, f32[256]{0:T(256)S(1)}, f32[256]{0:T(256)S(1)}, bf16[256,4096]{1,0:T(8,128)(2,1)}, /*index=5*/bf16...) fusion(f32[256,4096]{1,0:T(8,128)S(1)} %get-tuple-element.104, f32[256]{0:T(256)S(1)} %get-tuple-element.103, ...), kind=kLoop, calls=%fused_computation.32 | loop fusion | flops 18873344 | bytes 25195520 | tf_op jit(solution)/shard_map/reduce_sum | solution.py:99
  74.7 1.3 fusion.108
  76.0 1.3 fusion.109
  77.4 1.3 fusion.110
  78.7 1.3 fusion.111
  80.0 5.8 %fusion.24 = (f32[256]{0:T(256)S(1)}, f32[256]{0:T(256)S(1)}, f32[256]{0:T(256)S(1)}, f32[256]{0:T(256)S(1)}, bf16[256,4096]{1,0:T(8,128)(2,1)}, /*index=5*/bf16...) fusion(f32[256,4096]{1,0:T(8,128)S(1)} %get-tuple-element.112, ...), kind=kLoop, calls=%fused_computation.46 | loop fusion | flops 18873344 | bytes 25195520 | tf_op jit(solution)/shard_map/reduce_sum | solution.py:99
  85.9 28.4 %all-gather.7.cloned.1.call-done = bf16[4096,512]{0,1:T(8,128)(2,1)} async-done(((bf16[256,512]{0,1:T(8,128)(2,1)}), bf16[4096,512]{0,1:T(8,128)(2,1)}) %all-gather.7.cloned.1.call-update) | async-done | bytes 4194320 | tf_op jit(solution)/shard_map/all_gather | solution.py:69
  114.3 2.8 %fusion.33 = bf16[256,128]{0,1:T(8,128)(2,1)S(1)} fusion(bf16[256,4096]{1,0:T(8,128)(2,1)} %get-tuple-element.35, bf16[4096,512]{0,1:T(8,128)(2,1)} %all-gather.7.cloned.1.call-done), kind=kOutput, calls=%fused_computation.60 | convolution fusion | flops 268435456 | bytes 3211264 | tf_op jit(solution)/shard_map/dot_general | solution.py:104
  117.1 2.8 %fusion.38 = bf16[256,128]{0,1:T(8,128)(2,1)S(1)} fusion(bf16[256,4096]{1,0:T(8,128)(2,1)} %get-tuple-element.34, bf16[4096,512]{0,1:T(8,128)(2,1)} %all-gather.7.cloned.1.call-done), kind=kOutput, calls=%fused_computation.65 | convolution fusion | flops 268435456 | bytes 3211264 | tf_op jit(solution)/shard_map/dot_general | solution.py:104
  120.0 0.8 fusion.43
  120.9 0.8 fusion.48
  121.7 3.1 %collective-permute-start.3 = (bf16[256,512]{0,1:T(8,128)(2,1)S(1)}, bf16[256,512]{0,1:T(8,128)(2,1)S(1)}, u32[]{:S(2)}, u32[]{:S(2)}) collective-permute-start(bf16[256,512]{0,1:T(8,128)(2,1)S(1)} %pad_maximum_fusion), channel_id=1, source_target_pairs={{0,64},{64,128},{128,192},{192,256},{256,320},{320,384},{384,448},... | collective-permute-start | bytes 786440 | tf_op jit(solution)/shard_map/ppermute | solution.py:117
  124.9 3.3 %collective-permute-start.2 = (f32[256,8]{0,1:T(8,128)S(1)}, f32[256,8]{0,1:T(8,128)S(1)}, u32[]{:S(2)}, u32[]{:S(2)}) collective-permute-start(f32[256,8]{0,1:T(8,128)S(1)} %concatenate.18), channel_id=1, source_target_pairs={{0,64},{64,128},{128,192},{192,256},{256,320},{320,384},{384,448},... | collective-permute-start | bytes 24584 | tf_op jit(solution)/shard_map/ppermute | solution.py:117
  128.2 0.8 copy.18
  129.0 1.4 collective-permute-done.2
  130.6 2.8 %fusion.68 = bf16[256,128]{0,1:T(8,128)(2,1)S(1)} fusion(f32[256,512]{0,1:T(8,128)S(1)} %convert_element_type.89, f32[256]{0:T(256)S(1)} %bitcast.104, f32[256]{0:T(256)S(1)} %bitcast.105, f32[256]{0:T(256)S(1)} %bitcast.106, bf16[256,4096]{1,0:T(8,128)(2,1)} %get-tuple-element.59, bf16[4096,512]{0,1:T(8,128)(2,1)} %all-gather.7.cloned.1.call-done), kind=kOutput, calls=%fused_computation.103 | convolution fusion | flops 268599296 | bytes 3345408 | tf_op jit(solution)/shard_map/dot_general | solution.py:104
  133.4 2.1 %fusion.67 = bf16[256,128]{0,1:T(8,128)(2,1)S(1)} fusion(f32[256,512]{0,1:T(8,128)S(1)} %convert_element_type.89, f32[256]{0:T(256)S(1)} %bitcast.101, f32[256]{0:T(256)S(1)} %bitcast.102, f32[256]{0:T(256)S(1)} %bitcast.103, bf16[256,4096]{1,0:T(8,128)(2,1)S(1)} %copy-done.4, bf16[4096,512]{0,1:T(8,128)(2,1)} %all-gather.7.cloned.1.call-done), kind=kOutput, calls=%fused_computation.102 | convolution fusion | flops 268599296 | bytes 3345408 | tf_op jit(solution)/shard_map/dot_general | solution.py:104
  135.5 0.8 fusion.66
  136.4 0.8 fusion.65
  137.3 0.8 copy.19
  (56 shorter events, 3.8 us)
Async XLA Ops:
  7.2 7.5 %copy-start = (bf16[32,128]{1,0:T(8,128)(2,1)S(1)}, bf16[32,128]{1,0:T(8,128)(2,1)}, u32[]{:S(2)}) copy-start(bf16[32,128]{1,0:T(8,128)(2,1)} %param.9) | copy-start | bytes 24580
  7.2 54.6 %all-gather.5.cloned.1.call-start = ((), (), s32[]{:S(2)}) async-start(), calls=%async_computation | async-start | bytes 4456448 | tf_op jit(solution)/shard_map/all_gather | solution.py:69
  7.9 106.4 %all-gather.7.cloned.1.call-start = ((), (), s32[]{:S(2)}) async-start(), calls=%async_computation.1 | async-start | bytes 4456448 | tf_op jit(solution)/shard_map/all_gather | solution.py:69
  9.1 10.7 %collective-permute-start = (bf16[127,512]{1,0:T(8,128)(2,1)S(1)}, bf16[127,512]{1,0:T(8,128)(2,1)S(1)}, u32[]{:S(2)}, u32[]{:S(2)}) collective-permute-start(bf16[127,512]{1,0:T(8,128)(2,1)S(1)} %slice.132), channel_id=1, source_target_pairs={{0,4},{4,8},{8,12},{12,16},{16,20},{20,24},{24,28},{28,32},{32,36}... | collective-permute-start | bytes 390152 | tf_op jit(solution)/shard_map/ppermute | solution.py:21
  16.7 2.9 %copy-start.7 = (bf16[256,512]{1,0:T(8,128)(2,1)S(1)}, bf16[256,512]{1,0:T(8,128)(2,1)}, u32[]{:S(2)}) copy-start(bf16[256,512]{1,0:T(8,128)(2,1)} %param.6) | copy-start | bytes 786436
  19.2 2.6 %copy-start.11 = (bf16[256,512]{1,0:T(8,128)(2,1)S(1)}, bf16[256,512]{1,0:T(8,128)(2,1)}, u32[]{:S(2)}) copy-start(bf16[256,512]{1,0:T(8,128)(2,1)} %param.10) | copy-start | bytes 786436
  21.8 7.1 %collective-permute-start.1 = (bf16[256,512]{1,0:T(8,128)(2,1)S(1)}, bf16[256,512]{1,0:T(8,128)(2,1)S(1)}, u32[]{:S(2)}, u32[]{:S(2)}) collective-permute-start(bf16[256,512]{1,0:T(8,128)(2,1)S(1)} %copy-done.11), channel_id=1, source_target_pairs={{64,0},{128,64},{192,128},{256,192},{320,256},{384,320},{448,384},... | collective-permute-start | bytes 786440 | tf_op jit(solution)/shard_map/ppermute | solution.py:74
  61.8 2.7 %copy-start.8 = (bf16[4096,512]{1,0:T(8,128)(2,1)S(1)}, bf16[4096,512]{1,0:T(8,128)(2,1)}, u32[]{:S(2)}) copy-start(bf16[4096,512]{1,0:T(8,128)(2,1)} %all-gather.5.cloned.1.call-done) | copy-start | bytes 12582916
  114.3 5.7 %copy-start.6 = (bf16[256,4096]{1,0:T(8,128)(2,1)S(1)}, bf16[256,4096]{1,0:T(8,128)(2,1)}, u32[]{:S(2)}) copy-start(bf16[256,4096]{1,0:T(8,128)(2,1)} %get-tuple-element.33) | copy-start | bytes 6291460
  114.3 5.7 %copy-start.9 = (bf16[4096,512]{0,1:T(8,128)(2,1)S(1)}, bf16[4096,512]{0,1:T(8,128)(2,1)}, u32[]{:S(2)}) copy-start(bf16[4096,512]{0,1:T(8,128)(2,1)} %all-gather.7.cloned.1.call-done) | copy-start | bytes 12582916
  117.1 3.7 %copy-start.5 = (bf16[256,4096]{1,0:T(8,128)(2,1)S(1)}, bf16[256,4096]{1,0:T(8,128)(2,1)}, u32[]{:S(2)}) copy-start(bf16[256,4096]{1,0:T(8,128)(2,1)} %get-tuple-element.32) | copy-start | bytes 6291460
  120.0 8.2 %copy-start.2 = (bf16[256,512]{0,1:T(8,128)(2,1)S(1)}, bf16[256,512]{0,1:T(8,128)(2,1)}, u32[]{:S(2)}) copy-start(bf16[256,512]{0,1:T(8,128)(2,1)} %fusion.52) | copy-start | bytes 786436
  121.7 8.8 %collective-permute-start.3 = (bf16[256,512]{0,1:T(8,128)(2,1)S(1)}, bf16[256,512]{0,1:T(8,128)(2,1)S(1)}, u32[]{:S(2)}, u32[]{:S(2)}) collective-permute-start(bf16[256,512]{0,1:T(8,128)(2,1)S(1)} %pad_maximum_fusion), channel_id=1, source_target_pairs={{0,64},{64,128},{128,192},{192,256},{256,320},{320,384},{384,448},... | collective-permute-start | bytes 786440 | tf_op jit(solution)/shard_map/ppermute | solution.py:117
  124.9 5.6 %collective-permute-start.2 = (f32[256,8]{0,1:T(8,128)S(1)}, f32[256,8]{0,1:T(8,128)S(1)}, u32[]{:S(2)}, u32[]{:S(2)}) collective-permute-start(f32[256,8]{0,1:T(8,128)S(1)} %concatenate.18), channel_id=1, source_target_pairs={{0,64},{64,128},{128,192},{192,256},{256,320},{320,384},{384,448},... | collective-permute-start | bytes 24584 | tf_op jit(solution)/shard_map/ppermute | solution.py:117
  129.0 4.4 %copy-start.4 = (bf16[256,4096]{1,0:T(8,128)(2,1)S(1)}, bf16[256,4096]{1,0:T(8,128)(2,1)}, u32[]{:S(2)}) copy-start(bf16[256,4096]{1,0:T(8,128)(2,1)} %get-tuple-element.56) | copy-start | bytes 6291460
  130.5 5.0 %copy-start.3 = (bf16[256,4096]{1,0:T(8,128)(2,1)S(1)}, bf16[256,4096]{1,0:T(8,128)(2,1)}, u32[]{:S(2)}) copy-start(bf16[256,4096]{1,0:T(8,128)(2,1)} %get-tuple-element.53) | copy-start | bytes 6291460
  130.6 5.0 %copy-start.10 = (bf16[4096,512]{0,1:T(8,128)(2,1)S(1)}, bf16[4096,512]{0,1:T(8,128)(2,1)}, u32[]{:S(2)}) copy-start(bf16[4096,512]{0,1:T(8,128)(2,1)} %all-gather.7.cloned.1.call-done) | copy-start | bytes 12582916
  135.5 2.6 %copy-start.1 = (bf16[32,128]{1,0:T(8,128)(2,1)S(1)}, bf16[32,128]{1,0:T(8,128)(2,1)}, u32[]{:S(2)}) copy-start(bf16[32,128]{1,0:T(8,128)(2,1)} %param.9) | copy-start | bytes 24580
Sparse Core Ops, SparseCore 0:
  10.1 51.5 all-gather.4
  64.4 49.8 all-gather.6

commit v8 on v4

--- a/solution.py
+++ b/solution.py
@@ -104,17 +104,26 @@
         return jnp.dot(weights, values_row[:, lanes], preferred_element_type=jnp.float32)
 
     below_parts = [softmax_part(queries_below, visible_below, head) for head in range(local_heads)]
+    above_stats = lax.ppermute(
+        jnp.concatenate(
+            [jnp.concatenate([peak, total], axis=1) for _, peak, total in below_parts], axis=1
+        ),
+        "row",
+        row_down,
+    )
     own_parts = [softmax_part(query_rows, visible_own, head) for head in range(local_heads)]
+    values_row, above_stats = lax.optimization_barrier((values_row, above_stats))
     below_sums = jnp.concatenate(
         [weighted_part(weights, head) for head, (weights, _, _) in enumerate(below_parts)], axis=1
     )
-    below_stats = jnp.concatenate(
-        [jnp.concatenate([peak, total], axis=1) for _, peak, total in below_parts], axis=1
+    below_sums, own_weights = lax.optimization_barrier(
+        (below_sums, [weights for weights, _, _ in own_parts])
     )
-    above_sums, above_stats = lax.ppermute((below_sums, below_stats), "row", row_down)
+    above_sums = lax.ppermute(below_sums.astype(jnp.bfloat16), "row", row_down)
+    above_sums = above_sums.astype(jnp.float32)
 
     head_outputs = []
-    for head, (weights, own_peak, own_total) in enumerate(own_parts):
+    for head, (weights, (_, own_peak, own_total)) in enumerate(zip(own_weights, own_parts)):
         own_sum = weighted_part(weights, head)
         lanes = slice(head * HEAD_DIM, (head + 1) * HEAD_DIM)
         above_total = above_stats[:, 2 * head + 1 : 2 * head + 2]

time: 154 us -> 146 us (0.948)
  matrix products: 41.3 us -> 32.1 us
  waiting for transfers between devices: 64.5 us -> 67.4 us
    dot_general x8, matrix products: 20.7 us -> 13.2 us  [softmax_part(): lax.dot_general(queries[:, lanes], keys_row[:, lanes], (((1,), (1,)), (()...]
    ppermute x1, waiting for transfers between devices: 3.74 us -> 5.54 us  [body(): queries_below = lax.ppermute(query_rows, 'row', row_up)]
    dot_general x8, matrix products: 15.7 us -> 14 us  [weighted_part(): jnp.dot(weights, values_row[:, lanes], preferred_element_type=jnp.float32)]
    unnamed x28 -> x32, local copies, waits for them, and re-layouts: 3.44 us -> 2.5 us
  transfers between devices with their start and end apart: 6 -> 6, of which waited for: 4 -> 4; matrix products, arithmetic and copies ran while one was open for 35% -> 24% of each run, Pallas kernels for 0% -> 0%
where the time goes in v8:
time: 146 us; the launch traced here: 145 us
  waiting for transfers between devices  67.4 us (46%)
  matrix products  32.1 us (22%)
  between operations  14.5 us (10%)
  other arithmetic  13.9 us (10%)
  starting transfers between devices  13.6 us (9%)
  local copies, waits for them, and re-layouts  3.28 us (2%)
    all_gather x2, waiting for transfers between devices, row_gather(): gathered = lax.all_gather(array, ('col', 'core'), axis=0)  56.6 us
    dot_general x8, matrix products, weighted_part(): jnp.dot(weights, values_row[:, lanes], preferred_element_type=jnp.float32)  14 us
    dot_general x8, matrix products, softmax_part(): lax.dot_general(queries[:, lanes], keys_row[:, lanes], (((1,), (1,)), (()...  13.2 us
    reduce_sum x2, other arithmetic, softmax_part(): row_total = jnp.sum(exp_terms, axis=1, keepdims=True)  11.9 us
    ppermute x1, waiting for transfers between devices, body(): queries_below = lax.ppermute(query_rows, 'row', row_up)  5.54 us
    ppermute x1, starting transfers between devices, passed_along(): return lax.ppermute(block, axis, route)  5.39 us
    ppermute x1, waiting for transfers between devices, body(): above_sums = lax.ppermute(below_sums.astype(jnp.bfloat16), 'row', row_down)  4.53 us
    ppermute x1, starting transfers between devices, body(): lax.ppermute(jnp.concatenate([jnp.concatenate([peak, total], axis=1) for...  3.59 us
  transfers between devices with their start and end apart: 6, of which 4 were waited for; matrix products, arithmetic and copies ran while one was open for 24% of the time, Pallas kernels for 0%

profile of v8, /device:TPU:1, one launch (start us, length us, event | category | flops | bytes accessed | tf_op | source)
XLA Modules:
  0.0 144.8 jit_solution(12818379989420335885)
XLA Ops:
  8.0 1.1 multiply_convert_fusion
  9.1 5.4 %collective-permute-start = (bf16[127,512]{1,0:T(8,128)(2,1)S(1)}, bf16[127,512]{1,0:T(8,128)(2,1)S(1)}, u32[]{:S(2)}, u32[]{:S(2)}) collective-permute-start(bf16[127,512]{1,0:T(8,128)(2,1)S(1)} %slice.132), channel_id=1, source_target_pairs={{0,4},{4,8},{8,12},{12,16},{16,20},{20,24},{24,28},{28,32},{32,36}... | collective-permute-start | bytes 390152 | tf_op jit(solution)/shard_map/ppermute | solution.py:21
  14.7 1.8 %fusion.26 = bf16[4,8,128,128]{3,1,2,0:T(8,128)(2,1)S(1)} fusion(bf16[32,128]{1,0:T(8,128)(2,1)S(1)} %copy-done, s32[16384]{0:T(1024)S(1)} %subtract_bitcast_fusion), kind=kOutput, calls=%fused_computation.48 | convolution fusion | flops 136839168 | bytes 1122304 | tf_op jit(solution)/shard_map/dot_general | solution.py:30
  17.5 1.8 %fusion.27 = bf16[4,8,128,128]{3,1,2,0:T(8,128)(2,1)S(1)} fusion(bf16[32,128]{1,0:T(8,128)(2,1)S(1)} %copy-done, s32[16384]{0:T(1024)S(1)} %broadcast_add_fusion), kind=kOutput, calls=%fused_computation.49 | convolution fusion | flops 136839168 | bytes 1122304 | tf_op jit(solution)/shard_map/dot_general | solution.py:30
  21.0 0.8 fusion.64
  21.8 1.5 %collective-permute-start.1 = (bf16[256,512]{1,0:T(8,128)(2,1)S(1)}, bf16[256,512]{1,0:T(8,128)(2,1)S(1)}, u32[]{:S(2)}, u32[]{:S(2)}) collective-permute-start(bf16[256,512]{1,0:T(8,128)(2,1)S(1)} %copy-done.12), channel_id=1, source_target_pairs={{64,0},{128,64},{192,128},{256,192},{320,256},{384,320},{448,384},... | collective-permute-start | bytes 786440 | tf_op jit(solution)/shard_map/ppermute | solution.py:74
  23.4 5.5 %collective-permute-done.1 = bf16[256,512]{1,0:T(8,128)(2,1)S(1)} collective-permute-done((bf16[256,512]{1,0:T(8,128)(2,1)S(1)}, bf16[256,512]{1,0:T(8,128)(2,1)S(1)}, u32[]{:S(2)}, u32[]{:S(2)}) %collective-permute-start.1) | collective-permute-done | bytes 262176 | tf_op jit(solution)/shard_map/ppermute | solution.py:74
  28.9 32.8 %all-gather.5.cloned.1.call-done = bf16[4096,512]{1,0:T(8,128)(2,1)} async-done(((bf16[256,512]{1,0:T(8,128)(2,1)}), bf16[4096,512]{1,0:T(8,128)(2,1)}) %all-gather.5.cloned.1.call-update) | async-done | bytes 4194320 | tf_op jit(solution)/shard_map/all_gather | solution.py:69
  61.8 2.7 %fusion.96 = (f32[256]{0:T(256)S(1)}, f32[256,4096]{1,0:T(8,128)S(1)}) fusion(bf16[4096,512]{1,0:T(8,128)(2,1)} %all-gather.5.cloned.1.call-done, bf16[256,512]{1,0:T(8,128)(2,1)S(1)} %collective-permute-done.1, s32[256]{0:T(256)S(1)} %iota_add_fusion.2, s32[4096]{0:T(1024)S(1)} %iota_add_fusion, pred[4096]{0:T(1024)(128)(4,1)S(1)} %fusion.78), kind=kOutput, calls=%fused_computation.145 | convolution fusion | flops 273678080 | bytes 5330944 | tf_op jit(solution)/shard_map/dot_general | solution.py:88
  64.4 1.3 fusion.97
  65.8 1.3 fusion.98
  67.1 1.3 fusion.99
  68.4 6.1 %fusion.14 = (f32[256]{0:T(256)S(1)}, f32[256]{0:T(256)S(1)}, f32[256]{0:T(256)S(1)}, f32[256]{0:T(256)S(1)}, bf16[256,4096]{1,0:T(8,128)(2,1)}, /*index=5*/bf16...) fusion(f32[256,4096]{1,0:T(8,128)S(1)} %get-tuple-element.106, f32[256]{0:T(256)S(1)} %get-tuple-element.105, ...), kind=kLoop, calls=%fused_computation.36 | loop fusion | flops 18873344 | bytes 25195520 | tf_op jit(solution)/shard_map/reduce_sum | solution.py:99
  74.6 3.6 %collective-permute-start.2 = (f32[256,8]{0,1:T(8,128)S(1)}, f32[256,8]{0,1:T(8,128)S(1)}, u32[]{:S(2)}, u32[]{:S(2)}) collective-permute-start(f32[256,8]{0,1:T(8,128)S(1)} %concatenate.17), channel_id=1, source_target_pairs={{0,64},{64,128},{128,192},{192,256},{256,320},{320,384},{384,448},... | collective-permute-start | bytes 24584 | tf_op jit(solution)/shard_map/ppermute | solution.py:107
  78.2 2.5 %fusion.100 = (f32[256]{0:T(256)S(1)}, f32[256,4096]{1,0:T(8,128)S(1)}) fusion(bf16[4096,512]{1,0:T(8,128)(2,1)} %all-gather.5.cloned.1.call-done, bf16[256,512]{1,0:T(8,128)(2,1)S(1)} %copy-done.12, s32[256]{0:T(256)S(1)} %iota_add_fusion.1, s32[4096]{0:T(1024)S(1)} %iota_add_fusion, pred[4096]{0:T(1024)(128)(4,1)S(1)} %fusion.77), kind=kOutput, calls=%fused_computation.149 | convolution fusion | flops 273678080 | bytes 5330944 | tf_op jit(solution)/shard_map/dot_general | solution.py:88
  80.7 1.3 fusion.101
  82.0 1.3 fusion.102
  83.4 1.3 fusion.103
  84.7 5.8 %fusion.24 = (f32[256]{0:T(256)S(1)}, f32[256]{0:T(256)S(1)}, f32[256]{0:T(256)S(1)}, f32[256]{0:T(256)S(1)}, bf16[256,4096]{1,0:T(8,128)(2,1)}, /*index=5*/bf16...) fusion(f32[256,4096]{1,0:T(8,128)S(1)} %get-tuple-element.114, ...), kind=kLoop, calls=%fused_computation.46 | loop fusion | flops 18873344 | bytes 25195520 | tf_op jit(solution)/shard_map/reduce_sum | solution.py:99
  90.5 23.8 %all-gather.7.cloned.1.call-done = bf16[4096,512]{0,1:T(8,128)(2,1)} async-done(((bf16[256,512]{0,1:T(8,128)(2,1)}), bf16[4096,512]{0,1:T(8,128)(2,1)}) %all-gather.7.cloned.1.call-update) | async-done | bytes 4194320 | tf_op jit(solution)/shard_map/all_gather | solution.py:69
  114.3 2.8 %fusion.53 = bf16[256,128]{0,1:T(8,128)(2,1)S(1)} fusion(bf16[256,4096]{1,0:T(8,128)(2,1)} %get-tuple-element.45, bf16[4096,512]{0,1:T(8,128)(2,1)} %all-gather.7.cloned.1.call-done), kind=kOutput, calls=%fused_computation.80 | convolution fusion | flops 268435456 | bytes 3211264 | tf_op jit(solution)/shard_map/dot_general | solution.py:104
  117.2 2.8 %fusion.56 = bf16[256,128]{0,1:T(8,128)(2,1)S(1)} fusion(bf16[256,4096]{1,0:T(8,128)(2,1)} %get-tuple-element.44, bf16[4096,512]{0,1:T(8,128)(2,1)} %all-gather.7.cloned.1.call-done), kind=kOutput, calls=%fused_computation.83 | convolution fusion | flops 268435456 | bytes 3211264 | tf_op jit(solution)/shard_map/dot_general | solution.py:104
  120.0 0.8 fusion.59
  120.9 0.8 fusion.62
  121.8 3.1 %collective-permute-start.3 = (bf16[256,512]{0,1:T(8,128)(2,1)S(1)}, bf16[256,512]{0,1:T(8,128)(2,1)S(1)}, u32[]{:S(2)}, u32[]{:S(2)}) collective-permute-start(bf16[256,512]{0,1:T(8,128)(2,1)S(1)} %pad_maximum_fusion), channel_id=1, source_target_pairs={{0,64},{64,128},{128,192},{192,256},{256,320},{320,384},{384,448},... | collective-permute-start | bytes 786440 | tf_op jit(solution)/shard_map/ppermute | solution.py:122
  124.9 0.8 copy.18
  125.8 4.5 %collective-permute-done.3 = bf16[256,512]{0,1:T(8,128)(2,1)S(1)} collective-permute-done((bf16[256,512]{0,1:T(8,128)(2,1)S(1)}, bf16[256,512]{0,1:T(8,128)(2,1)S(1)}, u32[]{:S(2)}, u32[]{:S(2)}) %collective-permute-start.3) | collective-permute-done | bytes 262176 | tf_op jit(solution)/shard_map/ppermute | solution.py:122
  130.4 2.8 %fusion.40 = bf16[256,128]{0,1:T(8,128)(2,1)S(1)} fusion(bf16[256,4096]{1,0:T(8,128)(2,1)} %get-tuple-element.61, bf16[4096,512]{0,1:T(8,128)(2,1)} %all-gather.7.cloned.1.call-done, f32[256,512]{0,1:T(8,128)S(1)} %convert_element_type.89, f32[256]{0:T(256)S(1)} %bitcast.104, f32[256]{0:T(256)S(1)} %bitcast.105, f32[256]{0:T(256)S(1)} %bitcast.106), kind=kOutput, calls=%fused_computation.67 | convolution fusion | flops 268599296 | bytes 3345408 | tf_op jit(solution)/shard_map/dot_general | solution.py:104
  133.2 2.1 %fusion.39 = bf16[256,128]{0,1:T(8,128)(2,1)S(1)} fusion(bf16[256,4096]{1,0:T(8,128)(2,1)S(1)} %copy-done.4, bf16[4096,512]{0,1:T(8,128)(2,1)} %all-gather.7.cloned.1.call-done, f32[256,512]{0,1:T(8,128)S(1)} %convert_element_type.89, f32[256]{0:T(256)S(1)} %bitcast.101, f32[256]{0:T(256)S(1)} %bitcast.102, f32[256]{0:T(256)S(1)} %bitcast.103), kind=kOutput, calls=%fused_computation.66 | convolution fusion | flops 268599296 | bytes 3345408 | tf_op jit(solution)/shard_map/dot_general | solution.py:104
  135.3 0.9 fusion.38
  136.2 0.9 fusion.37
  137.1 0.8 copy.19
  (58 shorter events, 3.8 us)
Async XLA Ops:
  7.2 7.5 %copy-start = (bf16[32,128]{1,0:T(8,128)(2,1)S(1)}, bf16[32,128]{1,0:T(8,128)(2,1)}, u32[]{:S(2)}) copy-start(bf16[32,128]{1,0:T(8,128)(2,1)} %param.9) | copy-start | bytes 24580
  7.2 54.6 %all-gather.5.cloned.1.call-start = ((), (), s32[]{:S(2)}) async-start(), calls=%async_computation | async-start | bytes 4456448 | tf_op jit(solution)/shard_map/all_gather | solution.py:69
  7.9 106.4 %all-gather.7.cloned.1.call-start = ((), (), s32[]{:S(2)}) async-start(), calls=%async_computation.1 | async-start | bytes 4456448 | tf_op jit(solution)/shard_map/all_gather | solution.py:69
  9.1 10.7 %collective-permute-start = (bf16[127,512]{1,0:T(8,128)(2,1)S(1)}, bf16[127,512]{1,0:T(8,128)(2,1)S(1)}, u32[]{:S(2)}, u32[]{:S(2)}) collective-permute-start(bf16[127,512]{1,0:T(8,128)(2,1)S(1)} %slice.132), channel_id=1, source_target_pairs={{0,4},{4,8},{8,12},{12,16},{16,20},{20,24},{24,28},{28,32},{32,36}... | collective-permute-start | bytes 390152 | tf_op jit(solution)/shard_map/ppermute | solution.py:21
  16.7 2.9 %copy-start.7 = (bf16[256,512]{1,0:T(8,128)(2,1)S(1)}, bf16[256,512]{1,0:T(8,128)(2,1)}, u32[]{:S(2)}) copy-start(bf16[256,512]{1,0:T(8,128)(2,1)} %param.6) | copy-start | bytes 786436
  19.2 2.6 %copy-start.12 = (bf16[256,512]{1,0:T(8,128)(2,1)S(1)}, bf16[256,512]{1,0:T(8,128)(2,1)}, u32[]{:S(2)}) copy-start(bf16[256,512]{1,0:T(8,128)(2,1)} %param.10) | copy-start | bytes 786436
  21.8 7.1 %collective-permute-start.1 = (bf16[256,512]{1,0:T(8,128)(2,1)S(1)}, bf16[256,512]{1,0:T(8,128)(2,1)S(1)}, u32[]{:S(2)}, u32[]{:S(2)}) collective-permute-start(bf16[256,512]{1,0:T(8,128)(2,1)S(1)} %copy-done.12), channel_id=1, source_target_pairs={{64,0},{128,64},{192,128},{256,192},{320,256},{384,320},{448,384},... | collective-permute-start | bytes 786440 | tf_op jit(solution)/shard_map/ppermute | solution.py:74
  61.8 2.7 %copy-start.8 = (bf16[4096,512]{1,0:T(8,128)(2,1)S(1)}, bf16[4096,512]{1,0:T(8,128)(2,1)}, u32[]{:S(2)}) copy-start(bf16[4096,512]{1,0:T(8,128)(2,1)} %all-gather.5.cloned.1.call-done) | copy-start | bytes 12582916
  74.6 6.1 %copy-start.9 = (bf16[4096,512]{1,0:T(8,128)(2,1)S(1)}, bf16[4096,512]{1,0:T(8,128)(2,1)}, u32[]{:S(2)}) copy-start(bf16[4096,512]{1,0:T(8,128)(2,1)} %all-gather.5.cloned.1.call-done) | copy-start | bytes 12582916
  74.6 16.0 %collective-permute-start.2 = (f32[256,8]{0,1:T(8,128)S(1)}, f32[256,8]{0,1:T(8,128)S(1)}, u32[]{:S(2)}, u32[]{:S(2)}) collective-permute-start(f32[256,8]{0,1:T(8,128)S(1)} %concatenate.17), channel_id=1, source_target_pairs={{0,64},{64,128},{128,192},{192,256},{256,320},{320,384},{384,448},... | collective-permute-start | bytes 24584 | tf_op jit(solution)/shard_map/ppermute | solution.py:107
  114.3 5.7 %copy-start.6 = (bf16[256,4096]{1,0:T(8,128)(2,1)S(1)}, bf16[256,4096]{1,0:T(8,128)(2,1)}, u32[]{:S(2)}) copy-start(bf16[256,4096]{1,0:T(8,128)(2,1)} %get-tuple-element.43) | copy-start | bytes 6291460
  114.3 5.7 %copy-start.10 = (bf16[4096,512]{0,1:T(8,128)(2,1)S(1)}, bf16[4096,512]{0,1:T(8,128)(2,1)}, u32[]{:S(2)}) copy-start(bf16[4096,512]{0,1:T(8,128)(2,1)} %all-gather.7.cloned.1.call-done) | copy-start | bytes 12582916
  117.2 3.7 %copy-start.5 = (bf16[256,4096]{1,0:T(8,128)(2,1)S(1)}, bf16[256,4096]{1,0:T(8,128)(2,1)}, u32[]{:S(2)}) copy-start(bf16[256,4096]{1,0:T(8,128)(2,1)} %get-tuple-element.33) | copy-start | bytes 6291460
  120.0 4.9 %copy-start.2 = (bf16[256,512]{0,1:T(8,128)(2,1)S(1)}, bf16[256,512]{0,1:T(8,128)(2,1)}, u32[]{:S(2)}) copy-start(bf16[256,512]{0,1:T(8,128)(2,1)} %fusion.64) | copy-start | bytes 786436
  121.8 8.5 %collective-permute-start.3 = (bf16[256,512]{0,1:T(8,128)(2,1)S(1)}, bf16[256,512]{0,1:T(8,128)(2,1)S(1)}, u32[]{:S(2)}, u32[]{:S(2)}) collective-permute-start(bf16[256,512]{0,1:T(8,128)(2,1)S(1)} %pad_maximum_fusion), channel_id=1, source_target_pairs={{0,64},{64,128},{128,192},{192,256},{256,320},{320,384},{384,448},... | collective-permute-start | bytes 786440 | tf_op jit(solution)/shard_map/ppermute | solution.py:122
  125.7 7.5 %copy-start.4 = (bf16[256,4096]{1,0:T(8,128)(2,1)S(1)}, bf16[256,4096]{1,0:T(8,128)(2,1)}, u32[]{:S(2)}) copy-start(bf16[256,4096]{1,0:T(8,128)(2,1)} %get-tuple-element.58) | copy-start | bytes 6291460
  130.3 5.0 %copy-start.3 = (bf16[256,4096]{1,0:T(8,128)(2,1)S(1)}, bf16[256,4096]{1,0:T(8,128)(2,1)}, u32[]{:S(2)}) copy-start(bf16[256,4096]{1,0:T(8,128)(2,1)} %get-tuple-element.55) | copy-start | bytes 6291460
  130.3 5.0 %copy-start.11 = (bf16[4096,512]{0,1:T(8,128)(2,1)S(1)}, bf16[4096,512]{0,1:T(8,128)(2,1)}, u32[]{:S(2)}) copy-start(bf16[4096,512]{0,1:T(8,128)(2,1)} %all-gather.7.cloned.1.call-done) | copy-start | bytes 12582916
  135.3 2.7 %copy-start.1 = (bf16[32,128]{1,0:T(8,128)(2,1)S(1)}, bf16[32,128]{1,0:T(8,128)(2,1)}, u32[]{:S(2)}) copy-start(bf16[32,128]{1,0:T(8,128)(2,1)} %param.9) | copy-start | bytes 24580
Sparse Core Ops, SparseCore 0:
  10.1 51.5 all-gather.4
  64.4 49.8 all-gather.6

commit v9 on v8

--- a/solution.py
+++ b/solution.py
@@ -122,9 +122,10 @@
     above_sums = lax.ppermute(below_sums.astype(jnp.bfloat16), "row", row_down)
     above_sums = above_sums.astype(jnp.float32)
 
+    own_sums = [weighted_part(weights, head) for head, weights in enumerate(own_weights)]
+    above_sums, own_sums = lax.optimization_barrier((above_sums, own_sums))
     head_outputs = []
-    for head, (weights, (_, own_peak, own_total)) in enumerate(zip(own_weights, own_parts)):
-        own_sum = weighted_part(weights, head)
+    for head, (own_sum, (_, own_peak, own_total)) in enumerate(zip(own_sums, own_parts)):
         lanes = slice(head * HEAD_DIM, (head + 1) * HEAD_DIM)
         above_total = above_stats[:, 2 * head + 1 : 2 * head + 2]
         above_peak = jnp.where(

time: 146 us -> 140 us (0.959)
  waiting for transfers between devices: 67.4 us -> 62.5 us
  matrix products: 32.1 us -> 28.1 us
  local copies, waits for them, and re-layouts: 3.28 us -> 4.75 us
    dot_general x8, matrix products: 14 us -> 10 us  [weighted_part(): jnp.dot(weights, values_row[:, lanes], preferred_element_type=jnp.float32)]
    ppermute x1, waiting for transfers between devices: 4.53 us -> 2.08 us  [body(): above_sums = lax.ppermute(below_sums.astype(jnp.bfloat16), 'row', row_down)]
    ppermute x1, waiting for transfers between devices: 5.54 us -> 3.74 us  [body(): queries_below = lax.ppermute(query_rows, 'row', row_up)]
    unnamed x32 -> x30, local copies, waits for them, and re-layouts: 2.5 us -> 3.59 us
  transfers between devices with their start and end apart: 6 -> 6, of which waited for: 4 -> 4; matrix products, arithmetic and copies ran while one was open for 24% -> 28% of each run, Pallas kernels for 0% -> 0%
where the time goes in v9:
time: 140 us; the launch traced here: 139 us
  waiting for transfers between devices  62.5 us (45%)
  matrix products  28.1 us (20%)
  other arithmetic  14.7 us (10%)
  between operations  14.5 us (10%)
  starting transfers between devices  14 us (10%)
  local copies, waits for them, and re-layouts  4.75 us (3%)
    all_gather x2, waiting for transfers between devices, row_gather(): gathered = lax.all_gather(array, ('col', 'core'), axis=0)  56 us
    dot_general x8, matrix products, softmax_part(): lax.dot_general(queries[:, lanes], keys_row[:, lanes], (((1,), (1,)), (()...  13.2 us
    reduce_sum x2, other arithmetic, softmax_part(): row_total = jnp.sum(exp_terms, axis=1, keepdims=True)  12.5 us
    dot_general x8, matrix products, weighted_part(): jnp.dot(weights, values_row[:, lanes], preferred_element_type=jnp.float32)  10 us
    ppermute x1, starting transfers between devices, passed_along(): return lax.ppermute(block, axis, route)  5.39 us
    ppermute x1, waiting for transfers between devices, body(): queries_below = lax.ppermute(query_rows, 'row', row_up)  3.74 us
    ppermute x1, starting transfers between devices, body(): lax.ppermute(jnp.concatenate([jnp.concatenate([peak, total], axis=1) for...  3.59 us
    unnamed x30, local copies, waits for them, and re-layouts  3.59 us
  transfers between devices with their start and end apart: 6, of which 4 were waited for; matrix products, arithmetic and copies ran while one was open for 28% of the time, Pallas kernels for 0%

profile of v9, /device:TPU:1, one launch (start us, length us, event | category | flops | bytes accessed | tf_op | source)
XLA Modules:
  0.0 138.6 jit_solution(6335705145277381297)
XLA Ops:
  8.0 1.1 multiply_convert_fusion
  9.1 5.4 %collective-permute-start = (bf16[127,512]{1,0:T(8,128)(2,1)S(1)}, bf16[127,512]{1,0:T(8,128)(2,1)S(1)}, u32[]{:S(2)}, u32[]{:S(2)}) collective-permute-start(bf16[127,512]{1,0:T(8,128)(2,1)S(1)} %slice.132), channel_id=1, source_target_pairs={{0,4},{4,8},{8,12},{12,16},{16,20},{20,24},{24,28},{28,32},{32,36}... | collective-permute-start | bytes 390152 | tf_op jit(solution)/shard_map/ppermute | solution.py:21
  14.7 1.8 %fusion.26 = bf16[4,8,128,128]{3,1,2,0:T(8,128)(2,1)S(1)} fusion(bf16[32,128]{1,0:T(8,128)(2,1)S(1)} %copy-done, s32[16384]{0:T(1024)S(1)} %subtract_bitcast_fusion), kind=kOutput, calls=%fused_computation.48 | convolution fusion | flops 136839168 | bytes 1122304 | tf_op jit(solution)/shard_map/dot_general | solution.py:30
  17.5 1.8 %fusion.27 = bf16[4,8,128,128]{3,1,2,0:T(8,128)(2,1)S(1)} fusion(bf16[32,128]{1,0:T(8,128)(2,1)S(1)} %copy-done, s32[16384]{0:T(1024)S(1)} %broadcast_add_fusion), kind=kOutput, calls=%fused_computation.49 | convolution fusion | flops 136839168 | bytes 1122304 | tf_op jit(solution)/shard_map/dot_general | solution.py:30
  21.0 0.8 fusion.56
  21.8 1.5 %collective-permute-start.1 = (bf16[256,512]{1,0:T(8,128)(2,1)S(1)}, bf16[256,512]{1,0:T(8,128)(2,1)S(1)}, u32[]{:S(2)}, u32[]{:S(2)}) collective-permute-start(bf16[256,512]{1,0:T(8,128)(2,1)S(1)} %copy-done.11), channel_id=1, source_target_pairs={{64,0},{128,64},{192,128},{256,192},{320,256},{384,320},{448,384},... | collective-permute-start | bytes 786440 | tf_op jit(solution)/shard_map/ppermute | solution.py:74
  23.4 1.8 %copy.26 = bf16[256,512]{1,0:T(8,128)(2,1)} copy(bf16[256,512]{0,1:T(8,128)(2,1)} %fusion.56) | data formatting | bytes 524288
  25.2 3.7 %collective-permute-done.1 = bf16[256,512]{1,0:T(8,128)(2,1)S(1)} collective-permute-done((bf16[256,512]{1,0:T(8,128)(2,1)S(1)}, bf16[256,512]{1,0:T(8,128)(2,1)S(1)}, u32[]{:S(2)}, u32[]{:S(2)}) %collective-permute-start.1) | collective-permute-done | bytes 262176 | tf_op jit(solution)/shard_map/ppermute | solution.py:74
  28.9 32.8 %all-gather.5.cloned.1.call-done = bf16[4096,512]{1,0:T(8,128)(2,1)} async-done(((bf16[256,512]{1,0:T(8,128)(2,1)}), bf16[4096,512]{1,0:T(8,128)(2,1)}) %all-gather.5.cloned.1.call-update) | async-done | bytes 4194320 | tf_op jit(solution)/shard_map/all_gather | solution.py:69
  61.8 2.7 %fusion.88 = (f32[256]{0:T(256)S(1)}, f32[256,4096]{1,0:T(8,128)S(1)}) fusion(bf16[4096,512]{1,0:T(8,128)(2,1)} %all-gather.5.cloned.1.call-done, bf16[256,512]{1,0:T(8,128)(2,1)S(1)} %collective-permute-done.1, s32[256]{0:T(256)S(1)} %iota_add_fusion.2, s32[4096]{0:T(1024)S(1)} %iota_add_fusion, pred[4096]{0:T(1024)(128)(4,1)S(1)} %fusion.70), kind=kOutput, calls=%fused_computation.133 | convolution fusion | flops 273678080 | bytes 5330944 | tf_op jit(solution)/shard_map/dot_general | solution.py:88
  64.4 1.3 fusion.89
  65.8 1.3 fusion.90
  67.1 1.3 fusion.91
  68.4 6.0 %fusion.14 = (f32[256]{0:T(256)S(1)}, f32[256]{0:T(256)S(1)}, f32[256]{0:T(256)S(1)}, f32[256]{0:T(256)S(1)}, bf16[256,4096]{1,0:T(8,128)(2,1)}, /*index=5*/bf16...) fusion(f32[256,4096]{1,0:T(8,128)S(1)} %get-tuple-element.119, ...), kind=kLoop, calls=%fused_computation.36 | loop fusion | flops 18873344 | bytes 25195520 | tf_op jit(solution)/shard_map/reduce_sum | solution.py:99
  74.5 3.6 %collective-permute-start.2 = (f32[256,8]{0,1:T(8,128)S(1)}, f32[256,8]{0,1:T(8,128)S(1)}, u32[]{:S(2)}, u32[]{:S(2)}) collective-permute-start(f32[256,8]{0,1:T(8,128)S(1)} %concatenate.17), channel_id=1, source_target_pairs={{0,64},{64,128},{128,192},{192,256},{256,320},{320,384},{384,448},... | collective-permute-start | bytes 24584 | tf_op jit(solution)/shard_map/ppermute | solution.py:107
  78.1 2.5 %fusion.92 = (f32[256]{0:T(256)S(1)}, f32[256,4096]{1,0:T(8,128)S(1)}) fusion(bf16[4096,512]{1,0:T(8,128)(2,1)} %all-gather.5.cloned.1.call-done, bf16[256,512]{1,0:T(8,128)(2,1)S(1)} %copy-done.11, s32[256]{0:T(256)S(1)} %iota_add_fusion.1, s32[4096]{0:T(1024)S(1)} %iota_add_fusion, pred[4096]{0:T(1024)(128)(4,1)S(1)} %fusion.69), kind=kOutput, calls=%fused_computation.137 | convolution fusion | flops 273678080 | bytes 5330944 | tf_op jit(solution)/shard_map/dot_general | solution.py:88
  80.7 1.3 fusion.93
  82.0 1.3 fusion.94
  83.3 1.3 fusion.95
  84.7 6.5 %fusion.24 = (f32[256]{0:T(256)S(1)}, f32[256]{0:T(256)S(1)}, f32[256]{0:T(256)S(1)}, f32[256]{0:T(256)S(1)}, bf16[256,4096]{1,0:T(8,128)(2,1)}, /*index=5*/bf16...) fusion(f32[256,4096]{1,0:T(8,128)S(1)} %get-tuple-element.127, f32[256]{0:T(256)S(1)} %get-tuple-element.126, ...), kind=kLoop, calls=%fused_computation.46 | loop fusion | flops 18873344 | bytes 25195520 | tf_op jit(solution)/shard_map/reduce_sum | solution.py:99
  91.2 23.1 %all-gather.7.cloned.1.call-done = bf16[4096,512]{0,1:T(8,128)(2,1)} async-done(((bf16[256,512]{0,1:T(8,128)(2,1)}), bf16[4096,512]{0,1:T(8,128)(2,1)}) %all-gather.7.cloned.1.call-update) | async-done | bytes 4194320 | tf_op jit(solution)/shard_map/all_gather | solution.py:69
  114.3 2.8 %fusion.42 = bf16[256,128]{0,1:T(8,128)(2,1)S(1)} fusion(bf16[256,4096]{1,0:T(8,128)(2,1)} %get-tuple-element.50, bf16[4096,512]{0,1:T(8,128)(2,1)} %all-gather.7.cloned.1.call-done), kind=kOutput, calls=%fused_computation.65 | convolution fusion | flops 268435456 | bytes 3211264 | tf_op jit(solution)/shard_map/dot_general | solution.py:104
  117.2 2.7 %fusion.46 = bf16[256,128]{0,1:T(8,128)(2,1)S(1)} fusion(bf16[256,4096]{1,0:T(8,128)(2,1)} %get-tuple-element.49, bf16[4096,512]{0,1:T(8,128)(2,1)} %all-gather.7.cloned.1.call-done), kind=kOutput, calls=%fused_computation.69 | convolution fusion | flops 268435456 | bytes 3211264 | tf_op jit(solution)/shard_map/dot_general | solution.py:104
  119.9 0.8 fusion.50
  120.7 0.8 fusion.54
  121.6 3.5 %collective-permute-start.3 = (bf16[256,512]{0,1:T(8,128)(2,1)S(1)}, bf16[256,512]{0,1:T(8,128)(2,1)S(1)}, u32[]{:S(2)}, u32[]{:S(2)}) collective-permute-start(bf16[256,512]{0,1:T(8,128)(2,1)S(1)} %pad_maximum_fusion), channel_id=1, source_target_pairs={{0,64},{64,128},{128,192},{192,256},{256,320},{320,384},{384,448},... | collective-permute-start | bytes 786440 | tf_op jit(solution)/shard_map/ppermute | solution.py:122
  125.1 0.7 fusion.52
  125.9 0.7 fusion.48
  126.6 0.7 fusion.44
  127.5 0.7 fusion.40
  128.2 2.1 %collective-permute-done.3 = bf16[256,512]{0,1:T(8,128)(2,1)S(1)} collective-permute-done((bf16[256,512]{0,1:T(8,128)(2,1)S(1)}, bf16[256,512]{0,1:T(8,128)(2,1)S(1)}, u32[]{:S(2)}, u32[]{:S(2)}) %collective-permute-start.3) | collective-permute-done | bytes 262176 | tf_op jit(solution)/shard_map/ppermute | solution.py:122
  130.9 0.8 copy.27
  (62 shorter events, 4.5 us)
Async XLA Ops:
  7.2 7.5 %copy-start = (bf16[32,128]{1,0:T(8,128)(2,1)S(1)}, bf16[32,128]{1,0:T(8,128)(2,1)}, u32[]{:S(2)}) copy-start(bf16[32,128]{1,0:T(8,128)(2,1)} %param.9) | copy-start | bytes 24580
  7.2 54.6 %all-gather.5.cloned.1.call-start = ((), (), s32[]{:S(2)}) async-start(), calls=%async_computation | async-start | bytes 4456448 | tf_op jit(solution)/shard_map/all_gather | solution.py:69
  7.9 106.4 %all-gather.7.cloned.1.call-start = ((), (), s32[]{:S(2)}) async-start(), calls=%async_computation.1 | async-start | bytes 4456448 | tf_op jit(solution)/shard_map/all_gather | solution.py:69
  9.1 10.7 %collective-permute-start = (bf16[127,512]{1,0:T(8,128)(2,1)S(1)}, bf16[127,512]{1,0:T(8,128)(2,1)S(1)}, u32[]{:S(2)}, u32[]{:S(2)}) collective-permute-start(bf16[127,512]{1,0:T(8,128)(2,1)S(1)} %slice.132), channel_id=1, source_target_pairs={{0,4},{4,8},{8,12},{12,16},{16,20},{20,24},{24,28},{28,32},{32,36}... | collective-permute-start | bytes 390152 | tf_op jit(solution)/shard_map/ppermute | solution.py:21
  16.7 2.9 %copy-start.7 = (bf16[256,512]{1,0:T(8,128)(2,1)S(1)}, bf16[256,512]{1,0:T(8,128)(2,1)}, u32[]{:S(2)}) copy-start(bf16[256,512]{1,0:T(8,128)(2,1)} %param.6) | copy-start | bytes 786436
  19.2 2.6 %copy-start.11 = (bf16[256,512]{1,0:T(8,128)(2,1)S(1)}, bf16[256,512]{1,0:T(8,128)(2,1)}, u32[]{:S(2)}) copy-start(bf16[256,512]{1,0:T(8,128)(2,1)} %param.10) | copy-start | bytes 786436
  21.8 7.1 %collective-permute-start.1 = (bf16[256,512]{1,0:T(8,128)(2,1)S(1)}, bf16[256,512]{1,0:T(8,128)(2,1)S(1)}, u32[]{:S(2)}, u32[]{:S(2)}) collective-permute-start(bf16[256,512]{1,0:T(8,128)(2,1)S(1)} %copy-done.11), channel_id=1, source_target_pairs={{64,0},{128,64},{192,128},{256,192},{320,256},{384,320},{448,384},... | collective-permute-start | bytes 786440 | tf_op jit(solution)/shard_map/ppermute | solution.py:74
  61.8 2.7 %copy-start.8 = (bf16[4096,512]{1,0:T(8,128)(2,1)S(1)}, bf16[4096,512]{1,0:T(8,128)(2,1)}, u32[]{:S(2)}) copy-start(bf16[4096,512]{1,0:T(8,128)(2,1)} %all-gather.5.cloned.1.call-done) | copy-start | bytes 12582916
  74.5 6.1 %copy-start.9 = (bf16[4096,512]{1,0:T(8,128)(2,1)S(1)}, bf16[4096,512]{1,0:T(8,128)(2,1)}, u32[]{:S(2)}) copy-start(bf16[4096,512]{1,0:T(8,128)(2,1)} %all-gather.5.cloned.1.call-done) | copy-start | bytes 12582916
  74.5 16.6 %collective-permute-start.2 = (f32[256,8]{0,1:T(8,128)S(1)}, f32[256,8]{0,1:T(8,128)S(1)}, u32[]{:S(2)}, u32[]{:S(2)}) collective-permute-start(f32[256,8]{0,1:T(8,128)S(1)} %concatenate.17), channel_id=1, source_target_pairs={{0,64},{64,128},{128,192},{192,256},{256,320},{320,384},{384,448},... | collective-permute-start | bytes 24584 | tf_op jit(solution)/shard_map/ppermute | solution.py:107
  114.3 5.5 %copy-start.2 = (bf16[256,4096]{1,0:T(8,128)(2,1)S(1)}, bf16[256,4096]{1,0:T(8,128)(2,1)}, u32[]{:S(2)}) copy-start(bf16[256,4096]{1,0:T(8,128)(2,1)} %get-tuple-element.48) | copy-start | bytes 6291460
  114.3 5.6 %copy-start.10 = (bf16[4096,512]{0,1:T(8,128)(2,1)S(1)}, bf16[4096,512]{0,1:T(8,128)(2,1)}, u32[]{:S(2)}) copy-start(bf16[4096,512]{0,1:T(8,128)(2,1)} %all-gather.7.cloned.1.call-done) | copy-start | bytes 12582916
  119.9 5.3 %copy-start.6 = (bf16[256,4096]{1,0:T(8,128)(2,1)S(1)}, bf16[256,4096]{1,0:T(8,128)(2,1)}, u32[]{:S(2)}) copy-start(bf16[256,4096]{1,0:T(8,128)(2,1)} %get-tuple-element.56) | copy-start | bytes 6291460
  120.7 5.1 %copy-start.5 = (bf16[256,4096]{1,0:T(8,128)(2,1)S(1)}, bf16[256,4096]{1,0:T(8,128)(2,1)}, u32[]{:S(2)}) copy-start(bf16[256,4096]{1,0:T(8,128)(2,1)} %get-tuple-element.57) | copy-start | bytes 6291460
  121.6 5.0 %copy-start.4 = (bf16[256,4096]{1,0:T(8,128)(2,1)S(1)}, bf16[256,4096]{1,0:T(8,128)(2,1)}, u32[]{:S(2)}) copy-start(bf16[256,4096]{1,0:T(8,128)(2,1)} %get-tuple-element.58) | copy-start | bytes 6291460
  121.6 8.7 %collective-permute-start.3 = (bf16[256,512]{0,1:T(8,128)(2,1)S(1)}, bf16[256,512]{0,1:T(8,128)(2,1)S(1)}, u32[]{:S(2)}, u32[]{:S(2)}) collective-permute-start(bf16[256,512]{0,1:T(8,128)(2,1)S(1)} %pad_maximum_fusion), channel_id=1, source_target_pairs={{0,64},{64,128},{128,192},{192,256},{256,320},{320,384},{384,448},... | collective-permute-start | bytes 786440 | tf_op jit(solution)/shard_map/ppermute | solution.py:122
  125.9 1.6 %copy-start.3 = (bf16[256,4096]{1,0:T(8,128)(2,1)S(1)}, bf16[256,4096]{1,0:T(8,128)(2,1)}, u32[]{:S(2)}) copy-start(bf16[256,4096]{1,0:T(8,128)(2,1)} %get-tuple-element.59) | copy-start | bytes 6291460
  126.6 5.1 %copy-start.1 = (bf16[32,128]{1,0:T(8,128)(2,1)S(1)}, bf16[32,128]{1,0:T(8,128)(2,1)}, u32[]{:S(2)}) copy-start(bf16[32,128]{1,0:T(8,128)(2,1)} %param.9) | copy-start | bytes 24580
Sparse Core Ops, SparseCore 0:
  10.1 51.5 all-gather.4
  64.4 49.8 all-gather.6
